TPU v7x, 32 devices: a whole 2x2x4 slice. The times are simulated.
32 devices in a mesh: grp: 4 (over y, core), col: 8 (over z, x).
Axes of the slice: x: 2, y: 2, z: 4, core: 2. Of those that a mesh axis runs over, the one named last changes fastest.
Arguments:
- orbitals: float32 [32, 14336], P('grp', 'col'), may hold values from -6 to 6
- column_cell: int32 [448], replicated, may hold values from 0 to 2303, as said below
- column_length: int32 [448], replicated, may hold values from 1 to 32, as said below
- sources: int32 [3], replicated, may hold values from 0 to 31, as said below
- weights: float32 [3], replicated, may hold values from 0.5 to 2
Outputs:
- exchange_coefficients: float32 [32, 14336], P('grp', 'col')
Inputs may be any that keep to these rules, and one draw needn't show every extreme that they name: `column_cell`: the cells are distinct and are the 448 cells of smallest f(a)^2 + f(b)^2, f(k) = min(k, 48 - k), so they fill a disk around zero frequency. `column_length`: lengths fall from the centre of the disk to its rim like chords of a sphere; the centre column has 32 live slots and the outermost has 1. `sources`: distinct band indices.
All inputs are finite; a program needn't handle non-finite values.
Results may differ from a plain program's by a relative error of at most 0.0003.
Values sent between devices are 32-bit elements; how exact they have to be, the bound alone decides.
No kernel may reach another device: no remote copies, remote signals or barrier semaphores. Data moves between devices by JAX's collectives and lax.ppermute only.
A program may use at most 64 MiB of HBM per device.

v0:
```python
import math

import jax
import jax.numpy as jnp
from jax import lax
from jax.sharding import PartitionSpec as P

GRID = 48

kernel_scale = 20000.0
screen_shift = 4.0

HI = lax.Precision.HIGHEST
MID = lax.Precision.HIGH


def cas_matrix(extent):
    index = jnp.arange(extent, dtype=jnp.int32)
    phase = index[:, None] * index[None, :] % extent
    angle = phase.astype(jnp.float32) * (2.0 * math.pi / extent)
    return (jnp.cos(angle) + jnp.sin(angle)) / math.sqrt(extent)


def kernel_grid(extent):
    index = jnp.arange(extent, dtype=jnp.int32)
    freq = jnp.minimum(index, extent - index)
    square = freq * freq
    total = square[:, None, None] + square[None, :, None] + square[None, None, :]
    kernel = kernel_scale / (total.astype(jnp.float32) + screen_shift)
    return jnp.where(total > 0, kernel, 0.0)


def shift_tables(column_length, depth, extent):
    half = column_length // 2
    index = jnp.arange(extent, dtype=jnp.int32)
    phase = (half[:, None] * index[None, :]) % extent
    angle = phase.astype(jnp.float32) * (2.0 * math.pi / extent)
    slot = jnp.arange(depth, dtype=jnp.int32)
    live = slot[None, :] < column_length[:, None]
    return jnp.cos(angle), jnp.sin(angle), live


def plane_matrix(column_cell, table, extent):
    index = jnp.arange(extent, dtype=jnp.int32)
    first = (column_cell[None, :] // extent == index[:, None]).astype(jnp.float32)
    second = (column_cell[None, :] % extent == index[:, None]).astype(jnp.float32)
    ta = jnp.dot(table, first, precision=HI)
    tb = jnp.dot(table, second, precision=HI)
    return (ta[:, None, :] * tb[None, :, :]).reshape(extent * extent, -1)


def cas_three(field, table):
    field = jnp.einsum("absc,ck->absk", field, table, precision=MID)
    field = jnp.einsum("absc,kb->aksc", field, table, precision=MID)
    return jnp.einsum("absc,ka->kbsc", field, table, precision=MID)


def make_local(n_grp_bands, n_grp, n_col):
    def local(orbitals, column_cell, column_length, sources, weights):
        extent = GRID
        count = column_cell.shape[0]
        width = orbitals.shape[1]
        depth = width * n_col // count
        n_src = sources.shape[0]
        table = cas_matrix(extent)
        kernel = kernel_grid(extent)
        cos_h, sin_h, live = shift_tables(column_length, depth, extent)
        slot = jnp.arange(depth, dtype=jnp.int32)
        fwd = jnp.concatenate([table[:depth], table[(extent - slot) % extent]], axis=1)
        bwd = jnp.concatenate([table[:, :depth], table[:, (extent - slot) % extent]], axis=0)
        w = lax.optimization_barrier(plane_matrix(column_cell, table, extent))

        g = lax.axis_index("grp")
        owner = sources // n_grp_bands
        picked = orbitals[sources % n_grp_bands]
        picked = jnp.where((owner == g)[:, None], picked, 0.0)
        spread = jnp.broadcast_to(picked[None], (n_grp, n_src, width))
        picked = jnp.sum(lax.all_to_all(spread, "grp", 0, 0, tiled=True), axis=0)
        send = jnp.concatenate(
            [orbitals[:, None, :], jnp.broadcast_to(picked[None], (n_grp_bands, n_src, width))], axis=1)
        got = lax.all_to_all(send, "col", 0, 0, tiled=True)
        n = 1 + n_src
        coeff = got.reshape(n_col, n, width // depth, depth).transpose(0, 2, 1, 3).reshape(count, n, depth)
        coeff = jnp.where(live[:, None, :], coeff, 0.0)
        both = jnp.dot(coeff.reshape(count * n, depth), fwd, precision=MID).reshape(count, n, 2, extent)
        cols = cos_h[:, None, :] * both[:, :, 0] - sin_h[:, None, :] * both[:, :, 1]
        grids = jnp.dot(w, cols.reshape(count, n * extent), precision=MID)
        grids = grids.reshape(extent, extent, n, extent)
        own = grids[:, :, :1]
        src = grids[:, :, 1:]
        density = own * src
        potential = cas_three(kernel[:, :, None, :] * cas_three(density, table), table)
        total = jnp.sum(weights[None, None, :, None] * potential * src, axis=2)
        back = lax.dot_general(w, total.reshape(extent * extent, extent), (((0,), (0,)), ((), ())), precision=MID)
        scaled = jnp.concatenate([back * cos_h, -(back * sin_h)], axis=1)
        out = -jnp.dot(scaled, bwd, precision=MID)
        out = jnp.where(live, out, 0.0)
        return lax.all_to_all(out.reshape(n_col, 1, width), "col", 0, 0, tiled=True).reshape(n_col, width)

    return local


def solution(mesh):
    n_grp = mesh.shape["grp"]
    n_col = mesh.shape["col"]

    def run(orbitals, column_cell, column_length, sources, weights):
        n_grp_bands = orbitals.shape[0] // n_grp
        body = make_local(n_grp_bands, n_grp, n_col)
        return jax.shard_map(
            body,
            mesh=mesh,
            in_specs=(P("grp", "col"), P(), P(), P(), P()),
            out_specs=P("grp", "col"),
            check_vma=False,
        )(orbitals, column_cell, column_length, sources, weights)

    return run
```

profile of v0, /device:TPU:0, one launch (start us, length us, event | category | flops | bytes accessed | tf_op | source)
XLA Modules:
  0.0 68.1 jit_solution(9019507643158216125)
XLA Ops:
  0.0 0.7 compare_select_fusion.1
  0.7 0.7 fusion.57
  1.3 1.4 %gather_fusion = f32[3,1792]{1,0:T(4,128)S(1)} fusion(f32[8,1792]{1,0:T(8,128)} %param.5, s32[1024]{0:T(1024)S(1)} %pad_clamp_fusion.1), kind=kCustom, calls=%fused_computation | custom fusion | bytes 43020 | tf_op jit(solution)/shard_map/gather | solution.py:75
  2.7 0.1 broadcast_select_fusion.1
  2.8 0.7 broadcast_in_dim.41
  3.5 4.2 %all-to-all-start = ((f32[4,3,1792]{2,1,0:T(4,128)}), f32[4,3,1792]{2,1,0:T(4,128)S(1)}, u32[]{:S(2)}, u32[]{:S(2)}) async-start(f32[4,3,1792]{2,1,0:T(4,128)} %broadcast_in_dim.41), calls=%async_computation | async-start | bytes 229376 | tf_op jit(solution)/shard_map/all_to_all | solution.py:78
  7.7 0.1 add_multiply_fusion
  7.8 0.9 %broadcast_in_dim.37 = f32[8,1,1792]{2,1,0:T(1,128)S(1)} reshape(f32[8,1792]{1,0:T(8,128)} %param.5) | data formatting | bytes 114688 | tf_op jit(solution)/shard_map/broadcast_in_dim | solution.py:80
  8.7 0.8 %lt.104 = s32[8,56]{1,0:T(8,128)S(1)} reshape(s32[448]{0:T(512)} %param.7) | data formatting | bytes 3584 | tf_op jit(solution)/shard_map/lt | solution.py:39
  9.5 0.7 %add_select_fusion.2 = s32[448]{0:T(512)S(1)} fusion(s32[448]{0:T(512)} %param.7), kind=kLoop, calls=%fused_computation.81 | loop fusion | flops 6720 | bytes 3584 | tf_op jit(solution)/shard_map/jit(floor_divide)/jit(_where)/select_n | solution.py:34
  10.2 0.1 copy.46
  10.3 0.6 gather_fusion.1
  10.8 0.1 maximum_bitcast_fusion
  10.9 0.1 dot_general.50
  11.0 0.1 iota_compare_fusion
  11.1 0.4 fusion.28
  11.6 0.7 %add_select_fusion.4 = (s32[448]{0:T(512)S(1)}, s32[448]{0:T(512)S(1)}) fusion(s32[448]{0:T(512)} %param.6), kind=kLoop, calls=%fused_computation.86 | loop fusion | flops 5376 | bytes 5376 | tf_op jit(solution)/shard_map/jit(floor_divide)/jit(_where)/select_n | solution.py:45
  12.3 0.3 fusion.30
  12.6 0.3 fusion.31
  12.9 2.8 %broadcast_multiply_fusion = f32[48,48,448]{2,1,0:T(8,128)} fusion(f32[48,448]{1,0:T(8,128)S(1)} %fusion.31, f32[48,448]{1,0:T(8,128)S(1)} %fusion.30), kind=kLoop, calls=%fused_computation.15 | loop fusion | flops 1032192 | bytes 4300800 | tf_op jit(solution)/shard_map/mul | solution.py:49
  15.6 0.6 gather_fusion.2
  16.2 0.1 copy.47
  16.3 0.0 all-to-all-done
  16.3 0.8 %pad_maximum_fusion = f32[8,4,1792]{2,1,0:T(4,128)} fusion(f32[8,3,1792]{2,1,0:T(4,128)S(1)} %broadcast_in_dim.42, f32[8,1,1792]{2,1,0:T(1,128)S(1)} %broadcast_in_dim.37), kind=kLoop, calls=%fused_computation.32 | loop fusion | flops 57344 | bytes 458752 | tf_op jit(solution)/shard_map/concatenate | solution.py:79
  17.1 6.3 %all-to-all-start.1 = ((f32[8,4,1792]{2,1,0:T(4,128)}), f32[8,4,1792]{2,1,0:T(4,128)S(1)}, u32[]{:S(2)}, u32[]{:S(2)}) async-start(f32[8,4,1792]{2,1,0:T(4,128)} %pad_maximum_fusion), calls=%async_computation.1 | async-start | bytes 458752 | tf_op jit(solution)/shard_map/all_to_all | solution.py:81
  23.5 0.1 broadcast_add_fusion
  23.6 0.4 fusion.17
  24.0 8.6 %all-to-all-done.1 = f32[8,4,1792]{2,1,0:T(4,128)S(1)} async-done(((f32[8,4,1792]{2,1,0:T(4,128)}), f32[8,4,1792]{2,1,0:T(4,128)S(1)}, u32[]{:S(2)}, u32[]{:S(2)}) %all-to-all-start.1) | async-done | bytes 229408 | tf_op jit(solution)/shard_map/all_to_all | solution.py:81
  32.6 0.3 reshape.218
  32.9 0.0 copy-start
  32.9 0.1 broadcast_select_fusion
  33.0 0.7 %fusion.35 = f32[448,4,2,48]{0,3,2,1:T(8,128)S(1)} fusion(f32[448,4,32,1]{2,0,3,1:T(8,128)S(1)} %bitcast.78, f32[2,48,32]{1,0,2:T(2,128)S(1)} %dot_general.50), kind=kOutput, calls=%fused_computation.57 | convolution fusion | flops 33030144 | bytes 929792 | tf_op jit(solution)/shard_map/dot_general | solution.py:85
  33.7 0.1 fusion.91
  33.8 0.1 fusion.19
  33.9 1.3 %copy-done = f32[48,48,448]{2,1,0:T(8,128)S(1)} copy-done((f32[48,48,448]{2,1,0:T(8,128)S(1)}, f32[48,48,448]{2,1,0:T(8,128)}, u32[]{:S(2)}) %copy-start) | copy-done | bytes 4128792
  35.2 4.0 %fusion.92 = f32[48,48,4,48]{3,1,2,0:T(8,128)S(1)} fusion(f32[48,48,448,1]{2,1,3,0:T(8,128)S(1)} %bitcast.75, f32[4,48,448,1]{2,1,0,3:T(8,128)S(1)} %bitcast.80), kind=kOutput, calls=%fused_computation.139 | convolution fusion | flops 1189085184 | bytes 6242304 | tf_op jit(solution)/shard_map/dot_general | solution.py:87
  39.3 0.1 slice_bitcast_fusion
  39.4 1.7 %fusion.8 = f32[48,48,3,48]{3,1,2,0:T(8,128)S(1)} fusion(f32[48,48,4,48]{3,1,2,0:T(8,128)S(1)} %fusion.92, f32[48,48,48]{2,1,0:T(8,128)S(1)} %slice_bitcast_fusion), kind=kOutput, calls=%fused_computation.12 | convolution fusion | flops 95908608 | bytes 6045696 | tf_op jit(solution)/shard_map/absc,ck->absk/dot_general | solution.py:53
  41.1 1.9 %convolution_bitcast_fusion.1 = f32[48,48,3,48]{3,1,2,0:T(8,128)S(1)} fusion(f32[48,48,3,48]{3,1,2,0:T(8,128)S(1)} %fusion.8), kind=kOutput, calls=%fused_computation.17 | convolution fusion | flops 95576832 | bytes 2654208 | tf_op jit(solution)/shard_map/absc,kb->aksc/dot_general | solution.py:54
  43.0 3.0 %fusion.11 = f32[48,48,3,48]{3,0,2,1:T(8,128)S(1)} fusion(f32[48,48,3,48]{3,1,2,0:T(8,128)S(1)} %convolution_bitcast_fusion.1, f32[48,48,48]{2,0,1:T(8,128)S(1)} %fusion.17), kind=kOutput, calls=%fused_computation.18 | convolution fusion | flops 95908608 | bytes 3096576 | tf_op jit(solution)/shard_map/absc,ka->kbsc/dot_general | solution.py:55
  46.0 2.9 %fusion.4 = f32[48,48,3,48]{3,1,2,0:T(8,128)S(1)} fusion(f32[48,48,3,48]{3,0,2,1:T(8,128)S(1)} %fusion.11), kind=kOutput, calls=%fused_computation.8 | convolution fusion | flops 95576832 | bytes 2654208 | tf_op jit(solution)/shard_map/absc,ck->absk/dot_general | solution.py:53
  48.9 1.9 %convolution_bitcast_fusion = f32[48,48,3,48]{3,1,2,0:T(8,128)S(1)} fusion(f32[48,48,3,48]{3,1,2,0:T(8,128)S(1)} %fusion.4), kind=kOutput, calls=%fused_computation.16 | convolution fusion | flops 95576832 | bytes 2654208 | tf_op jit(solution)/shard_map/absc,kb->aksc/dot_general | solution.py:54
  50.8 0.0 copy-start.2
  50.8 3.0 %fusion.2 = f32[48,48,3,48]{3,0,2,1:T(8,128)S(1)} fusion(f32[48,48,3,48]{3,1,2,0:T(8,128)S(1)} %convolution_bitcast_fusion), kind=kOutput, calls=%fused_computation.6 | convolution fusion | flops 95576832 | bytes 2654208 | tf_op jit(solution)/shard_map/absc,ka->kbsc/dot_general | solution.py:55
  53.8 0.0 copy-done.2
  53.8 1.5 %fusion.1 = f32[48,48,48]{2,1,0:T(8,128)S(1)} fusion(f32[48,48,3,48]{3,0,2,1:T(8,128)S(1)} %fusion.2, f32[48,48,4,48]{3,1,2,0:T(8,128)S(1)} %fusion.92, f32[3]{0:T(128)S(1)} %copy-done.2), kind=kLoop, calls=%fused_computation.5 | loop fusion | flops 884736 | bytes 3096588 | tf_op jit(solution)/shard_map/reduce_sum | solution.py:93
  55.2 0.0 copy-start.1
  55.2 1.7 %fusion.34 = (f32[448,48]{0,1:T(8,128)S(1)}, f32[448,48]{0,1:T(8,128)S(1)}) fusion(s32[448]{0:T(512)S(1)} %add_select_fusion.2, f32[2304,448]{1,0:T(8,128)S(1)} %bitcast.76, f32[2304,48]{1,0:T(8,128)S(1)} %bitcast.77), kind=kOutput, calls=%fused_computation.56 | convolution fusion | flops 297529344 | bytes 4744960 | tf_op jit(solution)/shard_map/dot_general | solution.py:94
  57.0 0.0 copy-done.1
  57.0 0.2 fusion.18
  57.2 0.1 copy.48
  57.3 0.2 reshape.252
  57.5 10.0 %all_to_all.15 = f32[8,1,1792]{2,1,0:T(1,128)S(1)} all-to-all(f32[8,1,1792]{2,1,0:T(1,128)S(1)} %reshape.252), channel_id=1, replica_groups=mesh['grp'=4,'col'=8] {'col'}, dimensions={0} | all-to-all | bytes 114688 | tf_op jit(solution)/shard_map/all_to_all | solution.py:98
  67.5 0.6 copy.75
  (8 shorter events, 0.1 us)
Async XLA Ops:
  3.5 12.8 %all-to-all-start = ((f32[4,3,1792]{2,1,0:T(4,128)}), f32[4,3,1792]{2,1,0:T(4,128)S(1)}, u32[]{:S(2)}, u32[]{:S(2)}) async-start(f32[4,3,1792]{2,1,0:T(4,128)} %broadcast_in_dim.41), calls=%async_computation | async-start | bytes 229376 | tf_op jit(solution)/shard_map/all_to_all | solution.py:78
  17.1 15.4 %all-to-all-start.1 = ((f32[8,4,1792]{2,1,0:T(4,128)}), f32[8,4,1792]{2,1,0:T(4,128)S(1)}, u32[]{:S(2)}, u32[]{:S(2)}) async-start(f32[8,4,1792]{2,1,0:T(4,128)} %pad_maximum_fusion), calls=%async_computation.1 | async-start | bytes 458752 | tf_op jit(solution)/shard_map/all_to_all | solution.py:81
  32.9 2.3 %copy-start = (f32[48,48,448]{2,1,0:T(8,128)S(1)}, f32[48,48,448]{2,1,0:T(8,128)}, u32[]{:S(2)}) copy-start(f32[48,48,448]{2,1,0:T(8,128)} %broadcast_multiply_fusion) | copy-start | bytes 12386308
  50.8 3.0 %copy-start.2 = (f32[3]{0:T(128)S(1)}, f32[3]{0:T(128)}, u32[]{:S(2)}) copy-start(f32[3]{0:T(128)} %param.9) | copy-start | bytes 40
  55.2 1.7 %copy-start.1 = (s32[448]{0:T(512)S(1)}, s32[448]{0:T(512)}, u32[]{:S(2)}) copy-start(s32[448]{0:T(512)} %param.7) | copy-start | bytes 5380
where the time goes:
time: 68.7 us; the launch traced here: 68.1 us
  matrix products  21.6 us (31%)
  starting transfers between devices  10.6 us (15%)
  blocking collectives  10 us (15%)
  other arithmetic  9.24 us (13%)
  waiting for transfers between devices  8.61 us (13%)
  local copies, waits for them, and re-layouts  7.81 us (11%)
    all_to_all x1, blocking collectives, local(): lax.all_to_all(out.reshape(n_col, 1, width), 'col', 0, 0, tiled=True)  10 us
    all_to_all x1, waiting for transfers between devices, local(): got = lax.all_to_all(send, 'col', 0, 0, tiled=True)  8.61 us
    all_to_all x1, starting transfers between devices, local(): got = lax.all_to_all(send, 'col', 0, 0, tiled=True)  6.35 us
    dot_general x2, matrix products, cas_three(): return jnp.einsum('absc,ka->kbsc', field, table, precision=MID)  5.95 us
    dot_general x2, matrix products, cas_three(): field = jnp.einsum('absc,ck->absk', field, table, precision=MID)  4.6 us
    all_to_all x1, starting transfers between devices, local(): picked = jnp.sum(lax.all_to_all(spread, 'grp', 0, 0, tiled=True), axis=0)  4.24 us
    dot_general x1, matrix products, local(): grids = jnp.dot(w, cols.reshape(count, n * extent), precision=MID)  4.04 us
    dot_general x2, matrix products, cas_three(): field = jnp.einsum('absc,kb->aksc', field, table, precision=MID)  3.76 us
  transfers between devices with their start and end apart: 2, of which 1 were waited for; matrix products, arithmetic and copies ran while one was open for 13% of the time, Pallas kernels for 0%

commit v1 on v0

--- a/solution.py
+++ b/solution.py
@@ -55,6 +55,18 @@
     return jnp.einsum("absc,ka->kbsc", field, table, precision=MID)
 
 
+def exchange(blocks, axis, size):
+    me = lax.axis_index(axis)
+    got = [blocks[me]]
+    for shift in range(1, size):
+        part = lax.dynamic_index_in_dim(blocks, (me + shift) % size, 0, keepdims=False)
+        perm = [(i, (i + shift) % size) for i in range(size)]
+        got.append(lax.ppermute(part, axis, perm))
+    got = jnp.stack(got)
+    order = (me - jnp.arange(size, dtype=jnp.int32)) % size
+    return got[order]
+
+
 def make_local(n_grp_bands, n_grp, n_col):
     def local(orbitals, column_cell, column_length, sources, weights):
         extent = GRID
@@ -70,15 +82,15 @@
         bwd = jnp.concatenate([table[:, :depth], table[:, (extent - slot) % extent]], axis=0)
         w = lax.optimization_barrier(plane_matrix(column_cell, table, extent))
 
+        own_blocks = exchange(orbitals, "col", n_col)
         g = lax.axis_index("grp")
         owner = sources // n_grp_bands
         picked = orbitals[sources % n_grp_bands]
         picked = jnp.where((owner == g)[:, None], picked, 0.0)
         spread = jnp.broadcast_to(picked[None], (n_grp, n_src, width))
-        picked = jnp.sum(lax.all_to_all(spread, "grp", 0, 0, tiled=True), axis=0)
-        send = jnp.concatenate(
-            [orbitals[:, None, :], jnp.broadcast_to(picked[None], (n_grp_bands, n_src, width))], axis=1)
-        got = lax.all_to_all(send, "col", 0, 0, tiled=True)
+        picked = jnp.sum(exchange(spread, "grp", n_grp), axis=0)
+        src_blocks = exchange(jnp.broadcast_to(picked[None], (n_col, n_src, width)), "col", n_col)
+        got = jnp.concatenate([own_blocks[:, None, :], src_blocks], axis=1)
         n = 1 + n_src
         coeff = got.reshape(n_col, n, width // depth, depth).transpose(0, 2, 1, 3).reshape(count, n, depth)
         coeff = jnp.where(live[:, None, :], coeff, 0.0)
@@ -95,7 +107,7 @@
         scaled = jnp.concatenate([back * cos_h, -(back * sin_h)], axis=1)
         out = -jnp.dot(scaled, bwd, precision=MID)
         out = jnp.where(live, out, 0.0)
-        return lax.all_to_all(out.reshape(n_col, 1, width), "col", 0, 0, tiled=True).reshape(n_col, width)
+        return exchange(out.reshape(n_col, width), "col", n_col)
 
     return local
 

time: 68.7 us -> 85.6 us (1.25)
  starting transfers between devices: 10.6 us -> 39.4 us
  blocking collectives: 10 us -> 0 us
  waiting for transfers between devices: 8.61 us -> 5.21 us
  local copies, waits for them, and re-layouts: 7.81 us -> 10.6 us
  other arithmetic: 9.24 us -> 7.88 us
    ppermute x0 -> x24, starting transfers between devices: none -> 39.4 us  [exchange(): got.append(lax.ppermute(part, axis, perm))]
    all_to_all x2 -> x0, starting transfers between devices: 10.6 us -> none  [the longest x1 6.35 us: local(): got = lax.all_to_all(send, 'col', 0, 0, tiled=True)]
    all_to_all x1 -> x0, blocking collectives: 10 us -> none  [local(): lax.all_to_all(out.reshape(n_col, 1, width), 'col', 0, 0, tiled=True)]
    all_to_all x2 -> x0, waiting for transfers between devices: 8.61 us -> none  [the longest x1 8.61 us: local(): got = lax.all_to_all(send, 'col', 0, 0, tiled=True)]
    ppermute x0 -> x24, waiting for transfers between devices: none -> 5.21 us  [exchange(): got.append(lax.ppermute(part, axis, perm))]
    gather x0 -> x5, local copies, waits for them, and re-layouts: none -> 3.1 us  [exchange(): return got[order]]
    broadcast_in_dim x3 -> x0, local copies, waits for them, and re-layouts: 1.54 us -> none  [the longest x1 0.86 us: local(): orbitals[:, None, :]]
    dynamic_slice x0 -> x2, local copies, waits for them, and re-layouts: none -> 1.54 us  [exchange(): lax.dynamic_index_in_dim(blocks, (me + shift) % size, 0, keepdims=False)]
  transfers between devices with their start and end apart: 2 -> 24, of which waited for: 1 -> 6; matrix products, arithmetic and copies ran while one was open for 13% -> 13% of each run, Pallas kernels for 0% -> 0%
where the time goes in v1:
time: 85.6 us; the launch traced here: 85.3 us
  starting transfers between devices  39.4 us (46%)
  matrix products  21.7 us (25%)
  local copies, waits for them, and re-layouts  10.6 us (12%)
  other arithmetic  7.88 us (9%)
  waiting for transfers between devices  5.21 us (6%)
    ppermute x24, starting transfers between devices, exchange(): got.append(lax.ppermute(part, axis, perm))  39.4 us
    dot_general x2, matrix products, cas_three(): return jnp.einsum('absc,ka->kbsc', field, table, precision=MID)  5.95 us
    ppermute x24, waiting for transfers between devices, exchange(): got.append(lax.ppermute(part, axis, perm))  5.21 us
    dot_general x2, matrix products, cas_three(): field = jnp.einsum('absc,ck->absk', field, table, precision=MID)  4.64 us
    dot_general x1, matrix products, local(): grids = jnp.dot(w, cols.reshape(count, n * extent), precision=MID)  4.04 us
    dot_general x2, matrix products, cas_three(): field = jnp.einsum('absc,kb->aksc', field, table, precision=MID)  3.76 us
    gather x5, local copies, waits for them, and re-layouts, exchange(): return got[order]  3.1 us
    mul x1, other arithmetic, plane_matrix(): return (ta[:, None, :] * tb[None, :, :]).reshape(extent * extent, -1)  2.73 us
  transfers between devices with their start and end apart: 24, of which 6 were waited for; matrix products, arithmetic and copies ran while one was open for 13% of the time, Pallas kernels for 0%

profile of v1, /device:TPU:0, one launch (start us, length us, event | category | flops | bytes accessed | tf_op | source)
XLA Modules:
  0.0 85.3 jit_solution(2996854370278071151)
XLA Ops:
  0.0 1.4 %dynamic-slice_reduce_fusion.7 = (f32[1792]{0:T(1024)S(1)}, f32[1792]{0:T(1024)S(1)}, f32[1792]{0:T(1024)S(1)}, f32[1792]{0:T(1024)S(1)}, f32[1792]{0:T(1024)S(1...) fusion(f32[8,1792]{1,0:T(8,128)} %param.5, s32[]{:T(128)S(6)} %select_n.325, s32[]{:T(128)S(6)} %select_n.323, ...), kind=kLoop, calls=%fused_computation.98 | loop fusion | bytes 114720 | tf_op jit(solution)/shard_map/jit(dynamic_index_in_dim)/dynamic_slice | solution.py:62
  1.4 3.0 %collective-permute-start = (f32[1792]{0:T(1024)S(1)}, f32[1792]{0:T(1024)S(1)}, u32[]{:S(2)}, u32[]{:S(2)}) collective-permute-start(f32[1792]{0:T(1024)S(1)} %get-tuple-element.18), channel_id=1, source_target_pairs={{0,1},{1,2},{2,3},{3,4},{4,5},{5,6},{6,7},{7,0},{8,9},{9,10},{10,1... | collective-permute-start | bytes 21512 | tf_op jit(solution)/shard_map/ppermute | solution.py:64
  4.4 1.6 %collective-permute-start.1 = (f32[1792]{0:T(1024)S(1)}, f32[1792]{0:T(1024)S(1)}, u32[]{:S(2)}, u32[]{:S(2)}) collective-permute-start(f32[1792]{0:T(1024)S(1)} %get-tuple-element.17), channel_id=1, source_target_pairs={{0,2},{1,3},{2,4},{3,5},{4,6},{5,7},{6,0},{7,1},{8,10},{9,11},{10,... | collective-permute-start | bytes 21512 | tf_op jit(solution)/shard_map/ppermute | solution.py:64
  6.0 2.6 %collective-permute-start.2 = (f32[1792]{0:T(1024)S(1)}, f32[1792]{0:T(1024)S(1)}, u32[]{:S(2)}, u32[]{:S(2)}) collective-permute-start(f32[1792]{0:T(1024)S(1)} %get-tuple-element.16), channel_id=1, source_target_pairs={{0,3},{1,4},{2,5},{3,6},{4,7},{5,0},{6,1},{7,2},{8,11},{9,12},{10,... | collective-permute-start | bytes 21512 | tf_op jit(solution)/shard_map/ppermute | solution.py:64
  8.5 1.2 %collective-permute-start.3 = (f32[1792]{0:T(1024)S(1)}, f32[1792]{0:T(1024)S(1)}, u32[]{:S(2)}, u32[]{:S(2)}) collective-permute-start(f32[1792]{0:T(1024)S(1)} %get-tuple-element.15), channel_id=1, source_target_pairs={{0,4},{1,5},{2,6},{3,7},{4,0},{5,1},{6,2},{7,3},{8,12},{9,13},{10,... | collective-permute-start | bytes 21512 | tf_op jit(solution)/shard_map/ppermute | solution.py:64
  9.8 2.6 %collective-permute-start.4 = (f32[1792]{0:T(1024)S(1)}, f32[1792]{0:T(1024)S(1)}, u32[]{:S(2)}, u32[]{:S(2)}) collective-permute-start(f32[1792]{0:T(1024)S(1)} %get-tuple-element.14), channel_id=1, source_target_pairs={{0,5},{1,6},{2,7},{3,0},{4,1},{5,2},{6,3},{7,4},{8,13},{9,14},{10,... | collective-permute-start | bytes 21512 | tf_op jit(solution)/shard_map/ppermute | solution.py:64
  12.4 0.7 compare_select_fusion.2
  13.0 0.7 fusion.69
  13.7 1.4 %gather_fusion.1 = f32[3,1792]{1,0:T(4,128)S(1)} fusion(f32[8,1792]{1,0:T(8,128)} %param.5, s32[1024]{0:T(1024)S(1)} %pad_clamp_fusion.2), kind=kCustom, calls=%fused_computation.1 | custom fusion | bytes 43020 | tf_op jit(solution)/shard_map/gather | solution.py:88
  15.3 0.1 add_multiply_fusion
  15.4 0.8 lt.253
  16.2 0.1 iota_compare_fusion
  16.4 0.6 gather_fusion.4
  16.9 0.7 add_select_fusion.4
  17.6 0.4 fusion.28
  18.1 0.3 fusion.30
  18.4 0.3 fusion.31
  18.7 0.4 fusion.17
  19.2 2.7 %broadcast_multiply_fusion = f32[48,48,448]{2,1,0:T(8,128)} fusion(f32[48,448]{1,0:T(8,128)S(1)} %fusion.31, f32[48,448]{1,0:T(8,128)S(1)} %fusion.30), kind=kLoop, calls=%fused_computation.19 | loop fusion | flops 1032192 | bytes 4300800 | tf_op jit(solution)/shard_map/mul | solution.py:49
  22.0 1.6 %collective-permute-start.8 = (f32[3,1792]{1,0:T(4,128)S(1)}, f32[3,1792]{1,0:T(4,128)S(1)}, u32[]{:S(2)}, u32[]{:S(2)}) collective-permute-start(f32[3,1792]{1,0:T(4,128)S(1)} %broadcast_select_fusion), channel_id=1, source_target_pairs={{0,16},{8,24},{16,0},{24,8},{1,17},{9,25},{17,1},{25,9},{2,18},{10... | collective-permute-start | bytes 64520 | tf_op jit(solution)/shard_map/ppermute | solution.py:64
  23.6 1.4 %collective-permute-start.9 = (f32[3,1792]{1,0:T(4,128)S(1)}, f32[3,1792]{1,0:T(4,128)S(1)}, u32[]{:S(2)}, u32[]{:S(2)}) collective-permute-start(f32[3,1792]{1,0:T(4,128)S(1)} %broadcast_select_fusion), channel_id=1, source_target_pairs={{0,24},{8,0},{16,8},{24,16},{1,25},{9,1},{17,9},{25,17},{2,26},{10... | collective-permute-start | bytes 64520 | tf_op jit(solution)/shard_map/ppermute | solution.py:64
  25.0 1.3 %collective-permute-start.5 = (f32[1792]{0:T(1024)S(1)}, f32[1792]{0:T(1024)S(1)}, u32[]{:S(2)}, u32[]{:S(2)}) collective-permute-start(f32[1792]{0:T(1024)S(1)} %get-tuple-element.13), channel_id=1, source_target_pairs={{0,6},{1,7},{2,0},{3,1},{4,2},{5,3},{6,4},{7,5},{8,14},{9,15},{10,... | collective-permute-start | bytes 21512 | tf_op jit(solution)/shard_map/ppermute | solution.py:64
  26.4 1.4 %collective-permute-start.6 = (f32[1792]{0:T(1024)S(1)}, f32[1792]{0:T(1024)S(1)}, u32[]{:S(2)}, u32[]{:S(2)}) collective-permute-start(f32[1792]{0:T(1024)S(1)} %get-tuple-element.12), channel_id=1, source_target_pairs={{0,7},{1,0},{2,1},{3,2},{4,3},{5,4},{6,5},{7,6},{8,15},{9,8},{10,9... | collective-permute-start | bytes 21512 | tf_op jit(solution)/shard_map/ppermute | solution.py:64
  28.0 0.6 gather_fusion.5
  28.7 1.3 %collective-permute-done.6 = f32[1792]{0:T(1024)S(1)} collective-permute-done((f32[1792]{0:T(1024)S(1)}, f32[1792]{0:T(1024)S(1)}, u32[]{:S(2)}, u32[]{:S(2)}) %collective-permute-start.6) | collective-permute-done | bytes 7200 | tf_op jit(solution)/shard_map/ppermute | solution.py:64
  30.1 0.6 gather_fusion
  30.7 0.1 concatenate.17
  30.9 0.6 gather_fusion.2
  31.5 1.6 %collective-permute-start.10 = (f32[3,1792]{1,0:T(4,128)S(1)}, f32[3,1792]{1,0:T(4,128)S(1)}, u32[]{:S(2)}, u32[]{:S(2)}) collective-permute-start(f32[3,1792]{1,0:T(4,128)S(1)} %reduce_sum.18), channel_id=1, source_target_pairs={{0,1},{1,2},{2,3},{3,4},{4,5},{5,6},{6,7},{7,0},{8,9},{9,10},{10,1... | collective-permute-start | bytes 64520 | tf_op jit(solution)/shard_map/ppermute | solution.py:64
  33.1 0.2 collective-permute-start.11
  33.4 2.1 %collective-permute-start.12 = (f32[3,1792]{1,0:T(4,128)S(1)}, f32[3,1792]{1,0:T(4,128)S(1)}, u32[]{:S(2)}, u32[]{:S(2)}) collective-permute-start(f32[3,1792]{1,0:T(4,128)S(1)} %reduce_sum.18), channel_id=1, source_target_pairs={{0,3},{1,4},{2,5},{3,6},{4,7},{5,0},{6,1},{7,2},{8,11},{9,12},{10,... | collective-permute-start | bytes 64520 | tf_op jit(solution)/shard_map/ppermute | solution.py:64
  35.4 2.1 %collective-permute-start.13 = (f32[3,1792]{1,0:T(4,128)S(1)}, f32[3,1792]{1,0:T(4,128)S(1)}, u32[]{:S(2)}, u32[]{:S(2)}) collective-permute-start(f32[3,1792]{1,0:T(4,128)S(1)} %reduce_sum.18), channel_id=1, source_target_pairs={{0,4},{1,5},{2,6},{3,7},{4,0},{5,1},{6,2},{7,3},{8,12},{9,13},{10,... | collective-permute-start | bytes 64520 | tf_op jit(solution)/shard_map/ppermute | solution.py:64
  37.6 3.1 %collective-permute-start.14 = (f32[3,1792]{1,0:T(4,128)S(1)}, f32[3,1792]{1,0:T(4,128)S(1)}, u32[]{:S(2)}, u32[]{:S(2)}) collective-permute-start(f32[3,1792]{1,0:T(4,128)S(1)} %reduce_sum.18), channel_id=1, source_target_pairs={{0,5},{1,6},{2,7},{3,0},{4,1},{5,2},{6,3},{7,4},{8,13},{9,14},{10,... | collective-permute-start | bytes 64520 | tf_op jit(solution)/shard_map/ppermute | solution.py:64
  40.7 0.1 collective-permute-start.15
  40.8 1.6 %collective-permute-start.16 = (f32[3,1792]{1,0:T(4,128)S(1)}, f32[3,1792]{1,0:T(4,128)S(1)}, u32[]{:S(2)}, u32[]{:S(2)}) collective-permute-start(f32[3,1792]{1,0:T(4,128)S(1)} %reduce_sum.18), channel_id=1, source_target_pairs={{0,7},{1,0},{2,1},{3,2},{4,3},{5,4},{6,5},{7,6},{8,15},{9,8},{10,9... | collective-permute-start | bytes 64520 | tf_op jit(solution)/shard_map/ppermute | solution.py:64
  42.6 2.0 %collective-permute-done.15 = f32[3,1792]{1,0:T(4,128)S(1)} collective-permute-done((f32[3,1792]{1,0:T(4,128)S(1)}, f32[3,1792]{1,0:T(4,128)S(1)}, u32[]{:S(2)}, u32[]{:S(2)}) %collective-permute-start.15) | collective-permute-done | bytes 21536 | tf_op jit(solution)/shard_map/ppermute | solution.py:64
  44.6 0.4 collective-permute-done.16
  44.9 0.7 gather_fusion.3
  45.7 0.2 concatenate.18
  46.0 0.7 fusion.35
  46.9 1.3 %copy-done = f32[48,48,448]{2,1,0:T(8,128)S(1)} copy-done((f32[48,48,448]{2,1,0:T(8,128)S(1)}, f32[48,48,448]{2,1,0:T(8,128)}, u32[]{:S(2)}) %copy-start) | copy-done | bytes 4128792
  48.2 4.0 %fusion.96 = f32[48,48,4,48]{3,1,2,0:T(8,128)S(1)} fusion(f32[48,48,448,1]{2,1,3,0:T(8,128)S(1)} %bitcast.97, f32[4,48,448,1]{2,1,0,3:T(8,128)S(1)} %bitcast.102), kind=kOutput, calls=%fused_computation.181 | convolution fusion | flops 1189085184 | bytes 6242304 | tf_op jit(solution)/shard_map/dot_general | solution.py:99
  52.4 1.7 %fusion.8 = f32[48,48,3,48]{3,1,2,0:T(8,128)S(1)} fusion(f32[48,48,4,48]{3,1,2,0:T(8,128)S(1)} %fusion.96, f32[48,48,48]{2,1,0:T(8,128)S(1)} %slice_bitcast_fusion), kind=kOutput, calls=%fused_computation.16 | convolution fusion | flops 95908608 | bytes 6045696 | tf_op jit(solution)/shard_map/absc,ck->absk/dot_general | solution.py:53
  54.1 1.9 %convolution_bitcast_fusion.1 = f32[48,48,3,48]{3,1,2,0:T(8,128)S(1)} fusion(f32[48,48,3,48]{3,1,2,0:T(8,128)S(1)} %fusion.8), kind=kOutput, calls=%fused_computation.21 | convolution fusion | flops 95576832 | bytes 2654208 | tf_op jit(solution)/shard_map/absc,kb->aksc/dot_general | solution.py:54
  56.0 3.0 %fusion.11 = f32[48,48,3,48]{3,0,2,1:T(8,128)S(1)} fusion(f32[48,48,3,48]{3,1,2,0:T(8,128)S(1)} %convolution_bitcast_fusion.1, f32[48,48,48]{2,0,1:T(8,128)S(1)} %fusion.17), kind=kOutput, calls=%fused_computation.22 | convolution fusion | flops 95908608 | bytes 3096576 | tf_op jit(solution)/shard_map/absc,ka->kbsc/dot_general | solution.py:55
  59.0 3.0 %fusion.4 = f32[48,48,3,48]{3,1,2,0:T(8,128)S(1)} fusion(f32[48,48,3,48]{3,0,2,1:T(8,128)S(1)} %fusion.11), kind=kOutput, calls=%fused_computation.12 | convolution fusion | flops 95576832 | bytes 2654208 | tf_op jit(solution)/shard_map/absc,ck->absk/dot_general | solution.py:53
  61.9 1.9 %convolution_bitcast_fusion = f32[48,48,3,48]{3,1,2,0:T(8,128)S(1)} fusion(f32[48,48,3,48]{3,1,2,0:T(8,128)S(1)} %fusion.4), kind=kOutput, calls=%fused_computation.20 | convolution fusion | flops 95576832 | bytes 2654208 | tf_op jit(solution)/shard_map/absc,kb->aksc/dot_general | solution.py:54
  63.8 3.0 %fusion.2 = f32[48,48,3,48]{3,0,2,1:T(8,128)S(1)} fusion(f32[48,48,3,48]{3,1,2,0:T(8,128)S(1)} %convolution_bitcast_fusion), kind=kOutput, calls=%fused_computation.10 | convolution fusion | flops 95576832 | bytes 2654208 | tf_op jit(solution)/shard_map/absc,ka->kbsc/dot_general | solution.py:55
  66.8 1.5 %fusion.1 = f32[48,48,48]{2,1,0:T(8,128)S(1)} fusion(f32[48,48,3,48]{3,0,2,1:T(8,128)S(1)} %fusion.2, f32[48,48,4,48]{3,1,2,0:T(8,128)S(1)} %fusion.96, f32[3]{0:T(128)S(1)} %copy-done.2), kind=kLoop, calls=%fused_computation.9 | loop fusion | flops 884736 | bytes 3096588 | tf_op jit(solution)/shard_map/reduce_sum | solution.py:105
  68.3 1.7 %fusion.34 = (f32[448,48]{0,1:T(8,128)S(1)}, f32[448,48]{0,1:T(8,128)S(1)}) fusion(s32[448]{0:T(512)S(1)} %get-tuple-element.29, f32[2304,448]{1,0:T(8,128)S(1)} %bitcast.98, f32[2304,48]{1,0:T(8,128)S(1)} %bitcast.99), kind=kOutput, calls=%fused_computation.59 | convolution fusion | flops 297529344 | bytes 4744960 | tf_op jit(solution)/shard_map/dot_general | solution.py:106
  70.0 0.2 fusion.18
  70.2 0.1 copy.35
  70.4 0.1 reshape.332
  70.5 0.2 dynamic-slice_reduce_fusion
  70.7 1.5 %collective-permute-start.17 = (f32[1792]{0:T(1024)S(1)}, f32[1792]{0:T(1024)S(1)}, u32[]{:S(2)}, u32[]{:S(2)}) collective-permute-start(f32[1792]{0:T(1024)S(1)} %get-tuple-element.11), channel_id=1, source_target_pairs={{0,1},{1,2},{2,3},{3,4},{4,5},{5,6},{6,7},{7,0},{8,9},{9,10},{10,1... | collective-permute-start | bytes 21512 | tf_op jit(solution)/shard_map/ppermute | solution.py:64
  72.2 1.9 %collective-permute-start.18 = (f32[1792]{0:T(1024)S(1)}, f32[1792]{0:T(1024)S(1)}, u32[]{:S(2)}, u32[]{:S(2)}) collective-permute-start(f32[1792]{0:T(1024)S(1)} %get-tuple-element.10), channel_id=1, source_target_pairs={{0,2},{1,3},{2,4},{3,5},{4,6},{5,7},{6,0},{7,1},{8,10},{9,11},{10,... | collective-permute-start | bytes 21512 | tf_op jit(solution)/shard_map/ppermute | solution.py:64
  74.1 0.4 collective-permute-start.19
  74.5 3.4 %collective-permute-start.20 = (f32[1792]{0:T(1024)S(1)}, f32[1792]{0:T(1024)S(1)}, u32[]{:S(2)}, u32[]{:S(2)}) collective-permute-start(f32[1792]{0:T(1024)S(1)} %get-tuple-element.8), channel_id=1, source_target_pairs={{0,4},{1,5},{2,6},{3,7},{4,0},{5,1},{6,2},{7,3},{8,12},{9,13},{10,... | collective-permute-start | bytes 21512 | tf_op jit(solution)/shard_map/ppermute | solution.py:64
  77.9 1.8 %collective-permute-start.21 = (f32[1792]{0:T(1024)S(1)}, f32[1792]{0:T(1024)S(1)}, u32[]{:S(2)}, u32[]{:S(2)}) collective-permute-start(f32[1792]{0:T(1024)S(1)} %get-tuple-element.7), channel_id=1, source_target_pairs={{0,5},{1,6},{2,7},{3,0},{4,1},{5,2},{6,3},{7,4},{8,13},{9,14},{10,... | collective-permute-start | bytes 21512 | tf_op jit(solution)/shard_map/ppermute | solution.py:64
  79.7 0.6 collective-permute-start.22
  80.3 2.1 %collective-permute-start.23 = (f32[1792]{0:T(1024)S(1)}, f32[1792]{0:T(1024)S(1)}, u32[]{:S(2)}, u32[]{:S(2)}) collective-permute-start(f32[1792]{0:T(1024)S(1)} %get-tuple-element.5), channel_id=1, source_target_pairs={{0,7},{1,0},{2,1},{3,2},{4,3},{5,4},{6,5},{7,6},{8,15},{9,8},{10,9... | collective-permute-start | bytes 21512 | tf_op jit(solution)/shard_map/ppermute | solution.py:64
  82.5 0.9 %collective-permute-done.22 = f32[1792]{0:T(1024)S(1)} collective-permute-done((f32[1792]{0:T(1024)S(1)}, f32[1792]{0:T(1024)S(1)}, u32[]{:S(2)}, u32[]{:S(2)}) %collective-permute-start.22) | collective-permute-done | bytes 7200 | tf_op jit(solution)/shard_map/ppermute | solution.py:64
  83.4 0.6 collective-permute-done.23
  84.1 1.2 %gather_fusion.6 = f32[8,1792]{1,0:T(8,128)} fusion(f32[8,1792]{1,0:T(8,128)S(1)} %stack.111, s32[1024]{0:T(1024)S(1)} %pad_clamp_fusion.3), kind=kCustom, calls=%fused_computation.6 | custom fusion | bytes 114720 | tf_op jit(solution)/shard_map/gather | solution.py:67
  (71 shorter events, 1.6 us)
Async XLA Ops:
  1.4 20.6 %collective-permute-start = (f32[1792]{0:T(1024)S(1)}, f32[1792]{0:T(1024)S(1)}, u32[]{:S(2)}, u32[]{:S(2)}) collective-permute-start(f32[1792]{0:T(1024)S(1)} %get-tuple-element.18), channel_id=1, source_target_pairs={{0,1},{1,2},{2,3},{3,4},{4,5},{5,6},{6,7},{7,0},{8,9},{9,10},{10,1... | collective-permute-start | bytes 21512 | tf_op jit(solution)/shard_map/ppermute | solution.py:64
  4.4 17.6 %collective-permute-start.1 = (f32[1792]{0:T(1024)S(1)}, f32[1792]{0:T(1024)S(1)}, u32[]{:S(2)}, u32[]{:S(2)}) collective-permute-start(f32[1792]{0:T(1024)S(1)} %get-tuple-element.17), channel_id=1, source_target_pairs={{0,2},{1,3},{2,4},{3,5},{4,6},{5,7},{6,0},{7,1},{8,10},{9,11},{10,... | collective-permute-start | bytes 21512 | tf_op jit(solution)/shard_map/ppermute | solution.py:64
  6.0 17.7 %collective-permute-start.2 = (f32[1792]{0:T(1024)S(1)}, f32[1792]{0:T(1024)S(1)}, u32[]{:S(2)}, u32[]{:S(2)}) collective-permute-start(f32[1792]{0:T(1024)S(1)} %get-tuple-element.16), channel_id=1, source_target_pairs={{0,3},{1,4},{2,5},{3,6},{4,7},{5,0},{6,1},{7,2},{8,11},{9,12},{10,... | collective-permute-start | bytes 21512 | tf_op jit(solution)/shard_map/ppermute | solution.py:64
  8.5 16.5 %collective-permute-start.3 = (f32[1792]{0:T(1024)S(1)}, f32[1792]{0:T(1024)S(1)}, u32[]{:S(2)}, u32[]{:S(2)}) collective-permute-start(f32[1792]{0:T(1024)S(1)} %get-tuple-element.15), channel_id=1, source_target_pairs={{0,4},{1,5},{2,6},{3,7},{4,0},{5,1},{6,2},{7,3},{8,12},{9,13},{10,... | collective-permute-start | bytes 21512 | tf_op jit(solution)/shard_map/ppermute | solution.py:64
  9.8 16.6 %collective-permute-start.4 = (f32[1792]{0:T(1024)S(1)}, f32[1792]{0:T(1024)S(1)}, u32[]{:S(2)}, u32[]{:S(2)}) collective-permute-start(f32[1792]{0:T(1024)S(1)} %get-tuple-element.14), channel_id=1, source_target_pairs={{0,5},{1,6},{2,7},{3,0},{4,1},{5,2},{6,3},{7,4},{8,13},{9,14},{10,... | collective-permute-start | bytes 21512 | tf_op jit(solution)/shard_map/ppermute | solution.py:64
  22.0 8.9 %collective-permute-start.7 = (f32[3,1792]{1,0:T(4,128)S(1)}, f32[3,1792]{1,0:T(4,128)S(1)}, u32[]{:S(2)}, u32[]{:S(2)}) collective-permute-start(f32[3,1792]{1,0:T(4,128)S(1)} %broadcast_select_fusion), channel_id=1, source_target_pairs={{0,8},{8,16},{16,24},{24,0},{1,9},{9,17},{17,25},{25,1},{2,10},{10... | collective-permute-start | bytes 64520 | tf_op jit(solution)/shard_map/ppermute | solution.py:64
  22.0 8.8 %collective-permute-start.8 = (f32[3,1792]{1,0:T(4,128)S(1)}, f32[3,1792]{1,0:T(4,128)S(1)}, u32[]{:S(2)}, u32[]{:S(2)}) collective-permute-start(f32[3,1792]{1,0:T(4,128)S(1)} %broadcast_select_fusion), channel_id=1, source_target_pairs={{0,16},{8,24},{16,0},{24,8},{1,17},{9,25},{17,1},{25,9},{2,18},{10... | collective-permute-start | bytes 64520 | tf_op jit(solution)/shard_map/ppermute | solution.py:64
  23.6 7.2 %collective-permute-start.9 = (f32[3,1792]{1,0:T(4,128)S(1)}, f32[3,1792]{1,0:T(4,128)S(1)}, u32[]{:S(2)}, u32[]{:S(2)}) collective-permute-start(f32[3,1792]{1,0:T(4,128)S(1)} %broadcast_select_fusion), channel_id=1, source_target_pairs={{0,24},{8,0},{16,8},{24,16},{1,25},{9,1},{17,9},{25,17},{2,26},{10... | collective-permute-start | bytes 64520 | tf_op jit(solution)/shard_map/ppermute | solution.py:64
  25.0 3.7 %collective-permute-start.5 = (f32[1792]{0:T(1024)S(1)}, f32[1792]{0:T(1024)S(1)}, u32[]{:S(2)}, u32[]{:S(2)}) collective-permute-start(f32[1792]{0:T(1024)S(1)} %get-tuple-element.13), channel_id=1, source_target_pairs={{0,6},{1,7},{2,0},{3,1},{4,2},{5,3},{6,4},{7,5},{8,14},{9,15},{10,... | collective-permute-start | bytes 21512 | tf_op jit(solution)/shard_map/ppermute | solution.py:64
  26.4 3.7 %collective-permute-start.6 = (f32[1792]{0:T(1024)S(1)}, f32[1792]{0:T(1024)S(1)}, u32[]{:S(2)}, u32[]{:S(2)}) collective-permute-start(f32[1792]{0:T(1024)S(1)} %get-tuple-element.12), channel_id=1, source_target_pairs={{0,7},{1,0},{2,1},{3,2},{4,3},{5,4},{6,5},{7,6},{8,15},{9,8},{10,9... | collective-permute-start | bytes 21512 | tf_op jit(solution)/shard_map/ppermute | solution.py:64
  31.5 9.1 %collective-permute-start.10 = (f32[3,1792]{1,0:T(4,128)S(1)}, f32[3,1792]{1,0:T(4,128)S(1)}, u32[]{:S(2)}, u32[]{:S(2)}) collective-permute-start(f32[3,1792]{1,0:T(4,128)S(1)} %reduce_sum.18), channel_id=1, source_target_pairs={{0,1},{1,2},{2,3},{3,4},{4,5},{5,6},{6,7},{7,0},{8,9},{9,10},{10,1... | collective-permute-start | bytes 64520 | tf_op jit(solution)/shard_map/ppermute | solution.py:64
  33.1 7.7 %collective-permute-start.11 = (f32[3,1792]{1,0:T(4,128)S(1)}, f32[3,1792]{1,0:T(4,128)S(1)}, u32[]{:S(2)}, u32[]{:S(2)}) collective-permute-start(f32[3,1792]{1,0:T(4,128)S(1)} %reduce_sum.18), channel_id=1, source_target_pairs={{0,2},{1,3},{2,4},{3,5},{4,6},{5,7},{6,0},{7,1},{8,10},{9,11},{10,... | collective-permute-start | bytes 64520 | tf_op jit(solution)/shard_map/ppermute | solution.py:64
  33.4 9.1 %collective-permute-start.12 = (f32[3,1792]{1,0:T(4,128)S(1)}, f32[3,1792]{1,0:T(4,128)S(1)}, u32[]{:S(2)}, u32[]{:S(2)}) collective-permute-start(f32[3,1792]{1,0:T(4,128)S(1)} %reduce_sum.18), channel_id=1, source_target_pairs={{0,3},{1,4},{2,5},{3,6},{4,7},{5,0},{6,1},{7,2},{8,11},{9,12},{10,... | collective-permute-start | bytes 64520 | tf_op jit(solution)/shard_map/ppermute | solution.py:64
  35.4 7.0 %collective-permute-start.13 = (f32[3,1792]{1,0:T(4,128)S(1)}, f32[3,1792]{1,0:T(4,128)S(1)}, u32[]{:S(2)}, u32[]{:S(2)}) collective-permute-start(f32[3,1792]{1,0:T(4,128)S(1)} %reduce_sum.18), channel_id=1, source_target_pairs={{0,4},{1,5},{2,6},{3,7},{4,0},{5,1},{6,2},{7,3},{8,12},{9,13},{10,... | collective-permute-start | bytes 64520 | tf_op jit(solution)/shard_map/ppermute | solution.py:64
  37.6 5.0 %collective-permute-start.14 = (f32[3,1792]{1,0:T(4,128)S(1)}, f32[3,1792]{1,0:T(4,128)S(1)}, u32[]{:S(2)}, u32[]{:S(2)}) collective-permute-start(f32[3,1792]{1,0:T(4,128)S(1)} %reduce_sum.18), channel_id=1, source_target_pairs={{0,5},{1,6},{2,7},{3,0},{4,1},{5,2},{6,3},{7,4},{8,13},{9,14},{10,... | collective-permute-start | bytes 64520 | tf_op jit(solution)/shard_map/ppermute | solution.py:64
  40.7 3.9 %collective-permute-start.15 = (f32[3,1792]{1,0:T(4,128)S(1)}, f32[3,1792]{1,0:T(4,128)S(1)}, u32[]{:S(2)}, u32[]{:S(2)}) collective-permute-start(f32[3,1792]{1,0:T(4,128)S(1)} %reduce_sum.18), channel_id=1, source_target_pairs={{0,6},{1,7},{2,0},{3,1},{4,2},{5,3},{6,4},{7,5},{8,14},{9,15},{10,... | collective-permute-start | bytes 64520 | tf_op jit(solution)/shard_map/ppermute | solution.py:64
  40.8 4.1 %collective-permute-start.16 = (f32[3,1792]{1,0:T(4,128)S(1)}, f32[3,1792]{1,0:T(4,128)S(1)}, u32[]{:S(2)}, u32[]{:S(2)}) collective-permute-start(f32[3,1792]{1,0:T(4,128)S(1)} %reduce_sum.18), channel_id=1, source_target_pairs={{0,7},{1,0},{2,1},{3,2},{4,3},{5,4},{6,5},{7,6},{8,15},{9,8},{10,9... | collective-permute-start | bytes 64520 | tf_op jit(solution)/shard_map/ppermute | solution.py:64
  45.9 2.3 %copy-start = (f32[48,48,448]{2,1,0:T(8,128)S(1)}, f32[48,48,448]{2,1,0:T(8,128)}, u32[]{:S(2)}) copy-start(f32[48,48,448]{2,1,0:T(8,128)} %broadcast_multiply_fusion) | copy-start | bytes 12386308
  63.8 3.0 %copy-start.2 = (f32[3]{0:T(128)S(1)}, f32[3]{0:T(128)}, u32[]{:S(2)}) copy-start(f32[3]{0:T(128)} %param.9) | copy-start | bytes 40
  68.3 1.7 %copy-start.1 = (s32[448]{0:T(512)S(1)}, s32[448]{0:T(512)}, u32[]{:S(2)}) copy-start(s32[448]{0:T(512)} %param.7) | copy-start | bytes 5380
  70.7 9.1 %collective-permute-start.17 = (f32[1792]{0:T(1024)S(1)}, f32[1792]{0:T(1024)S(1)}, u32[]{:S(2)}, u32[]{:S(2)}) collective-permute-start(f32[1792]{0:T(1024)S(1)} %get-tuple-element.11), channel_id=1, source_target_pairs={{0,1},{1,2},{2,3},{3,4},{4,5},{5,6},{6,7},{7,0},{8,9},{9,10},{10,1... | collective-permute-start | bytes 21512 | tf_op jit(solution)/shard_map/ppermute | solution.py:64
  72.2 8.1 %collective-permute-start.18 = (f32[1792]{0:T(1024)S(1)}, f32[1792]{0:T(1024)S(1)}, u32[]{:S(2)}, u32[]{:S(2)}) collective-permute-start(f32[1792]{0:T(1024)S(1)} %get-tuple-element.10), channel_id=1, source_target_pairs={{0,2},{1,3},{2,4},{3,5},{4,6},{5,7},{6,0},{7,1},{8,10},{9,11},{10,... | collective-permute-start | bytes 21512 | tf_op jit(solution)/shard_map/ppermute | solution.py:64
  74.1 8.3 %collective-permute-start.19 = (f32[1792]{0:T(1024)S(1)}, f32[1792]{0:T(1024)S(1)}, u32[]{:S(2)}, u32[]{:S(2)}) collective-permute-start(f32[1792]{0:T(1024)S(1)} %get-tuple-element.9), channel_id=1, source_target_pairs={{0,3},{1,4},{2,5},{3,6},{4,7},{5,0},{6,1},{7,2},{8,11},{9,12},{10,... | collective-permute-start | bytes 21512 | tf_op jit(solution)/shard_map/ppermute | solution.py:64
  74.5 8.0 %collective-permute-start.20 = (f32[1792]{0:T(1024)S(1)}, f32[1792]{0:T(1024)S(1)}, u32[]{:S(2)}, u32[]{:S(2)}) collective-permute-start(f32[1792]{0:T(1024)S(1)} %get-tuple-element.8), channel_id=1, source_target_pairs={{0,4},{1,5},{2,6},{3,7},{4,0},{5,1},{6,2},{7,3},{8,12},{9,13},{10,... | collective-permute-start | bytes 21512 | tf_op jit(solution)/shard_map/ppermute | solution.py:64
  77.9 4.6 %collective-permute-start.21 = (f32[1792]{0:T(1024)S(1)}, f32[1792]{0:T(1024)S(1)}, u32[]{:S(2)}, u32[]{:S(2)}) collective-permute-start(f32[1792]{0:T(1024)S(1)} %get-tuple-element.7), channel_id=1, source_target_pairs={{0,5},{1,6},{2,7},{3,0},{4,1},{5,2},{6,3},{7,4},{8,13},{9,14},{10,... | collective-permute-start | bytes 21512 | tf_op jit(solution)/shard_map/ppermute | solution.py:64
  79.7 3.7 %collective-permute-start.22 = (f32[1792]{0:T(1024)S(1)}, f32[1792]{0:T(1024)S(1)}, u32[]{:S(2)}, u32[]{:S(2)}) collective-permute-start(f32[1792]{0:T(1024)S(1)} %get-tuple-element.6), channel_id=1, source_target_pairs={{0,6},{1,7},{2,0},{3,1},{4,2},{5,3},{6,4},{7,5},{8,14},{9,15},{10,... | collective-permute-start | bytes 21512 | tf_op jit(solution)/shard_map/ppermute | solution.py:64
  80.3 3.7 %collective-permute-start.23 = (f32[1792]{0:T(1024)S(1)}, f32[1792]{0:T(1024)S(1)}, u32[]{:S(2)}, u32[]{:S(2)}) collective-permute-start(f32[1792]{0:T(1024)S(1)} %get-tuple-element.5), channel_id=1, source_target_pairs={{0,7},{1,0},{2,1},{3,2},{4,3},{5,4},{6,5},{7,6},{8,15},{9,8},{10,9... | collective-permute-start | bytes 21512 | tf_op jit(solution)/shard_map/ppermute | solution.py:64

commit v2 on v0

--- a/solution.py
+++ b/solution.py
@@ -62,23 +62,25 @@
         width = orbitals.shape[1]
         depth = width * n_col // count
         n_src = sources.shape[0]
-        table = cas_matrix(extent)
+
+        g = lax.axis_index("grp")
+        owner = sources // n_grp_bands
+        rows = (sources % n_grp_bands)[:, None] == jnp.arange(n_grp_bands, dtype=jnp.int32)[None, :]
+        picked = jnp.dot(rows.astype(jnp.float32), orbitals, precision=HI)
+        picked = jnp.where((owner == g)[:, None], picked, 0.0)
+        spread = jnp.broadcast_to(picked[None], (n_grp, n_src, width))
+        picked = jnp.sum(lax.all_to_all(spread, "grp", 0, 0, tiled=True), axis=0)
+        send = jnp.concatenate(
+            [orbitals[:, None, :], jnp.broadcast_to(picked[None], (n_grp_bands, n_src, width))], axis=1)
+        send, column_cell, column_length = lax.optimization_barrier((send, column_cell, column_length))
+        got = lax.all_to_all(send, "col", 0, 0, tiled=True)
+        table = cas_matrix(extent) + 0.0 * column_length[0]
         kernel = kernel_grid(extent)
         cos_h, sin_h, live = shift_tables(column_length, depth, extent)
         slot = jnp.arange(depth, dtype=jnp.int32)
         fwd = jnp.concatenate([table[:depth], table[(extent - slot) % extent]], axis=1)
         bwd = jnp.concatenate([table[:, :depth], table[:, (extent - slot) % extent]], axis=0)
         w = lax.optimization_barrier(plane_matrix(column_cell, table, extent))
-
-        g = lax.axis_index("grp")
-        owner = sources // n_grp_bands
-        picked = orbitals[sources % n_grp_bands]
-        picked = jnp.where((owner == g)[:, None], picked, 0.0)
-        spread = jnp.broadcast_to(picked[None], (n_grp, n_src, width))
-        picked = jnp.sum(lax.all_to_all(spread, "grp", 0, 0, tiled=True), axis=0)
-        send = jnp.concatenate(
-            [orbitals[:, None, :], jnp.broadcast_to(picked[None], (n_grp_bands, n_src, width))], axis=1)
-        got = lax.all_to_all(send, "col", 0, 0, tiled=True)
         n = 1 + n_src
         coeff = got.reshape(n_col, n, width // depth, depth).transpose(0, 2, 1, 3).reshape(count, n, depth)
         coeff = jnp.where(live[:, None, :], coeff, 0.0)

time: 68.7 us -> 66.8 us (0.972)
  waiting for transfers between devices: 8.61 us -> 6.62 us
  other arithmetic: 9.24 us -> 7.81 us
  matrix products: 21.6 us -> 22.7 us
    all_to_all x1, waiting for transfers between devices: 8.61 us -> 3.53 us  [local(): got = lax.all_to_all(send, 'col', 0, 0, tiled=True)]
    all_to_all x1, waiting for transfers between devices: 0.01 us -> 3.09 us  [local(): picked = jnp.sum(lax.all_to_all(spread, 'grp', 0, 0, tiled=True), axis=0)]
    gather x1 -> x0, local copies, waits for them, and re-layouts: 1.39 us -> none  [local(): picked = orbitals[sources % n_grp_bands]]
    slice x0 -> x1, local copies, waits for them, and re-layouts: none -> 1.19 us  [local(): table = cas_matrix(extent) + 0.0 * column_length[0]]
    dot_general x0 -> x1, matrix products: none -> 1.03 us  [local(): picked = jnp.dot(rows.astype(jnp.float32), orbitals, precision=HI)]
    select_n x3 -> x1, other arithmetic: 1.43 us -> 0.69 us  [local(): sources % n_grp_bands]
    unnamed x7 -> x9, local copies, waits for them, and re-layouts: 1.97 us -> 1.97 us
  transfers between devices with their start and end apart: 2 -> 2, of which waited for: 1 -> 2; matrix products, arithmetic and copies ran while one was open for 13% -> 9% of each run, Pallas kernels for 0% -> 0%
where the time goes in v2:
time: 66.8 us; the launch traced here: 66.2 us
  matrix products  22.7 us (34%)
  starting transfers between devices  10.5 us (16%)
  blocking collectives  10 us (15%)
  other arithmetic  7.81 us (12%)
  local copies, waits for them, and re-layouts  7.62 us (11%)
  waiting for transfers between devices  6.62 us (10%)
  between operations  0.93 us (1%)
    all_to_all x1, blocking collectives, local(): lax.all_to_all(out.reshape(n_col, 1, width), 'col', 0, 0, tiled=True)  10 us
    all_to_all x1, starting transfers between devices, local(): got = lax.all_to_all(send, 'col', 0, 0, tiled=True)  6.31 us
    dot_general x2, matrix products, cas_three(): return jnp.einsum('absc,ka->kbsc', field, table, precision=MID)  6.14 us
    dot_general x2, matrix products, cas_three(): field = jnp.einsum('absc,ck->absk', field, table, precision=MID)  4.45 us
    all_to_all x1, starting transfers between devices, local(): picked = jnp.sum(lax.all_to_all(spread, 'grp', 0, 0, tiled=True), axis=0)  4.24 us
    dot_general x1, matrix products, local(): grids = jnp.dot(w, cols.reshape(count, n * extent), precision=MID)  4.04 us
    dot_general x2, matrix products, cas_three(): field = jnp.einsum('absc,kb->aksc', field, table, precision=MID)  3.76 us
    all_to_all x1, waiting for transfers between devices, local(): got = lax.all_to_all(send, 'col', 0, 0, tiled=True)  3.53 us
  transfers between devices with their start and end apart: 2, of which 2 were waited for; matrix products, arithmetic and copies ran while one was open for 9% of the time, Pallas kernels for 0%

profile of v2, /device:TPU:0, one launch (start us, length us, event | category | flops | bytes accessed | tf_op | source)
XLA Modules:
  0.0 66.2 jit_solution(7048241533448565824)
XLA Ops:
  0.0 0.0 copy-start.2
  0.0 0.0 copy-start.1
  0.0 0.7 %and_select_fusion.1 = s32[3]{0:T(128)S(1)} fusion(s32[3]{0:T(128)} %param.8), kind=kLoop, calls=%fused_computation.93 | loop fusion | flops 33 | bytes 24 | tf_op jit(solution)/shard_map/jit(remainder)/select_n | solution.py:68
  0.7 0.7 %fusion.58 = pred[3]{0:T(512)(128)(4,1)S(1)} fusion(s32[3]{0:T(128)} %param.8, s32[]{:T(128)S(6)} %axis_index.15), kind=kLoop, calls=%fused_computation.103 | loop fusion | flops 48 | bytes 19 | tf_op jit(solution)/shard_map/eq | solution.py:70
  1.4 1.0 %convolution_select_fusion = f32[3,1792]{1,0:T(4,128)S(1)} fusion(f32[8,1792]{1,0:T(8,128)} %param.5, pred[3]{0:T(512)(128)(4,1)S(1)} %fusion.58, s32[3]{0:T(128)S(1)} %and_select_fusion.1), kind=kOutput, calls=%fused_computation.15 | convolution fusion | flops 521496 | bytes 78863 | tf_op jit(solution)/shard_map/dot_general | solution.py:69
  2.4 0.7 broadcast_in_dim.36
  3.1 4.2 %all-to-all-start = ((f32[4,3,1792]{2,1,0:T(4,128)}), f32[4,3,1792]{2,1,0:T(4,128)S(1)}, u32[]{:S(2)}, u32[]{:S(2)}) async-start(f32[4,3,1792]{2,1,0:T(4,128)} %broadcast_in_dim.36), calls=%async_computation | async-start | bytes 229376 | tf_op jit(solution)/shard_map/all_to_all | solution.py:72
  7.3 0.9 %broadcast_in_dim.33 = f32[8,1,1792]{2,1,0:T(1,128)S(1)} reshape(f32[8,1792]{1,0:T(8,128)} %param.5) | data formatting | bytes 114688 | tf_op jit(solution)/shard_map/broadcast_in_dim | solution.py:74
  8.2 0.1 broadcast_add_fusion
  8.3 0.4 fusion.17
  8.7 3.1 %all-to-all-done = f32[4,3,1792]{2,1,0:T(4,128)S(1)} async-done(((f32[4,3,1792]{2,1,0:T(4,128)}), f32[4,3,1792]{2,1,0:T(4,128)S(1)}, u32[]{:S(2)}, u32[]{:S(2)}) %all-to-all-start) | async-done | bytes 86048 | tf_op jit(solution)/shard_map/all_to_all | solution.py:72
  11.8 0.8 %pad_maximum_fusion = f32[8,4,1792]{2,1,0:T(4,128)} fusion(f32[8,3,1792]{2,1,0:T(4,128)S(1)} %broadcast_in_dim.37, f32[8,1,1792]{2,1,0:T(1,128)S(1)} %broadcast_in_dim.33), kind=kLoop, calls=%fused_computation.32 | loop fusion | flops 57344 | bytes 458752 | tf_op jit(solution)/shard_map/concatenate | solution.py:73
  12.6 1.2 %slice.21 = s32[1]{0:T(128)} slice(s32[448]{0:T(512)} %param.7), slice={[0:1]} | slice | bytes 8 | tf_op jit(solution)/shard_map/slice | solution.py:77
  13.8 0.8 %lt.80 = s32[8,56]{1,0:T(8,128)S(1)} reshape(s32[448]{0:T(512)} %param.7) | data formatting | bytes 3584 | tf_op jit(solution)/shard_map/lt | solution.py:39
  15.3 0.1 multiply_add_fusion
  15.4 0.1 copy.46
  15.5 0.6 gather_fusion
  16.0 0.1 maximum_bitcast_fusion
  16.1 0.1 dot_general.54
  16.2 6.3 %all-to-all-start.1 = ((f32[8,4,1792]{2,1,0:T(4,128)}), f32[8,4,1792]{2,1,0:T(4,128)S(1)}, u32[]{:S(2)}, u32[]{:S(2)}) async-start(f32[8,4,1792]{2,1,0:T(4,128)} %pad_maximum_fusion), calls=%async_computation.1 | async-start | bytes 458752 | tf_op jit(solution)/shard_map/all_to_all | solution.py:76
  22.5 0.0 copy-done.2
  22.5 0.0 copy-done.1
  22.6 0.3 fusion.30
  22.9 0.3 fusion.31
  23.2 2.7 %broadcast_multiply_fusion = f32[48,48,448]{2,1,0:T(8,128)} fusion(f32[48,448]{1,0:T(8,128)S(1)} %fusion.31, f32[48,448]{1,0:T(8,128)S(1)} %fusion.30), kind=kLoop, calls=%fused_computation.14 | loop fusion | flops 1032192 | bytes 4300800 | tf_op jit(solution)/shard_map/mul | solution.py:49
  25.9 0.6 gather_fusion.1
  26.5 0.1 copy.47
  26.6 0.1 iota_compare_fusion
  26.7 0.4 fusion.28
  27.1 3.5 %all-to-all-done.1 = f32[8,4,1792]{2,1,0:T(4,128)S(1)} async-done(((f32[8,4,1792]{2,1,0:T(4,128)}), f32[8,4,1792]{2,1,0:T(4,128)S(1)}, u32[]{:S(2)}, u32[]{:S(2)}) %all-to-all-start.1) | async-done | bytes 229408 | tf_op jit(solution)/shard_map/all_to_all | solution.py:76
  30.7 0.3 reshape.210
  31.0 0.0 copy-start
  31.0 0.1 broadcast_select_fusion
  31.1 0.7 %fusion.35 = f32[448,4,2,48]{0,3,2,1:T(8,128)S(1)} fusion(f32[448,4,32,1]{2,0,3,1:T(8,128)S(1)} %bitcast.80, f32[2,48,32]{1,0,2:T(2,128)S(1)} %dot_general.54), kind=kOutput, calls=%fused_computation.57 | convolution fusion | flops 33030144 | bytes 929792 | tf_op jit(solution)/shard_map/dot_general | solution.py:87
  31.8 0.1 fusion.92
  31.9 0.1 fusion.19
  32.0 1.3 %copy-done = f32[48,48,448]{2,1,0:T(8,128)S(1)} copy-done((f32[48,48,448]{2,1,0:T(8,128)S(1)}, f32[48,48,448]{2,1,0:T(8,128)}, u32[]{:S(2)}) %copy-start) | copy-done | bytes 4128792
  33.3 4.0 %fusion.93 = f32[48,48,4,48]{3,1,2,0:T(8,128)S(1)} fusion(f32[48,48,448,1]{2,1,3,0:T(8,128)S(1)} %bitcast.77, f32[4,48,448,1]{2,1,0,3:T(8,128)S(1)} %bitcast.82), kind=kOutput, calls=%fused_computation.138 | convolution fusion | flops 1189085184 | bytes 6242304 | tf_op jit(solution)/shard_map/dot_general | solution.py:89
  37.4 0.1 slice_bitcast_fusion
  37.5 1.7 %fusion.8 = f32[48,48,3,48]{3,1,2,0:T(8,128)S(1)} fusion(f32[48,48,4,48]{3,1,2,0:T(8,128)S(1)} %fusion.93, f32[48,48,48]{2,1,0:T(8,128)S(1)} %slice_bitcast_fusion, f32[]{:T(128)} %bitcast), kind=kOutput, calls=%fused_computation.11 | convolution fusion | flops 95910912 | bytes 6045700 | tf_op jit(solution)/shard_map/absc,ck->absk/dot_general | solution.py:53
  39.2 1.9 %convolution_bitcast_fusion.1 = f32[48,48,3,48]{3,1,2,0:T(8,128)S(1)} fusion(f32[48,48,3,48]{3,1,2,0:T(8,128)S(1)} %fusion.8, f32[]{:T(128)} %bitcast), kind=kOutput, calls=%fused_computation.17 | convolution fusion | flops 95579136 | bytes 2654212 | tf_op jit(solution)/shard_map/absc,kb->aksc/dot_general | solution.py:54
  41.0 3.2 %fusion.11 = f32[48,48,3,48]{3,0,2,1:T(8,128)S(1)} fusion(f32[48,48,3,48]{3,1,2,0:T(8,128)S(1)} %convolution_bitcast_fusion.1, f32[48,48,48]{2,0,1:T(8,128)S(1)} %fusion.17, f32[]{:T(128)} %bitcast), kind=kOutput, calls=%fused_computation.18 | convolution fusion | flops 95910912 | bytes 3096580 | tf_op jit(solution)/shard_map/absc,ka->kbsc/dot_general | solution.py:55
  44.2 2.8 %fusion.4 = f32[48,48,3,48]{3,1,2,0:T(8,128)S(1)} fusion(f32[48,48,3,48]{3,0,2,1:T(8,128)S(1)} %fusion.11, f32[]{:T(128)} %bitcast), kind=kOutput, calls=%fused_computation.7 | convolution fusion | flops 95579136 | bytes 2654212 | tf_op jit(solution)/shard_map/absc,ck->absk/dot_general | solution.py:53
  47.0 1.9 %convolution_bitcast_fusion = f32[48,48,3,48]{3,1,2,0:T(8,128)S(1)} fusion(f32[48,48,3,48]{3,1,2,0:T(8,128)S(1)} %fusion.4, f32[]{:T(128)} %bitcast), kind=kOutput, calls=%fused_computation.16 | convolution fusion | flops 95579136 | bytes 2654212 | tf_op jit(solution)/shard_map/absc,kb->aksc/dot_general | solution.py:54
  48.9 0.0 copy-start.3
  48.9 3.0 %fusion.2 = f32[48,48,3,48]{3,0,2,1:T(8,128)S(1)} fusion(f32[48,48,3,48]{3,1,2,0:T(8,128)S(1)} %convolution_bitcast_fusion, f32[]{:T(128)} %bitcast), kind=kOutput, calls=%fused_computation.5 | convolution fusion | flops 95579136 | bytes 2654212 | tf_op jit(solution)/shard_map/absc,ka->kbsc/dot_general | solution.py:55
  51.9 0.0 copy-done.3
  51.9 1.5 %fusion.1 = f32[48,48,48]{2,1,0:T(8,128)S(1)} fusion(f32[48,48,3,48]{3,0,2,1:T(8,128)S(1)} %fusion.2, f32[48,48,4,48]{3,1,2,0:T(8,128)S(1)} %fusion.93, f32[3]{0:T(128)S(1)} %copy-done.3), kind=kLoop, calls=%fused_computation.4 | loop fusion | flops 884736 | bytes 3096588 | tf_op jit(solution)/shard_map/reduce_sum | solution.py:95
  53.4 1.7 %fusion.34 = (f32[448,48]{0,1:T(8,128)S(1)}, f32[448,48]{0,1:T(8,128)S(1)}) fusion(s32[448]{0:T(512)S(1)} %get-tuple-element.19, f32[2304,448]{1,0:T(8,128)S(1)} %bitcast.78, f32[2304,48]{1,0:T(8,128)S(1)} %bitcast.79), kind=kOutput, calls=%fused_computation.56 | convolution fusion | flops 297529344 | bytes 4744960 | tf_op jit(solution)/shard_map/dot_general | solution.py:96
  55.1 0.2 fusion.18
  55.3 0.1 copy.48
  55.4 0.2 reshape.235
  55.6 10.0 %all_to_all.15 = f32[8,1,1792]{2,1,0:T(1,128)S(1)} all-to-all(f32[8,1,1792]{2,1,0:T(1,128)S(1)} %reshape.235), channel_id=1, replica_groups=mesh['grp'=4,'col'=8] {'col'}, dimensions={0} | all-to-all | bytes 114688 | tf_op jit(solution)/shard_map/all_to_all | solution.py:100
  65.6 0.6 copy.75
  (8 shorter events, 0.2 us)
Async XLA Ops:
  0.0 22.5 %copy-start.2 = (s32[448]{0:T(512)S(1)}, s32[448]{0:T(512)}, u32[]{:S(2)}) copy-start(s32[448]{0:T(512)} %param.6) | copy-start | bytes 5380
  0.0 22.5 %copy-start.1 = (s32[448]{0:T(512)S(1)}, s32[448]{0:T(512)}, u32[]{:S(2)}) copy-start(s32[448]{0:T(512)} %param.7) | copy-start | bytes 5380
  3.1 8.7 %all-to-all-start = ((f32[4,3,1792]{2,1,0:T(4,128)}), f32[4,3,1792]{2,1,0:T(4,128)S(1)}, u32[]{:S(2)}, u32[]{:S(2)}) async-start(f32[4,3,1792]{2,1,0:T(4,128)} %broadcast_in_dim.36), calls=%async_computation | async-start | bytes 229376 | tf_op jit(solution)/shard_map/all_to_all | solution.py:72
  16.2 14.4 %all-to-all-start.1 = ((f32[8,4,1792]{2,1,0:T(4,128)}), f32[8,4,1792]{2,1,0:T(4,128)S(1)}, u32[]{:S(2)}, u32[]{:S(2)}) async-start(f32[8,4,1792]{2,1,0:T(4,128)} %pad_maximum_fusion), calls=%async_computation.1 | async-start | bytes 458752 | tf_op jit(solution)/shard_map/all_to_all | solution.py:76
  31.0 2.3 %copy-start = (f32[48,48,448]{2,1,0:T(8,128)S(1)}, f32[48,48,448]{2,1,0:T(8,128)}, u32[]{:S(2)}) copy-start(f32[48,48,448]{2,1,0:T(8,128)} %broadcast_multiply_fusion) | copy-start | bytes 12386308
  48.9 3.0 %copy-start.3 = (f32[3]{0:T(128)S(1)}, f32[3]{0:T(128)}, u32[]{:S(2)}) copy-start(f32[3]{0:T(128)} %param.9) | copy-start | bytes 40

commit v3 on v2

--- a/solution.py
+++ b/solution.py
@@ -69,11 +69,13 @@
         picked = jnp.dot(rows.astype(jnp.float32), orbitals, precision=HI)
         picked = jnp.where((owner == g)[:, None], picked, 0.0)
         spread = jnp.broadcast_to(picked[None], (n_grp, n_src, width))
-        picked = jnp.sum(lax.all_to_all(spread, "grp", 0, 0, tiled=True), axis=0)
+        spread = spread.reshape(n_grp, n_src * width // 128, 128)
+        picked = jnp.sum(lax.all_to_all(spread, "grp", 0, 0, tiled=True), axis=0).reshape(n_src, width)
         send = jnp.concatenate(
             [orbitals[:, None, :], jnp.broadcast_to(picked[None], (n_grp_bands, n_src, width))], axis=1)
         send, column_cell, column_length = lax.optimization_barrier((send, column_cell, column_length))
-        got = lax.all_to_all(send, "col", 0, 0, tiled=True)
+        got = lax.all_to_all(send.reshape(n_grp_bands, -1, 128), "col", 0, 0, tiled=True)
+        got = got.reshape(n_col, 1 + n_src, width)
         table = cas_matrix(extent) + 0.0 * column_length[0]
         kernel = kernel_grid(extent)
         cos_h, sin_h, live = shift_tables(column_length, depth, extent)
@@ -97,7 +99,8 @@
         scaled = jnp.concatenate([back * cos_h, -(back * sin_h)], axis=1)
         out = -jnp.dot(scaled, bwd, precision=MID)
         out = jnp.where(live, out, 0.0)
-        return lax.all_to_all(out.reshape(n_col, 1, width), "col", 0, 0, tiled=True).reshape(n_col, width)
+        back = lax.all_to_all(out.reshape(n_col, width // 128, 128), "col", 0, 0, tiled=True)
+        return back.reshape(n_col, width)
 
     return local
 

time: 66.8 us -> 67.8 us (1.015)
  matrix products: 22.7 us -> 24.6 us
  other arithmetic: 7.81 us -> 7.11 us
    dot_general x1, matrix products: 4.04 us -> 6.15 us  [local(): grids = jnp.dot(w, cols.reshape(count, n * extent), precision=MID)]
    unnamed x9 -> x11, local copies, waits for them, and re-layouts: 1.97 us -> 0.67 us
    concatenate x1, other arithmetic: 0.82 us -> 0.11 us  [local(): jnp.concatenate([orbitals[:, None, :], jnp.broadcast_to(picked[None], (n_...]
where the time goes in v3:
time: 67.8 us; the launch traced here: 67.3 us
  matrix products  24.6 us (36%)
  starting transfers between devices  10.5 us (15%)
  blocking collectives  10.1 us (15%)
  local copies, waits for them, and re-layouts  7.5 us (11%)
  other arithmetic  7.11 us (10%)
  waiting for transfers between devices  6.48 us (10%)
  between operations  0.98 us (1%)
    all_to_all x1, blocking collectives, local(): lax.all_to_all(out.reshape(n_col, width // 128, 128), 'col', 0, 0, tiled=...  10.1 us
    all_to_all x1, starting transfers between devices, local(): lax.all_to_all(send.reshape(n_grp_bands, -1, 128), 'col', 0, 0, tiled=True)  6.29 us
    dot_general x1, matrix products, local(): grids = jnp.dot(w, cols.reshape(count, n * extent), precision=MID)  6.15 us
    dot_general x2, matrix products, cas_three(): return jnp.einsum('absc,ka->kbsc', field, table, precision=MID)  6.14 us
    dot_general x2, matrix products, cas_three(): field = jnp.einsum('absc,ck->absk', field, table, precision=MID)  4.44 us
    all_to_all x1, starting transfers between devices, local(): lax.all_to_all(spread, 'grp', 0, 0, tiled=True)  4.24 us
    dot_general x2, matrix products, cas_three(): field = jnp.einsum('absc,kb->aksc', field, table, precision=MID)  3.76 us
    all_to_all x1, waiting for transfers between devices, local(): lax.all_to_all(send.reshape(n_grp_bands, -1, 128), 'col', 0, 0, tiled=True)  3.56 us
  transfers between devices with their start and end apart: 2, of which 2 were waited for; matrix products, arithmetic and copies ran while one was open for 9% of the time, Pallas kernels for 0%

profile of v3, /device:TPU:0, one launch (start us, length us, event | category | flops | bytes accessed | tf_op | source)
XLA Modules:
  0.0 67.3 jit_solution(8186384254143187488)
XLA Ops:
  0.0 0.0 copy-start.1
  0.0 0.0 copy-start
  0.0 0.7 %and_select_fusion.1 = s32[3]{0:T(128)S(1)} fusion(s32[3]{0:T(128)} %param.8), kind=kLoop, calls=%fused_computation.94 | loop fusion | flops 33 | bytes 24 | tf_op jit(solution)/shard_map/jit(remainder)/select_n | solution.py:68
  0.7 0.7 fusion.59
  1.4 1.0 %convolution_select_fusion = f32[3,1792]{1,0:T(4,128)S(1)} fusion(f32[8,1792]{1,0:T(8,128)} %param.5, pred[3]{0:T(512)(128)(4,1)S(1)} %fusion.59, s32[3]{0:T(128)S(1)} %and_select_fusion.1), kind=kOutput, calls=%fused_computation.15 | convolution fusion | flops 521496 | bytes 78863 | tf_op jit(solution)/shard_map/dot_general | solution.py:69
  2.4 0.6 broadcast_in_dim.41
  3.1 4.2 %all-to-all-start = ((f32[4,42,128]{2,1,0:T(8,128)}), f32[4,42,128]{2,1,0:T(8,128)S(1)}, u32[]{:S(2)}, u32[]{:S(2)}) async-start(f32[4,42,128]{2,1,0:T(8,128)} %broadcast_in_dim.41), calls=%async_computation | async-start | bytes 196608 | tf_op jit(solution)/shard_map/all_to_all | solution.py:73
  7.3 0.9 %copy.47 = f32[8,1,1792]{2,1,0:T(1,128)S(1)} copy(f32[8,1,1792]{2,0,1:T(8,128)} %bitcast.87) | data formatting | bytes 114688 | tf_op jit(solution)/shard_map/broadcast_in_dim | solution.py:75
  8.2 0.1 broadcast_add_fusion
  8.3 0.4 fusion.17
  8.7 2.9 %all-to-all-done = f32[4,42,128]{2,1,0:T(8,128)S(1)} async-done(((f32[4,42,128]{2,1,0:T(8,128)}), f32[4,42,128]{2,1,0:T(8,128)S(1)}, u32[]{:S(2)}, u32[]{:S(2)}) %all-to-all-start) | async-done | bytes 86048 | tf_op jit(solution)/shard_map/all_to_all | solution.py:73
  11.7 0.1 pad_maximum_fusion
  11.8 1.2 %slice.21 = s32[1]{0:T(128)} slice(s32[448]{0:T(512)} %param.7), slice={[0:1]} | slice | bytes 8 | tf_op jit(solution)/shard_map/slice | solution.py:79
  13.0 0.8 %lt.80 = s32[8,56]{1,0:T(8,128)S(1)} reshape(s32[448]{0:T(512)} %param.7) | data formatting | bytes 3584 | tf_op jit(solution)/shard_map/lt | solution.py:39
  14.4 0.1 multiply_add_fusion
  14.5 0.1 copy.54
  14.6 0.6 gather_fusion
  15.2 0.1 maximum_bitcast_fusion
  15.3 0.1 dot_general.54
  15.4 0.8 %reshape.213 = f32[8,56,128]{2,1,0:T(8,128)} reshape(f32[8,4,1792]{2,1,0:T(4,128)S(1)} %pad_maximum_fusion) | data formatting | bytes 458752 | tf_op jit(solution)/shard_map/reshape | solution.py:77
  16.2 6.3 %all-to-all-start.1 = ((f32[8,56,128]{2,1,0:T(8,128)}), f32[8,56,128]{2,1,0:T(8,128)S(1)}, u32[]{:S(2)}, u32[]{:S(2)}) async-start(f32[8,56,128]{2,1,0:T(8,128)} %reshape.213), calls=%async_computation.1 | async-start | bytes 458752 | tf_op jit(solution)/shard_map/all_to_all | solution.py:77
  22.5 0.0 copy-done.1
  22.5 0.0 copy-done
  22.5 0.3 fusion.32
  22.8 0.3 fusion.33
  23.1 2.7 %broadcast_multiply_fusion = f32[48,48,448]{2,1,0:T(8,128)} fusion(f32[48,448]{1,0:T(8,128)S(1)} %fusion.33, f32[48,448]{1,0:T(8,128)S(1)} %fusion.32), kind=kLoop, calls=%fused_computation.14 | loop fusion | flops 1032192 | bytes 4300800 | tf_op jit(solution)/shard_map/mul | solution.py:49
  25.9 0.6 gather_fusion.1
  26.4 0.1 copy.55
  26.5 0.1 iota_compare_fusion
  26.6 0.4 fusion.30
  27.1 3.6 %all-to-all-done.1 = f32[8,56,128]{2,1,0:T(8,128)S(1)} async-done(((f32[8,56,128]{2,1,0:T(8,128)}), f32[8,56,128]{2,1,0:T(8,128)S(1)}, u32[]{:S(2)}, u32[]{:S(2)}) %all-to-all-start.1) | async-done | bytes 229408 | tf_op jit(solution)/shard_map/all_to_all | solution.py:77
  30.6 0.2 reshape_reshape.3
  30.9 0.1 select_bitcast_fusion
  30.9 0.3 copy.48
  31.3 0.2 reshape.233
  31.5 0.5 fusion.20
  32.0 0.1 fusion.93
  32.0 0.1 fusion.19
  32.2 6.2 %fusion.94 = f32[48,48,4,48]{3,1,2,0:T(8,128)S(1)} fusion(f32[48,48,448,1]{2,1,3,0:T(8,128)} %bitcast.78, f32[4,48,448,1]{2,1,0,3:T(8,128)S(1)} %bitcast.84), kind=kOutput, calls=%fused_computation.139 | convolution fusion | flops 1189085184 | bytes 6242304 | tf_op jit(solution)/shard_map/dot_general | solution.py:91
  38.3 0.1 slice_bitcast_fusion
  38.4 1.7 %fusion.8 = f32[48,48,3,48]{3,1,2,0:T(8,128)S(1)} fusion(f32[48,48,4,48]{3,1,2,0:T(8,128)S(1)} %fusion.94, f32[48,48,48]{2,1,0:T(8,128)S(1)} %slice_bitcast_fusion, f32[]{:T(128)} %bitcast.1), kind=kOutput, calls=%fused_computation.11 | convolution fusion | flops 95910912 | bytes 6045700 | tf_op jit(solution)/shard_map/absc,ck->absk/dot_general | solution.py:53
  40.1 1.9 %convolution_bitcast_fusion.1 = f32[48,48,3,48]{3,1,2,0:T(8,128)S(1)} fusion(f32[48,48,3,48]{3,1,2,0:T(8,128)S(1)} %fusion.8, f32[]{:T(128)} %bitcast.1), kind=kOutput, calls=%fused_computation.17 | convolution fusion | flops 95579136 | bytes 2654212 | tf_op jit(solution)/shard_map/absc,kb->aksc/dot_general | solution.py:54
  42.0 3.0 %fusion.11 = f32[48,48,3,48]{3,0,2,1:T(8,128)S(1)} fusion(f32[48,48,3,48]{3,1,2,0:T(8,128)S(1)} %convolution_bitcast_fusion.1, f32[48,48,48]{2,0,1:T(8,128)S(1)} %fusion.17, f32[]{:T(128)} %bitcast.1), kind=kOutput, calls=%fused_computation.18 | convolution fusion | flops 95910912 | bytes 3096580 | tf_op jit(solution)/shard_map/absc,ka->kbsc/dot_general | solution.py:55
  45.0 2.8 %fusion.4 = f32[48,48,3,48]{3,1,2,0:T(8,128)S(1)} fusion(f32[48,48,3,48]{3,0,2,1:T(8,128)S(1)} %fusion.11, f32[]{:T(128)} %bitcast.1), kind=kOutput, calls=%fused_computation.7 | convolution fusion | flops 95579136 | bytes 2654212 | tf_op jit(solution)/shard_map/absc,ck->absk/dot_general | solution.py:53
  47.7 1.9 %convolution_bitcast_fusion = f32[48,48,3,48]{3,1,2,0:T(8,128)S(1)} fusion(f32[48,48,3,48]{3,1,2,0:T(8,128)S(1)} %fusion.4, f32[]{:T(128)} %bitcast.1), kind=kOutput, calls=%fused_computation.16 | convolution fusion | flops 95579136 | bytes 2654212 | tf_op jit(solution)/shard_map/absc,kb->aksc/dot_general | solution.py:54
  49.6 0.0 copy-start.2
  49.6 0.0 slice-start
  49.7 3.2 %fusion.2 = f32[48,48,3,48]{3,0,2,1:T(8,128)S(1)} fusion(f32[48,48,3,48]{3,1,2,0:T(8,128)S(1)} %convolution_bitcast_fusion, f32[]{:T(128)} %bitcast.1), kind=kOutput, calls=%fused_computation.5 | convolution fusion | flops 95579136 | bytes 2654212 | tf_op jit(solution)/shard_map/absc,ka->kbsc/dot_general | solution.py:55
  52.8 0.0 copy-done.2
  52.8 0.0 slice-start.1
  52.8 1.5 %fusion.1 = f32[48,48,48]{2,1,0:T(8,128)S(1)} fusion(f32[48,48,3,48]{3,0,2,1:T(8,128)S(1)} %fusion.2, f32[48,48,4,48]{3,1,2,0:T(8,128)S(1)} %fusion.94, f32[3]{0:T(128)S(1)} %copy-done.2), kind=kLoop, calls=%fused_computation.4 | loop fusion | flops 884736 | bytes 3096588 | tf_op jit(solution)/shard_map/reduce_sum | solution.py:97
  54.3 0.0 slice-done
  54.3 0.0 slice-done.1
  54.3 1.7 %fusion.36 = (f32[448,48]{0,1:T(8,128)S(1)}, f32[448,48]{0,1:T(8,128)S(1)}) fusion(s32[448]{0:T(512)S(1)} %get-tuple-element.19, f32[2304,448]{1,0:T(8,128)S(1)} %bitcast.81, f32[2304,48]{1,0:T(8,128)S(1)} %bitcast.82), kind=kOutput, calls=%fused_computation.58 | convolution fusion | flops 297529344 | bytes 4744960 | tf_op jit(solution)/shard_map/dot_general | solution.py:98
  56.1 0.2 fusion.18
  56.3 0.1 copy.56
  56.4 0.1 reshape.215
  56.5 10.1 %all_to_all.15 = f32[8,14,128]{2,1,0:T(8,128)S(1)} all-to-all(f32[8,14,128]{2,1,0:T(8,128)S(1)} %reshape.215), channel_id=1, replica_groups=mesh['grp'=4,'col'=8] {'col'}, dimensions={0} | all-to-all | bytes 114688 | tf_op jit(solution)/shard_map/all_to_all | solution.py:102
  66.6 0.6 copy.80
  (10 shorter events, 0.1 us)
Async XLA Ops:
  0.0 22.5 %copy-start.1 = (s32[448]{0:T(512)S(1)}, s32[448]{0:T(512)}, u32[]{:S(2)}) copy-start(s32[448]{0:T(512)} %param.6) | copy-start | bytes 5380
  0.0 22.5 %copy-start = (s32[448]{0:T(512)S(1)}, s32[448]{0:T(512)}, u32[]{:S(2)}) copy-start(s32[448]{0:T(512)} %param.7) | copy-start | bytes 5380
  3.1 8.5 %all-to-all-start = ((f32[4,42,128]{2,1,0:T(8,128)}), f32[4,42,128]{2,1,0:T(8,128)S(1)}, u32[]{:S(2)}, u32[]{:S(2)}) async-start(f32[4,42,128]{2,1,0:T(8,128)} %broadcast_in_dim.41), calls=%async_computation | async-start | bytes 196608 | tf_op jit(solution)/shard_map/all_to_all | solution.py:73
  16.2 14.4 %all-to-all-start.1 = ((f32[8,56,128]{2,1,0:T(8,128)}), f32[8,56,128]{2,1,0:T(8,128)S(1)}, u32[]{:S(2)}, u32[]{:S(2)}) async-start(f32[8,56,128]{2,1,0:T(8,128)} %reshape.213), calls=%async_computation.1 | async-start | bytes 458752 | tf_op jit(solution)/shard_map/all_to_all | solution.py:77
  49.6 3.2 %copy-start.2 = (f32[3]{0:T(128)S(1)}, f32[3]{0:T(128)}, u32[]{:S(2)}) copy-start(f32[3]{0:T(128)} %param.9) | copy-start | bytes 40
  49.6 4.7 %slice-start = ((s8[4718592]{0:T(1024)(128)(4,1)}), s8[4194304]{0:T(1024)(128)(4,1)S(1)}, s32[]{:S(2)}) async-start(s8[4718592]{0:T(1024)(128)(4,1)} %bitcast.79), calls=%async_computation.3 | async-start | bytes 8388608
  52.8 1.5 %slice-start.1 = ((s8[4718592]{0:T(1024)(128)(4,1)}), s8[524288]{0:T(1024)(128)(4,1)S(1)}, s32[]{:S(2)}) async-start(s8[4718592]{0:T(1024)(128)(4,1)} %bitcast.79), calls=%async_computation.4 | async-start | bytes 1048576

commit v4 on v2

--- a/solution.py
+++ b/solution.py
@@ -49,10 +49,26 @@
     return (ta[:, None, :] * tb[None, :, :]).reshape(extent * extent, -1)
 
 
+def halves(value):
+    high = lax.reduce_precision(value, exponent_bits=8, mantissa_bits=7)
+    return high.astype(jnp.bfloat16), (value - high).astype(jnp.bfloat16)
+
+
+def stacked(table):
+    high, low = halves(table)
+    return jnp.concatenate([high, low, high], axis=0)
+
+
+def split_stack(field, axis):
+    high, low = halves(field)
+    return jnp.concatenate([high, high, low], axis=axis)
+
+
 def cas_three(field, table):
-    field = jnp.einsum("absc,ck->absk", field, table, precision=MID)
-    field = jnp.einsum("absc,kb->aksc", field, table, precision=MID)
-    return jnp.einsum("absc,ka->kbsc", field, table, precision=MID)
+    parts = stacked(table)
+    field = jnp.einsum("absc,ck->absk", split_stack(field, 3), parts, preferred_element_type=jnp.float32)
+    field = jnp.einsum("absc,kb->aksc", split_stack(field, 1), parts.T, preferred_element_type=jnp.float32)
+    return jnp.einsum("absc,ka->kbsc", split_stack(field, 0), parts.T, preferred_element_type=jnp.float32)
 
 
 def make_local(n_grp_bands, n_grp, n_col):

time: 66.8 us -> 75.9 us (1.14)
  other arithmetic: 7.81 us -> 14 us
  matrix products: 22.7 us -> 25.1 us
    concatenate x0 -> x3, other arithmetic: none -> 5.38 us  [split_stack(): return jnp.concatenate([high, high, low], axis=axis)]
    dot_general x6, matrix products: 14.3 us -> 16.6 us  [the longest x2 6.23 us: cas_three(): jnp.einsum('absc,ck->absk', split_stack(field, 3), parts, preferred_eleme...]
    convert_element_type x0 -> x2, other arithmetic: none -> 0.78 us  [halves(): return (high.astype(jnp.bfloat16), (value - high).astype(jnp.bfloat16))]
  transfers between devices with their start and end apart: 2 -> 2, of which waited for: 2 -> 2; matrix products, arithmetic and copies ran while one was open for 9% -> 7% of each run, Pallas kernels for 0% -> 0%
where the time goes in v4:
time: 75.9 us; the launch traced here: 75.3 us
  matrix products  25.1 us (33%)
  other arithmetic  14 us (18%)
  starting transfers between devices  10.5 us (14%)
  blocking collectives  10 us (13%)
  local copies, waits for them, and re-layouts  7.61 us (10%)
  waiting for transfers between devices  7.17 us (9%)
  between operations  0.95 us (1%)
    all_to_all x1, blocking collectives, local(): lax.all_to_all(out.reshape(n_col, 1, width), 'col', 0, 0, tiled=True)  10 us
    all_to_all x1, starting transfers between devices, local(): got = lax.all_to_all(send, 'col', 0, 0, tiled=True)  6.31 us
    dot_general x2, matrix products, cas_three(): jnp.einsum('absc,ck->absk', split_stack(field, 3), parts, preferred_eleme...  6.23 us
    dot_general x2, matrix products, cas_three(): jnp.einsum('absc,kb->aksc', split_stack(field, 1), parts.T, preferred_ele...  6.19 us
    concatenate x3, other arithmetic, split_stack(): return jnp.concatenate([high, high, low], axis=axis)  5.38 us
    all_to_all x1, starting transfers between devices, local(): picked = jnp.sum(lax.all_to_all(spread, 'grp', 0, 0, tiled=True), axis=0)  4.24 us
    dot_general x2, matrix products, cas_three(): jnp.einsum('absc,ka->kbsc', split_stack(field, 0), parts.T, preferred_ele...  4.17 us
    all_to_all x1, waiting for transfers between devices, local(): got = lax.all_to_all(send, 'col', 0, 0, tiled=True)  4.07 us
  transfers between devices with their start and end apart: 2, of which 2 were waited for; matrix products, arithmetic and copies ran while one was open for 7% of the time, Pallas kernels for 0%

profile of v4, /device:TPU:0, one launch (start us, length us, event | category | flops | bytes accessed | tf_op | source)
XLA Modules:
  0.0 75.3 jit_solution(13958098253044932832)
XLA Ops:
  0.0 0.0 copy-start.2
  0.0 0.0 copy-start.1
  0.0 0.7 and_select_fusion.1
  0.7 0.7 fusion.70
  1.4 1.0 %convolution_select_fusion = f32[3,1792]{1,0:T(4,128)S(1)} fusion(f32[8,1792]{1,0:T(8,128)} %param.5, pred[3]{0:T(512)(128)(4,1)S(1)} %fusion.70, s32[3]{0:T(128)S(1)} %and_select_fusion.1), kind=kOutput, calls=%fused_computation.52 | convolution fusion | flops 521496 | bytes 78863 | tf_op jit(solution)/shard_map/dot_general | solution.py:85
  2.4 0.7 broadcast_in_dim.36
  3.1 4.2 %all-to-all-start = ((f32[4,3,1792]{2,1,0:T(4,128)}), f32[4,3,1792]{2,1,0:T(4,128)S(1)}, u32[]{:S(2)}, u32[]{:S(2)}) async-start(f32[4,3,1792]{2,1,0:T(4,128)} %broadcast_in_dim.36), calls=%async_computation | async-start | bytes 229376 | tf_op jit(solution)/shard_map/all_to_all | solution.py:88
  7.3 0.9 %broadcast_in_dim.33 = f32[8,1,1792]{2,1,0:T(1,128)S(1)} reshape(f32[8,1792]{1,0:T(8,128)} %param.5) | data formatting | bytes 114688 | tf_op jit(solution)/shard_map/broadcast_in_dim | solution.py:90
  8.2 0.1 broadcast_add_fusion
  8.3 0.4 fusion.34
  8.7 3.1 %all-to-all-done = f32[4,3,1792]{2,1,0:T(4,128)S(1)} async-done(((f32[4,3,1792]{2,1,0:T(4,128)}), f32[4,3,1792]{2,1,0:T(4,128)S(1)}, u32[]{:S(2)}, u32[]{:S(2)}) %all-to-all-start) | async-done | bytes 86048 | tf_op jit(solution)/shard_map/all_to_all | solution.py:88
  11.8 0.8 %pad_maximum_fusion.3 = f32[8,4,1792]{2,1,0:T(4,128)} fusion(f32[8,3,1792]{2,1,0:T(4,128)S(1)} %broadcast_in_dim.37, f32[8,1,1792]{2,1,0:T(1,128)S(1)} %broadcast_in_dim.33), kind=kLoop, calls=%fused_computation.65 | loop fusion | flops 57344 | bytes 458752 | tf_op jit(solution)/shard_map/concatenate | solution.py:89
  12.6 1.2 %slice.21 = s32[1]{0:T(128)} slice(s32[448]{0:T(512)} %param.7), slice={[0:1]} | slice | bytes 8 | tf_op jit(solution)/shard_map/slice | solution.py:93
  13.8 0.8 %lt.80 = s32[8,56]{1,0:T(8,128)S(1)} reshape(s32[448]{0:T(512)} %param.7) | data formatting | bytes 3584 | tf_op jit(solution)/shard_map/lt | solution.py:39
  15.2 0.1 multiply_add_fusion
  15.4 0.1 reduce-precision_convert_fusion.6
  15.5 0.1 copy.47
  15.6 0.6 gather_fusion.1
  16.2 0.6 gather_fusion
  16.7 0.1 copy.48
  16.8 0.1 maximum_bitcast_fusion.1
  16.9 0.1 dot_general.54
  17.0 6.3 %all-to-all-start.1 = ((f32[8,4,1792]{2,1,0:T(4,128)}), f32[8,4,1792]{2,1,0:T(4,128)S(1)}, u32[]{:S(2)}, u32[]{:S(2)}) async-start(f32[8,4,1792]{2,1,0:T(4,128)} %pad_maximum_fusion.3), calls=%async_computation.1 | async-start | bytes 458752 | tf_op jit(solution)/shard_map/all_to_all | solution.py:92
  23.3 0.0 copy-done.2
  23.3 0.0 copy-done.1
  23.3 0.4 fusion.47
  23.7 0.4 fusion.48
  24.1 2.7 %broadcast_multiply_fusion = f32[48,48,448]{2,1,0:T(8,128)} fusion(f32[48,448]{1,0:T(8,128)S(1)} %fusion.48, f32[48,448]{1,0:T(8,128)S(1)} %fusion.47), kind=kLoop, calls=%fused_computation.51 | loop fusion | flops 1032192 | bytes 4300800 | tf_op jit(solution)/shard_map/mul | solution.py:49
  26.8 0.1 iota_compare_fusion
  26.9 0.4 fusion.45
  27.3 4.1 %all-to-all-done.1 = f32[8,4,1792]{2,1,0:T(4,128)S(1)} async-done(((f32[8,4,1792]{2,1,0:T(4,128)}), f32[8,4,1792]{2,1,0:T(4,128)S(1)}, u32[]{:S(2)}, u32[]{:S(2)}) %all-to-all-start.1) | async-done | bytes 229408 | tf_op jit(solution)/shard_map/all_to_all | solution.py:92
  31.5 0.3 reshape.210
  31.8 0.0 copy-start
  31.8 0.1 broadcast_select_fusion
  31.8 0.7 fusion.52
  32.6 0.1 fusion.83
  32.6 0.1 fusion.36
  32.8 1.3 %copy-done = f32[48,48,448]{2,1,0:T(8,128)S(1)} copy-done((f32[48,48,448]{2,1,0:T(8,128)S(1)}, f32[48,48,448]{2,1,0:T(8,128)}, u32[]{:S(2)}) %copy-start) | copy-done | bytes 4128792
  34.1 4.0 %fusion.84 = f32[48,48,4,48]{3,1,2,0:T(8,128)S(1)} fusion(f32[48,48,448,1]{2,1,3,0:T(8,128)S(1)} %bitcast.82, f32[4,48,448,1]{2,1,0,3:T(8,128)S(1)} %bitcast.87), kind=kOutput, calls=%fused_computation.148 | convolution fusion | flops 1189085184 | bytes 6242304 | tf_op jit(solution)/shard_map/dot_general | solution.py:105
  38.1 0.1 slice_bitcast_fusion
  38.2 0.7 reduce-precision_convert_fusion.5
  38.9 3.8 %reduce-precision_convert_fusion.4 = (bf16[48,48,3,48]{1,3,2,0:T(8,128)(2,1)S(1)}, bf16[48,48,3,48]{1,3,2,0:T(8,128)(2,1)S(1)}) fusion(bf16[48,48]{0,1:T(8,128)(2,1)S(1)} %get-tuple-element.32, bf16[48,48]{0,1:T(8,128)(2,1)S(1)} %get-tuple-element.33, bf16[48,48,3,48]{3,1,2,0:T(8,128)(2,1)S(1)} %get-tuple-element.12, ...), kind=kOutput, calls=%fused_computation.17 | convolution fusion | flops 102892032 | bytes 2663424 | tf_op jit(solution)/shard_map/absc,ck->absk/dot_general | solution.py:69
  42.7 3.1 %reduce-precision_convert_fusion.3 = (bf16[48,48,3,48]{3,1,2,0:T(8,128)(2,1)S(1)}, bf16[48,48,3,48]{3,1,2,0:T(8,128)(2,1)S(1)}) fusion(bf16[48,48,3,48]{1,3,2,0:T(8,128)(2,1)S(1)} %get-tuple-element.22, bf16[48,48,3,48]{1,3,2,0:T(8,128)(2,1)S(1)} %get-tuple-element.21, bf16[48,48]{0,1:T(8,128)(2,1)S(1)} %get-tuple-element.32, ...), kind=kOutput, calls=%fused_computation.15 | convolution fusion | flops 102892032 | bytes 2663424 | tf_op jit(solution)/shard_map/absc,kb->aksc/dot_general | solution.py:70
  45.8 1.4 %pad_maximum_fusion = bf16[144,48,3,48]{3,1,2,0:T(8,128)(2,1)S(1)} fusion(bf16[48,48,3,48]{3,1,2,0:T(8,128)(2,1)S(1)} %get-tuple-element.20, bf16[48,48,3,48]{3,1,2,0:T(8,128)(2,1)S(1)} %get-tuple-element.19), kind=kLoop, calls=%fused_computation.2 | loop fusion | flops 1990656 | bytes 3317760 | tf_op jit(solution)/shard_map/concatenate | solution.py:64
  47.3 2.6 %reduce-precision_convert_fusion.2 = (bf16[48,48,3,48]{3,0,2,1:T(8,128)(2,1)S(1)}, bf16[48,48,3,48]{3,0,2,1:T(8,128)(2,1)S(1)}) fusion(f32[48,48,48]{2,0,1:T(8,128)S(1)} %fusion.34, bf16[144,48,3,48]{3,1,2,0:T(8,128)(2,1)S(1)} %pad_maximum_fusion, bf16[48,48]{0,1:T(8,128)(2,1)S(1)} %get-tuple-element.32, bf16[48,48]{0,1:T(8,128)(2,1)S(1)} %get-tuple-element.33), kind=kOutput, calls=%fused_computation.13 | convolution fusion | flops 97251840 | bytes 3769344 | tf_op jit(solution)/shard_map/absc,ka->kbsc/dot_general | solution.py:71
  49.8 2.6 %pad_maximum_fusion.2 = bf16[48,48,3,144]{3,0,2,1:T(8,128)(2,1)S(1)} fusion(bf16[48,48,3,48]{3,0,2,1:T(8,128)(2,1)S(1)} %get-tuple-element.14, bf16[48,48,3,48]{3,0,2,1:T(8,128)(2,1)S(1)} %get-tuple-element.13), kind=kLoop, calls=%fused_computation.38 | loop fusion | flops 5971968 | bytes 3317760 | tf_op jit(solution)/shard_map/concatenate | solution.py:64
  52.4 2.4 %reduce-precision_convert_fusion.1 = (bf16[48,48,3,48]{1,3,2,0:T(8,128)(2,1)S(1)}, bf16[48,48,3,48]{1,3,2,0:T(8,128)(2,1)S(1)}) fusion(bf16[48,48]{0,1:T(8,128)(2,1)S(1)} %get-tuple-element.32, bf16[48,48]{0,1:T(8,128)(2,1)S(1)} %get-tuple-element.33, bf16[48,48,3,144]{3,0,2,1:T(8,128)(2,1)S(1)} %pad_maximum_fusion.2), kind=kOutput, calls=%fused_computation.11 | convolution fusion | flops 96920064 | bytes 3326976 | tf_op jit(solution)/shard_map/absc,ck->absk/dot_general | solution.py:69
  54.8 3.1 %reduce-precision_convert_fusion = (bf16[48,48,3,48]{3,1,2,0:T(8,128)(2,1)S(1)}, bf16[48,48,3,48]{3,1,2,0:T(8,128)(2,1)S(1)}) fusion(bf16[48,48,3,48]{1,3,2,0:T(8,128)(2,1)S(1)} %get-tuple-element.18, bf16[48,48,3,48]{1,3,2,0:T(8,128)(2,1)S(1)} %get-tuple-element.17, bf16[48,48]{0,1:T(8,128)(2,1)S(1)} %get-tuple-element.32, ...), kind=kOutput, calls=%fused_computation.9 | convolution fusion | flops 102892032 | bytes 2663424 | tf_op jit(solution)/shard_map/absc,kb->aksc/dot_general | solution.py:70
  57.9 1.4 %pad_maximum_fusion.1 = bf16[144,48,3,48]{3,1,2,0:T(8,128)(2,1)S(1)} fusion(bf16[48,48,3,48]{3,1,2,0:T(8,128)(2,1)S(1)} %get-tuple-element.16, bf16[48,48,3,48]{3,1,2,0:T(8,128)(2,1)S(1)} %get-tuple-element.15), kind=kLoop, calls=%fused_computation.3 | loop fusion | flops 1990656 | bytes 3317760 | tf_op jit(solution)/shard_map/concatenate | solution.py:64
  59.3 0.0 copy-start.3
  59.3 1.6 %fusion = f32[48,48,3,48]{3,0,2,1:T(8,128)S(1)} fusion(bf16[144,48,3,48]{3,1,2,0:T(8,128)(2,1)S(1)} %pad_maximum_fusion.1, bf16[48,48]{0,1:T(8,128)(2,1)S(1)} %get-tuple-element.32, bf16[48,48]{0,1:T(8,128)(2,1)S(1)} %get-tuple-element.33), kind=kOutput, calls=%fused_computation.4 | convolution fusion | flops 95592960 | bytes 3326976 | tf_op jit(solution)/shard_map/absc,ka->kbsc/dot_general | solution.py:71
  61.0 0.0 copy-done.3
  61.0 1.5 %fusion.29 = f32[48,48,48]{2,1,0:T(8,128)S(1)} fusion(f32[48,48,3,48]{3,0,2,1:T(8,128)S(1)} %fusion, f32[48,48,4,48]{3,1,2,0:T(8,128)S(1)} %fusion.84, f32[3]{0:T(128)S(1)} %copy-done.3), kind=kLoop, calls=%fused_computation.47 | loop fusion | flops 884736 | bytes 3096588 | tf_op jit(solution)/shard_map/reduce_sum | solution.py:111
  62.4 1.7 %fusion.51 = (f32[448,48]{0,1:T(8,128)S(1)}, f32[448,48]{0,1:T(8,128)S(1)}) fusion(s32[448]{0:T(512)S(1)} %get-tuple-element.31, f32[2304,448]{1,0:T(8,128)S(1)} %bitcast.83, f32[2304,48]{1,0:T(8,128)S(1)} %bitcast.84), kind=kOutput, calls=%fused_computation.89 | convolution fusion | flops 297529344 | bytes 4744960 | tf_op jit(solution)/shard_map/dot_general | solution.py:112
  64.2 0.2 fusion.35
  64.4 0.1 copy.55
  64.5 0.2 reshape.235
  64.7 10.0 %all_to_all.15 = f32[8,1,1792]{2,1,0:T(1,128)S(1)} all-to-all(f32[8,1,1792]{2,1,0:T(1,128)S(1)} %reshape.235), channel_id=1, replica_groups=mesh['grp'=4,'col'=8] {'col'}, dimensions={0} | all-to-all | bytes 114688 | tf_op jit(solution)/shard_map/all_to_all | solution.py:116
  74.7 0.6 copy.84
  (8 shorter events, 0.1 us)
Async XLA Ops:
  0.0 23.3 %copy-start.2 = (s32[448]{0:T(512)S(1)}, s32[448]{0:T(512)}, u32[]{:S(2)}) copy-start(s32[448]{0:T(512)} %param.6) | copy-start | bytes 5380
  0.0 23.3 %copy-start.1 = (s32[448]{0:T(512)S(1)}, s32[448]{0:T(512)}, u32[]{:S(2)}) copy-start(s32[448]{0:T(512)} %param.7) | copy-start | bytes 5380
  3.1 8.7 %all-to-all-start = ((f32[4,3,1792]{2,1,0:T(4,128)}), f32[4,3,1792]{2,1,0:T(4,128)S(1)}, u32[]{:S(2)}, u32[]{:S(2)}) async-start(f32[4,3,1792]{2,1,0:T(4,128)} %broadcast_in_dim.36), calls=%async_computation | async-start | bytes 229376 | tf_op jit(solution)/shard_map/all_to_all | solution.py:88
  17.0 14.4 %all-to-all-start.1 = ((f32[8,4,1792]{2,1,0:T(4,128)}), f32[8,4,1792]{2,1,0:T(4,128)S(1)}, u32[]{:S(2)}, u32[]{:S(2)}) async-start(f32[8,4,1792]{2,1,0:T(4,128)} %pad_maximum_fusion.3), calls=%async_computation.1 | async-start | bytes 458752 | tf_op jit(solution)/shard_map/all_to_all | solution.py:92
  31.8 2.3 %copy-start = (f32[48,48,448]{2,1,0:T(8,128)S(1)}, f32[48,48,448]{2,1,0:T(8,128)}, u32[]{:S(2)}) copy-start(f32[48,48,448]{2,1,0:T(8,128)} %broadcast_multiply_fusion) | copy-start | bytes 12386308
  59.3 1.6 %copy-start.3 = (f32[3]{0:T(128)S(1)}, f32[3]{0:T(128)}, u32[]{:S(2)}) copy-start(f32[3]{0:T(128)} %param.9) | copy-start | bytes 40

commit v5 on v2

--- a/solution.py
+++ b/solution.py
@@ -68,12 +68,14 @@
         rows = (sources % n_grp_bands)[:, None] == jnp.arange(n_grp_bands, dtype=jnp.int32)[None, :]
         picked = jnp.dot(rows.astype(jnp.float32), orbitals, precision=HI)
         picked = jnp.where((owner == g)[:, None], picked, 0.0)
-        spread = jnp.broadcast_to(picked[None], (n_grp, n_src, width))
-        picked = jnp.sum(lax.all_to_all(spread, "grp", 0, 0, tiled=True), axis=0)
         send = jnp.concatenate(
             [orbitals[:, None, :], jnp.broadcast_to(picked[None], (n_grp_bands, n_src, width))], axis=1)
+        send = jnp.broadcast_to(send[None], (n_grp,) + send.shape).reshape((n_grp * n_col,) + send.shape[1:])
         send, column_cell, column_length = lax.optimization_barrier((send, column_cell, column_length))
-        got = lax.all_to_all(send, "col", 0, 0, tiled=True)
+        got = lax.all_to_all(send, ("grp", "col"), 0, 0, tiled=True)
+        got = got.reshape(n_grp, n_col, 1 + n_src, width)
+        own_blocks = lax.dynamic_index_in_dim(got[:, :, 0], g, 0, keepdims=False)
+        got = jnp.concatenate([own_blocks[:, None, :], jnp.sum(got[:, :, 1:], axis=0)], axis=1)
         table = cas_matrix(extent) + 0.0 * column_length[0]
         kernel = kernel_grid(extent)
         cos_h, sin_h, live = shift_tables(column_length, depth, extent)

time: 66.8 us -> 72.3 us (1.082)
  waiting for transfers between devices: 6.62 us -> 17.5 us
  starting transfers between devices: 10.5 us -> 7.3 us
    all_to_all x2 -> x1, waiting for transfers between devices: 6.62 us -> 17.5 us  [local(): got = lax.all_to_all(send, ('grp', 'col'), 0, 0, tiled=True)]
    all_to_all x2 -> x1, starting transfers between devices: 10.5 us -> 7.3 us  [local(): got = lax.all_to_all(send, ('grp', 'col'), 0, 0, tiled=True)]
  transfers between devices with their start and end apart: 2 -> 1, of which waited for: 2 -> 1; matrix products, arithmetic and copies ran while one was open for 9% -> 9% of each run, Pallas kernels for 0% -> 0%
where the time goes in v5:
time: 72.3 us; the launch traced here: 71.9 us
  matrix products  22.7 us (31%)
  waiting for transfers between devices  17.5 us (24%)
  blocking collectives  9.44 us (13%)
  starting transfers between devices  7.3 us (10%)
  other arithmetic  7.13 us (10%)
  local copies, waits for them, and re-layouts  6.91 us (10%)
  between operations  0.97 us (1%)
    all_to_all x1, waiting for transfers between devices, local(): got = lax.all_to_all(send, ('grp', 'col'), 0, 0, tiled=True)  17.5 us
    all_to_all x1, blocking collectives, local(): lax.all_to_all(out.reshape(n_col, 1, width), 'col', 0, 0, tiled=True)  9.44 us
    all_to_all x1, starting transfers between devices, local(): got = lax.all_to_all(send, ('grp', 'col'), 0, 0, tiled=True)  7.3 us
    dot_general x2, matrix products, cas_three(): return jnp.einsum('absc,ka->kbsc', field, table, precision=MID)  6.12 us
    dot_general x2, matrix products, cas_three(): field = jnp.einsum('absc,ck->absk', field, table, precision=MID)  4.45 us
    dot_general x1, matrix products, local(): grids = jnp.dot(w, cols.reshape(count, n * extent), precision=MID)  4.04 us
    dot_general x2, matrix products, cas_three(): field = jnp.einsum('absc,kb->aksc', field, table, precision=MID)  3.76 us
    mul x1, other arithmetic, plane_matrix(): return (ta[:, None, :] * tb[None, :, :]).reshape(extent * extent, -1)  2.74 us
  transfers between devices with their start and end apart: 1, of which 1 were waited for; matrix products, arithmetic and copies ran while one was open for 9% of the time, Pallas kernels for 0%

profile of v5, /device:TPU:0, one launch (start us, length us, event | category | flops | bytes accessed | tf_op | source)
XLA Modules:
  0.0 71.9 jit_solution(13602603084215440126)
XLA Ops:
  0.0 0.0 copy-start.2
  0.0 0.0 copy-start.1
  0.0 0.7 and_select_fusion.1
  0.7 0.7 fusion.58
  1.4 0.9 %copy.26 = f32[8,1,1792]{2,1,0:T(1,128)S(1)} copy(f32[8,1,1792]{2,0,1:T(8,128)} %bitcast.95) | data formatting | bytes 114688 | tf_op jit(solution)/shard_map/broadcast_in_dim | solution.py:72
  2.2 1.0 %convolution_select_fusion = f32[3,1792]{1,0:T(4,128)S(1)} fusion(f32[8,1792]{1,0:T(8,128)} %param.5, pred[3]{0:T(512)(128)(4,1)S(1)} %fusion.58, s32[3]{0:T(128)S(1)} %and_select_fusion.1), kind=kOutput, calls=%fused_computation.15 | convolution fusion | flops 521496 | bytes 78863 | tf_op jit(solution)/shard_map/dot_general | solution.py:69
  3.3 0.1 pad_maximum_fusion
  3.4 1.1 %broadcast_in_dim.37 = f32[4,8,4,1792]{3,2,1,0:T(4,128)} broadcast(f32[8,4,1792]{2,1,0:T(4,128)S(1)} %pad_maximum_fusion), dimensions={1,2,3} | broadcast | bytes 1146880 | tf_op jit(solution)/shard_map/broadcast_in_dim | solution.py:73
  4.5 7.3 %all-to-all-start = ((f32[32,4,1792]{2,1,0:T(4,128)}), f32[32,4,1792]{2,1,0:T(4,128)S(1)}, u32[]{:S(2)}, u32[]{:S(2)}) async-start(f32[32,4,1792]{2,1,0:T(4,128)} %bitcast.1), calls=%async_computation | async-start | bytes 1835008 | tf_op jit(solution)/shard_map/all_to_all | solution.py:75
  11.9 0.0 copy-done.1
  11.9 0.5 slice.27
  12.4 0.1 lt.84
  13.1 0.1 multiply_add_fusion
  13.3 0.1 copy.34
  13.3 0.6 gather_fusion
  13.9 0.1 maximum_bitcast_fusion
  14.0 0.1 dot_general.54
  14.1 0.0 copy-done.2
  14.1 0.3 fusion.30
  14.4 0.3 fusion.31
  14.7 2.7 %broadcast_multiply_fusion = f32[48,48,448]{2,1,0:T(8,128)} fusion(f32[48,448]{1,0:T(8,128)S(1)} %fusion.31, f32[48,448]{1,0:T(8,128)S(1)} %fusion.30), kind=kLoop, calls=%fused_computation.14 | loop fusion | flops 1032192 | bytes 4300800 | tf_op jit(solution)/shard_map/mul | solution.py:49
  17.5 0.6 gather_fusion.1
  18.0 0.1 copy.35
  18.1 0.1 broadcast_add_fusion
  18.2 0.1 iota_compare_fusion
  18.3 0.4 fusion.28
  18.8 0.4 fusion.17
  19.1 17.5 %all-to-all-done = f32[32,4,1792]{2,1,0:T(4,128)S(1)} async-done(((f32[32,4,1792]{2,1,0:T(4,128)}), f32[32,4,1792]{2,1,0:T(4,128)S(1)}, u32[]{:S(2)}, u32[]{:S(2)}) %all-to-all-start) | async-done | bytes 917536 | tf_op jit(solution)/shard_map/all_to_all | solution.py:75
  36.6 0.2 copy.63
  36.9 0.1 concatenate.21
  37.0 0.2 concatenate.22
  37.2 0.0 copy-start
  37.3 0.1 maximum_select_fusion
  37.4 0.7 %fusion.35 = f32[448,4,2,48]{0,3,2,1:T(8,128)S(1)} fusion(f32[448,4,32,1]{2,0,3,1:T(8,128)S(1)} %bitcast.91, f32[2,48,32]{1,0,2:T(2,128)S(1)} %dot_general.54), kind=kOutput, calls=%fused_computation.59 | convolution fusion | flops 33030144 | bytes 929792 | tf_op jit(solution)/shard_map/dot_general | solution.py:89
  38.1 0.1 fusion.92
  38.2 0.1 fusion.19
  38.3 1.3 %copy-done = f32[48,48,448]{2,1,0:T(8,128)S(1)} copy-done((f32[48,48,448]{2,1,0:T(8,128)S(1)}, f32[48,48,448]{2,1,0:T(8,128)}, u32[]{:S(2)}) %copy-start) | copy-done | bytes 4128792
  39.6 4.0 %fusion.93 = f32[48,48,4,48]{3,1,2,0:T(8,128)S(1)} fusion(f32[48,48,448,1]{2,1,3,0:T(8,128)S(1)} %bitcast.86, f32[4,48,448,1]{2,1,0,3:T(8,128)S(1)} %bitcast.93), kind=kOutput, calls=%fused_computation.141 | convolution fusion | flops 1189085184 | bytes 6242304 | tf_op jit(solution)/shard_map/dot_general | solution.py:91
  43.6 0.1 slice_bitcast_fusion
  43.7 1.7 %fusion.8 = f32[48,48,3,48]{3,1,2,0:T(8,128)S(1)} fusion(f32[48,48,4,48]{3,1,2,0:T(8,128)S(1)} %fusion.93, f32[48,48,48]{2,1,0:T(8,128)S(1)} %slice_bitcast_fusion, f32[]{:T(128)} %bitcast.2), kind=kOutput, calls=%fused_computation.11 | convolution fusion | flops 95910912 | bytes 6045700 | tf_op jit(solution)/shard_map/absc,ck->absk/dot_general | solution.py:53
  45.4 1.9 %convolution_bitcast_fusion.1 = f32[48,48,3,48]{3,1,2,0:T(8,128)S(1)} fusion(f32[48,48,3,48]{3,1,2,0:T(8,128)S(1)} %fusion.8, f32[]{:T(128)} %bitcast.2), kind=kOutput, calls=%fused_computation.17 | convolution fusion | flops 95579136 | bytes 2654212 | tf_op jit(solution)/shard_map/absc,kb->aksc/dot_general | solution.py:54
  47.3 3.2 %fusion.11 = f32[48,48,3,48]{3,0,2,1:T(8,128)S(1)} fusion(f32[48,48,3,48]{3,1,2,0:T(8,128)S(1)} %convolution_bitcast_fusion.1, f32[48,48,48]{2,0,1:T(8,128)S(1)} %fusion.17, f32[]{:T(128)} %bitcast.2), kind=kOutput, calls=%fused_computation.18 | convolution fusion | flops 95910912 | bytes 3096580 | tf_op jit(solution)/shard_map/absc,ka->kbsc/dot_general | solution.py:55
  50.5 2.8 %fusion.4 = f32[48,48,3,48]{3,1,2,0:T(8,128)S(1)} fusion(f32[48,48,3,48]{3,0,2,1:T(8,128)S(1)} %fusion.11, f32[]{:T(128)} %bitcast.2), kind=kOutput, calls=%fused_computation.7 | convolution fusion | flops 95579136 | bytes 2654212 | tf_op jit(solution)/shard_map/absc,ck->absk/dot_general | solution.py:53
  53.2 1.9 %convolution_bitcast_fusion = f32[48,48,3,48]{3,1,2,0:T(8,128)S(1)} fusion(f32[48,48,3,48]{3,1,2,0:T(8,128)S(1)} %fusion.4, f32[]{:T(128)} %bitcast.2), kind=kOutput, calls=%fused_computation.16 | convolution fusion | flops 95579136 | bytes 2654212 | tf_op jit(solution)/shard_map/absc,kb->aksc/dot_general | solution.py:54
  55.1 0.0 copy-start.3
  55.2 2.9 %fusion.2 = f32[48,48,3,48]{3,0,2,1:T(8,128)S(1)} fusion(f32[48,48,3,48]{3,1,2,0:T(8,128)S(1)} %convolution_bitcast_fusion, f32[]{:T(128)} %bitcast.2), kind=kOutput, calls=%fused_computation.5 | convolution fusion | flops 95579136 | bytes 2654212 | tf_op jit(solution)/shard_map/absc,ka->kbsc/dot_general | solution.py:55
  58.1 0.0 copy-done.3
  58.1 1.5 %fusion.1 = f32[48,48,48]{2,1,0:T(8,128)S(1)} fusion(f32[48,48,3,48]{3,0,2,1:T(8,128)S(1)} %fusion.2, f32[48,48,4,48]{3,1,2,0:T(8,128)S(1)} %fusion.93, f32[3]{0:T(128)S(1)} %copy-done.3), kind=kLoop, calls=%fused_computation.4 | loop fusion | flops 884736 | bytes 3096588 | tf_op jit(solution)/shard_map/reduce_sum | solution.py:97
  59.6 1.7 %fusion.34 = (f32[448,48]{0,1:T(8,128)S(1)}, f32[448,48]{0,1:T(8,128)S(1)}) fusion(s32[448]{0:T(512)S(1)} %get-tuple-element.19, f32[2304,448]{1,0:T(8,128)S(1)} %bitcast.87, f32[2304,48]{1,0:T(8,128)S(1)} %bitcast.88), kind=kOutput, calls=%fused_computation.58 | convolution fusion | flops 297529344 | bytes 4744960 | tf_op jit(solution)/shard_map/dot_general | solution.py:98
  61.3 0.2 fusion.18
  61.5 0.1 copy.36
  61.7 0.2 reshape.246
  61.8 9.4 %all_to_all.10 = f32[8,1,1792]{2,1,0:T(1,128)S(1)} all-to-all(f32[8,1,1792]{2,1,0:T(1,128)S(1)} %reshape.246), channel_id=1, replica_groups=mesh['grp'=4,'col'=8] {'col'}, dimensions={0} | all-to-all | bytes 114688 | tf_op jit(solution)/shard_map/all_to_all | solution.py:102
  71.3 0.6 copy.64
  (9 shorter events, 0.1 us)
Async XLA Ops:
  0.0 14.1 %copy-start.2 = (s32[448]{0:T(512)S(1)}, s32[448]{0:T(512)}, u32[]{:S(2)}) copy-start(s32[448]{0:T(512)} %param.6) | copy-start | bytes 5380
  0.0 11.9 %copy-start.1 = (s32[448]{0:T(512)S(1)}, s32[448]{0:T(512)}, u32[]{:S(2)}) copy-start(s32[448]{0:T(512)} %param.7) | copy-start | bytes 5380
  4.5 32.1 %all-to-all-start = ((f32[32,4,1792]{2,1,0:T(4,128)}), f32[32,4,1792]{2,1,0:T(4,128)S(1)}, u32[]{:S(2)}, u32[]{:S(2)}) async-start(f32[32,4,1792]{2,1,0:T(4,128)} %bitcast.1), calls=%async_computation | async-start | bytes 1835008 | tf_op jit(solution)/shard_map/all_to_all | solution.py:75
  37.2 2.3 %copy-start = (f32[48,48,448]{2,1,0:T(8,128)S(1)}, f32[48,48,448]{2,1,0:T(8,128)}, u32[]{:S(2)}) copy-start(f32[48,48,448]{2,1,0:T(8,128)} %broadcast_multiply_fusion) | copy-start | bytes 12386308
  55.1 3.0 %copy-start.3 = (f32[3]{0:T(128)S(1)}, f32[3]{0:T(128)}, u32[]{:S(2)}) copy-start(f32[3]{0:T(128)} %param.9) | copy-start | bytes 40

commit v6 on v2

--- a/solution.py
+++ b/solution.py
@@ -91,8 +91,14 @@
         own = grids[:, :, :1]
         src = grids[:, :, 1:]
         density = own * src
-        potential = cas_three(kernel[:, :, None, :] * cas_three(density, table), table)
-        total = jnp.sum(weights[None, None, :, None] * potential * src, axis=2)
+        field = jnp.einsum("absc,ck->absk", density, table, precision=MID)
+        field = jnp.einsum("absk,lb->askl", field, table, precision=MID)
+        field = jnp.einsum("askl,ma->sklm", field, table, precision=MID)
+        field = kernel[None] * field
+        field = jnp.einsum("sxyz,zw->sxyw", field, table, precision=MID)
+        field = jnp.einsum("sxyw,vy->sxwv", field, table, precision=MID)
+        potential = jnp.einsum("sxwv,ux->swvu", field, table, precision=MID)
+        total = jnp.sum(weights[:, None, None, None] * potential * jnp.transpose(src, (2, 0, 1, 3)), axis=0)
         back = lax.dot_general(w, total.reshape(extent * extent, extent), (((0,), (0,)), ((), ())), precision=MID)
         scaled = jnp.concatenate([back * cos_h, -(back * sin_h)], axis=1)
         out = -jnp.dot(scaled, bwd, precision=MID)

time: 66.8 us -> 82.5 us (1.24)
  matrix products: 22.7 us -> 36.1 us
  local copies, waits for them, and re-layouts: 7.62 us -> 11.9 us
  other arithmetic: 7.81 us -> 6.33 us
    dot_general x6, matrix products: 14.3 us -> 27.7 us  [the longest x1 6.39 us: local(): field = jnp.einsum('absk,lb->askl', field, table, precision=MID)]
    dot_general x0 -> x1, local copies, waits for them, and re-layouts: none -> 3.64 us  [local(): field = jnp.einsum('sxyz,zw->sxyw', field, table, precision=MID)]
    reduce_sum x1 -> x0, other arithmetic: 1.47 us -> none  [local(): total = jnp.sum(weights[None, None, :, None] * potential * src, axis=2)]
    unnamed x9 -> x23, local copies, waits for them, and re-layouts: 1.97 us -> 2.01 us
  transfers between devices with their start and end apart: 2 -> 2, of which waited for: 2 -> 2; matrix products, arithmetic and copies ran while one was open for 9% -> 8% of each run, Pallas kernels for 0% -> 0%
where the time goes in v6:
time: 82.5 us; the launch traced here: 81.9 us
  matrix products  36.1 us (44%)
  local copies, waits for them, and re-layouts  11.9 us (14%)
  starting transfers between devices  10.5 us (13%)
  blocking collectives  10 us (12%)
  other arithmetic  6.33 us (8%)
  waiting for transfers between devices  6.01 us (7%)
  between operations  1.04 us (1%)
    all_to_all x1, blocking collectives, local(): lax.all_to_all(out.reshape(n_col, 1, width), 'col', 0, 0, tiled=True)  10 us
    dot_general x1, matrix products, local(): field = jnp.einsum('absk,lb->askl', field, table, precision=MID)  6.39 us
    dot_general x1, matrix products, local(): field = jnp.einsum('absc,ck->absk', density, table, precision=MID)  6.33 us
    all_to_all x1, starting transfers between devices, local(): got = lax.all_to_all(send, 'col', 0, 0, tiled=True)  6.31 us
    dot_general x1, matrix products, local(): field = jnp.einsum('sxyw,vy->sxwv', field, table, precision=MID)  6.11 us
    all_to_all x1, starting transfers between devices, local(): picked = jnp.sum(lax.all_to_all(spread, 'grp', 0, 0, tiled=True), axis=0)  4.24 us
    dot_general x1, matrix products, local(): grids = jnp.dot(w, cols.reshape(count, n * extent), precision=MID)  4.14 us
    dot_general x1, local copies, waits for them, and re-layouts, local(): field = jnp.einsum('sxyz,zw->sxyw', field, table, precision=MID)  3.64 us
  transfers between devices with their start and end apart: 2, of which 2 were waited for; matrix products, arithmetic and copies ran while one was open for 8% of the time, Pallas kernels for 0%

profile of v6, /device:TPU:0, one launch (start us, length us, event | category | flops | bytes accessed | tf_op | source)
XLA Modules:
  0.0 81.9 jit_solution(2283053908529867394)
XLA Ops:
  0.0 0.7 and_select_fusion.1
  0.7 0.7 fusion.59
  1.4 1.0 %convolution_select_fusion = f32[3,1792]{1,0:T(4,128)S(1)} fusion(f32[8,1792]{1,0:T(8,128)} %param.5, pred[3]{0:T(512)(128)(4,1)S(1)} %fusion.59, s32[3]{0:T(128)S(1)} %and_select_fusion.1), kind=kOutput, calls=%fused_computation.14 | convolution fusion | flops 521496 | bytes 78863 | tf_op jit(solution)/shard_map/dot_general | solution.py:69
  2.4 0.7 broadcast_in_dim.36
  3.1 4.2 %all-to-all-start = ((f32[4,3,1792]{2,1,0:T(4,128)}), f32[4,3,1792]{2,1,0:T(4,128)S(1)}, u32[]{:S(2)}, u32[]{:S(2)}) async-start(f32[4,3,1792]{2,1,0:T(4,128)} %broadcast_in_dim.36), calls=%async_computation | async-start | bytes 229376 | tf_op jit(solution)/shard_map/all_to_all | solution.py:72
  7.3 0.9 %broadcast_in_dim.33 = f32[8,1,1792]{2,1,0:T(1,128)S(1)} reshape(f32[8,1792]{1,0:T(8,128)} %param.5) | data formatting | bytes 114688 | tf_op jit(solution)/shard_map/broadcast_in_dim | solution.py:74
  8.2 0.1 broadcast_add_fusion
  8.3 0.4 fusion.16
  8.7 3.1 %all-to-all-done = f32[4,3,1792]{2,1,0:T(4,128)S(1)} async-done(((f32[4,3,1792]{2,1,0:T(4,128)}), f32[4,3,1792]{2,1,0:T(4,128)S(1)}, u32[]{:S(2)}, u32[]{:S(2)}) %all-to-all-start) | async-done | bytes 86048 | tf_op jit(solution)/shard_map/all_to_all | solution.py:72
  11.8 0.8 pad_maximum_fusion
  12.6 1.2 %slice.21 = s32[1]{0:T(128)} slice(s32[448]{0:T(512)} %param.7), slice={[0:1]} | slice | bytes 8 | tf_op jit(solution)/shard_map/slice | solution.py:77
  13.8 0.8 lt.80
  15.3 0.1 multiply_add_fusion
  15.4 0.1 copy.49
  15.5 0.6 gather_fusion
  16.0 0.1 maximum_bitcast_fusion
  16.1 0.1 dot_general.54
  16.2 6.3 %all-to-all-start.1 = ((f32[8,4,1792]{2,1,0:T(4,128)}), f32[8,4,1792]{2,1,0:T(4,128)S(1)}, u32[]{:S(2)}, u32[]{:S(2)}) async-start(f32[8,4,1792]{2,1,0:T(4,128)} %pad_maximum_fusion), calls=%async_computation.1 | async-start | bytes 458752 | tf_op jit(solution)/shard_map/all_to_all | solution.py:76
  22.5 0.0 copy-done.7
  22.5 0.0 copy-done.5
  22.6 0.0 copy-start.3
  22.6 0.3 fusion.29
  22.9 0.3 fusion.30
  23.2 2.7 %broadcast_multiply_fusion = f32[48,48,448]{2,1,0:T(8,128)} fusion(f32[48,448]{1,0:T(8,128)S(1)} %fusion.30, f32[48,448]{1,0:T(8,128)S(1)} %fusion.29), kind=kLoop, calls=%fused_computation.13 | loop fusion | flops 1032192 | bytes 4300800 | tf_op jit(solution)/shard_map/mul | solution.py:49
  25.9 0.6 gather_fusion.1
  26.5 0.7 copy.50
  27.2 0.1 iota_compare_fusion
  27.3 0.4 fusion.27
  27.7 2.9 %all-to-all-done.1 = f32[8,4,1792]{2,1,0:T(4,128)S(1)} async-done(((f32[8,4,1792]{2,1,0:T(4,128)}), f32[8,4,1792]{2,1,0:T(4,128)S(1)}, u32[]{:S(2)}, u32[]{:S(2)}) %all-to-all-start.1) | async-done | bytes 229408 | tf_op jit(solution)/shard_map/all_to_all | solution.py:76
  30.6 0.0 copy-done.3
  30.7 0.3 reshape.210
  31.0 0.0 copy-start
  31.0 0.1 broadcast_select_fusion
  31.1 0.7 fusion.34
  31.8 0.1 fusion.93
  31.9 0.1 fusion.18
  32.0 1.3 %copy-done = f32[48,48,448]{2,1,0:T(8,128)S(1)} copy-done((f32[48,48,448]{2,1,0:T(8,128)S(1)}, f32[48,48,448]{2,1,0:T(8,128)}, u32[]{:S(2)}) %copy-start) | copy-done | bytes 4128792
  33.3 4.1 %fusion.94 = f32[48,48,4,48]{3,1,2,0:T(8,128)S(1)} fusion(f32[48,48,448,1]{2,1,3,0:T(8,128)S(1)} %bitcast.77, f32[4,48,448,1]{2,1,0,3:T(8,128)S(1)} %bitcast.84), kind=kOutput, calls=%fused_computation.137 | convolution fusion | flops 1189085184 | bytes 6242304 | tf_op jit(solution)/shard_map/dot_general | solution.py:89
  37.5 0.0 copy-start.1
  37.5 0.1 slice_bitcast_fusion
  37.6 6.3 %fusion.7 = f32[48,48,3,48]{1,3,2,0:T(8,128)S(1)} fusion(f32[48,48,4,48]{3,1,2,0:T(8,128)S(1)} %fusion.94, f32[48,48,48]{2,1,0:T(8,128)S(1)} %slice_bitcast_fusion, f32[]{:T(128)} %bitcast), kind=kOutput, calls=%fused_computation.10 | convolution fusion | flops 95910912 | bytes 6045700 | tf_op jit(solution)/shard_map/absc,ck->absk/dot_general | solution.py:94
  43.9 0.0 copy-done.1
  43.9 6.4 %fusion.3 = f32[48,3,48,48]{0,3,2,1:T(8,128)S(1)} fusion(f32[48,48,3,48]{1,3,2,0:T(8,128)S(1)} %fusion.7, f32[]{:T(128)} %bitcast), kind=kOutput, calls=%fused_computation.6 | convolution fusion | flops 95579136 | bytes 2654212 | tf_op jit(solution)/shard_map/absk,lb->askl/dot_general | solution.py:95
  50.3 1.7 %fusion.42 = f32[3,48,48,48]{3,2,1,0:T(8,128)S(1)} fusion(f32[48,3,48,48]{0,3,2,1:T(8,128)S(1)} %fusion.3, f32[]{:T(128)} %bitcast), kind=kOutput, calls=%fused_computation.62 | convolution fusion | flops 95579136 | bytes 2654212 | tf_op jit(solution)/shard_map/askl,ma->sklm/dot_general | solution.py:96
  52.0 3.6 %fusion.5 = f32[3,48,48,48]{3,2,1,0:T(8,128)} fusion(f32[3,48,48,48]{3,2,1,0:T(8,128)S(1)} %fusion.42, f32[48,48,48]{2,1,0:T(8,128)S(1)} %fusion.16, f32[]{:T(128)} %bitcast), kind=kOutput, calls=%fused_computation.8 | convolution fusion | flops 95910912 | bytes 3096580 | tf_op jit(solution)/shard_map/sxyz,zw->sxyw/dot_general | solution.py:98
  55.6 3.6 %copy.46 = f32[3,48,48,48]{2,1,3,0:T(8,128)S(1)} copy(f32[3,48,48,48]{3,2,1,0:T(8,128)} %fusion.5) | data formatting | bytes 2654208 | tf_op jit(solution)/shard_map/sxyz,zw->sxyw/dot_general | solution.py:98
  59.2 0.0 copy-start.8
  59.2 0.0 slice-start
  59.2 6.1 %fusion.39 = f32[3,48,48,48]{1,3,2,0:T(8,128)S(1)} fusion(f32[3,48,48,48]{2,1,3,0:T(8,128)S(1)} %copy.46, f32[]{:T(128)} %bitcast), kind=kOutput, calls=%fused_computation.59 | convolution fusion | flops 95579136 | bytes 2654212 | tf_op jit(solution)/shard_map/sxyw,vy->sxwv/dot_general | solution.py:99
  65.4 0.0 copy-done.8
  65.4 0.0 slice-start.1
  65.4 0.0 copy-start.4
  65.4 3.6 %fusion = f32[48,48,48]{2,1,0:T(8,128)S(1)} fusion(f32[48,48,4,48]{3,1,2,0:T(8,128)} %copy-done.1, f32[3,48,48,48]{1,3,2,0:T(8,128)S(1)} %fusion.39, f32[3]{0:T(128)S(1)} %copy-done.8, f32[]{:T(128)} %bitcast), kind=kOutput, calls=%fused_computation.3 | convolution fusion | flops 96463872 | bytes 3096592 | tf_op jit(solution)/shard_map/sxwv,ux->swvu/dot_general | solution.py:100
  69.0 0.0 copy-start.2
  69.0 0.0 copy-start.6
  69.0 0.0 slice-done
  69.1 0.0 slice-done.1
  69.1 0.0 copy-done.4
  69.1 1.6 %fusion.33 = (f32[448,48]{0,1:T(8,128)S(1)}, f32[448,48]{0,1:T(8,128)S(1)}) fusion(s32[448]{0:T(512)S(1)} %copy-done.4, f32[2304,448]{1,0:T(8,128)S(1)} %bitcast.80, f32[2304,48]{1,0:T(8,128)S(1)} %bitcast.81), kind=kOutput, calls=%fused_computation.53 | convolution fusion | flops 297529344 | bytes 4744960 | tf_op jit(solution)/shard_map/dot_general | solution.py:102
  70.7 0.2 fusion.17
  71.0 0.1 copy.51
  71.1 0.2 reshape.235
  71.3 10.0 %all_to_all.15 = f32[8,1,1792]{2,1,0:T(1,128)S(1)} all-to-all(f32[8,1,1792]{2,1,0:T(1,128)S(1)} %reshape.235), channel_id=1, replica_groups=mesh['grp'=4,'col'=8] {'col'}, dimensions={0} | all-to-all | bytes 114688 | tf_op jit(solution)/shard_map/all_to_all | solution.py:106
  81.3 0.6 copy.77
  (13 shorter events, 0.2 us)
Async XLA Ops:
  0.0 22.5 %copy-start.7 = (s32[448]{0:T(512)S(1)}, s32[448]{0:T(512)}, u32[]{:S(2)}) copy-start(s32[448]{0:T(512)} %param.6) | copy-start | bytes 5380
  0.0 22.5 %copy-start.5 = (s32[448]{0:T(512)S(1)}, s32[448]{0:T(512)}, u32[]{:S(2)}) copy-start(s32[448]{0:T(512)} %param.7) | copy-start | bytes 5380
  3.1 8.7 %all-to-all-start = ((f32[4,3,1792]{2,1,0:T(4,128)}), f32[4,3,1792]{2,1,0:T(4,128)S(1)}, u32[]{:S(2)}, u32[]{:S(2)}) async-start(f32[4,3,1792]{2,1,0:T(4,128)} %broadcast_in_dim.36), calls=%async_computation | async-start | bytes 229376 | tf_op jit(solution)/shard_map/all_to_all | solution.py:72
  16.2 14.4 %all-to-all-start.1 = ((f32[8,4,1792]{2,1,0:T(4,128)}), f32[8,4,1792]{2,1,0:T(4,128)S(1)}, u32[]{:S(2)}, u32[]{:S(2)}) async-start(f32[8,4,1792]{2,1,0:T(4,128)} %pad_maximum_fusion), calls=%async_computation.1 | async-start | bytes 458752 | tf_op jit(solution)/shard_map/all_to_all | solution.py:76
  22.6 8.1 %copy-start.3 = (s32[448]{0:T(512)}, s32[448]{0:T(512)S(1)}, u32[]{:S(2)}) copy-start(s32[448]{0:T(512)S(1)} %get-tuple-element.19) | copy-start | bytes 5380
  31.0 2.3 %copy-start = (f32[48,48,448]{2,1,0:T(8,128)S(1)}, f32[48,48,448]{2,1,0:T(8,128)}, u32[]{:S(2)}) copy-start(f32[48,48,448]{2,1,0:T(8,128)} %broadcast_multiply_fusion) | copy-start | bytes 12386308
  37.5 6.4 %copy-start.1 = (f32[48,48,4,48]{3,1,2,0:T(8,128)}, f32[48,48,4,48]{3,1,2,0:T(8,128)S(1)}, u32[]{:S(2)}) copy-start(f32[48,48,4,48]{3,1,2,0:T(8,128)S(1)} %fusion.94) | copy-start | bytes 5308420
  59.2 6.1 %copy-start.8 = (f32[3]{0:T(128)S(1)}, f32[3]{0:T(128)}, u32[]{:S(2)}) copy-start(f32[3]{0:T(128)} %param.9) | copy-start | bytes 40
  59.2 9.8 %slice-start = ((s8[4718592]{0:T(1024)(128)(4,1)}), s8[4194304]{0:T(1024)(128)(4,1)S(1)}, s32[]{:S(2)}) async-start(s8[4718592]{0:T(1024)(128)(4,1)} %bitcast.78), calls=%async_computation.3 | async-start | bytes 8388608
  65.4 3.7 %slice-start.1 = ((s8[4718592]{0:T(1024)(128)(4,1)}), s8[524288]{0:T(1024)(128)(4,1)S(1)}, s32[]{:S(2)}) async-start(s8[4718592]{0:T(1024)(128)(4,1)} %bitcast.78), calls=%async_computation.4 | async-start | bytes 1048576
  65.4 3.7 %copy-start.4 = (s32[448]{0:T(512)S(1)}, s32[448]{0:T(512)}, u32[]{:S(2)}) copy-start(s32[448]{0:T(512)} %copy-done.3) | copy-start | bytes 5380
  69.0 1.7 %copy-start.2 = (f32[48,32]{0,1:T(8,128)S(1)}, f32[48,32]{0,1:T(8,128)}, u32[]{:S(2)}) copy-start(f32[48,32]{0,1:T(8,128)} %copy.50) | copy-start | bytes 18436
  69.0 1.7 %copy-start.6 = (s32[448]{0:T(512)S(1)}, s32[448]{0:T(512)}, u32[]{:S(2)}) copy-start(s32[448]{0:T(512)} %param.7) | copy-start | bytes 5380

commit v7 on v2

--- a/solution.py
+++ b/solution.py
@@ -84,18 +84,18 @@
         n = 1 + n_src
         coeff = got.reshape(n_col, n, width // depth, depth).transpose(0, 2, 1, 3).reshape(count, n, depth)
         coeff = jnp.where(live[:, None, :], coeff, 0.0)
-        both = jnp.dot(coeff.reshape(count * n, depth), fwd, precision=MID).reshape(count, n, 2, extent)
+        both = jnp.dot(coeff.reshape(count * n, depth), fwd, precision=HI).reshape(count, n, 2, extent)
         cols = cos_h[:, None, :] * both[:, :, 0] - sin_h[:, None, :] * both[:, :, 1]
-        grids = jnp.dot(w, cols.reshape(count, n * extent), precision=MID)
+        grids = jnp.dot(w, cols.reshape(count, n * extent), precision=HI)
         grids = grids.reshape(extent, extent, n, extent)
         own = grids[:, :, :1]
         src = grids[:, :, 1:]
         density = own * src
         potential = cas_three(kernel[:, :, None, :] * cas_three(density, table), table)
         total = jnp.sum(weights[None, None, :, None] * potential * src, axis=2)
-        back = lax.dot_general(w, total.reshape(extent * extent, extent), (((0,), (0,)), ((), ())), precision=MID)
+        back = lax.dot_general(w, total.reshape(extent * extent, extent), (((0,), (0,)), ((), ())), precision=HI)
         scaled = jnp.concatenate([back * cos_h, -(back * sin_h)], axis=1)
-        out = -jnp.dot(scaled, bwd, precision=MID)
+        out = -jnp.dot(scaled, bwd, precision=HI)
         out = jnp.where(live, out, 0.0)
         return lax.all_to_all(out.reshape(n_col, 1, width), "col", 0, 0, tiled=True).reshape(n_col, width)
 

time: 66.8 us -> 72.8 us (1.090)
  matrix products: 22.7 us -> 29.3 us
    dot_general x3, matrix products: 5.01 us -> 9.8 us  [the longest x1 8.18 us: local(): grids = jnp.dot(w, cols.reshape(count, n * extent), precision=HI)]
    dot_general x1, matrix products: 1.7 us -> 3.29 us  [local(): lax.dot_general(w, total.reshape(extent * extent, extent), (((0,), (0,)),...]
  transfers between devices with their start and end apart: 2 -> 2, of which waited for: 2 -> 2; matrix products, arithmetic and copies ran while one was open for 9% -> 8% of each run, Pallas kernels for 0% -> 0%
where the time goes in v7:
time: 72.8 us; the launch traced here: 72.2 us
  matrix products  29.3 us (40%)
  starting transfers between devices  10.5 us (14%)
  blocking collectives  10 us (14%)
  other arithmetic  7.81 us (11%)
  local copies, waits for them, and re-layouts  7.01 us (10%)
  waiting for transfers between devices  6.62 us (9%)
  between operations  0.93 us (1%)
    all_to_all x1, blocking collectives, local(): lax.all_to_all(out.reshape(n_col, 1, width), 'col', 0, 0, tiled=True)  10 us
    dot_general x1, matrix products, local(): grids = jnp.dot(w, cols.reshape(count, n * extent), precision=HI)  8.18 us
    all_to_all x1, starting transfers between devices, local(): got = lax.all_to_all(send, 'col', 0, 0, tiled=True)  6.31 us
    dot_general x2, matrix products, cas_three(): return jnp.einsum('absc,ka->kbsc', field, table, precision=MID)  6.18 us
    dot_general x2, matrix products, cas_three(): field = jnp.einsum('absc,ck->absk', field, table, precision=MID)  4.65 us
    all_to_all x1, starting transfers between devices, local(): picked = jnp.sum(lax.all_to_all(spread, 'grp', 0, 0, tiled=True), axis=0)  4.24 us
    dot_general x2, matrix products, cas_three(): field = jnp.einsum('absc,kb->aksc', field, table, precision=MID)  3.76 us
    all_to_all x1, waiting for transfers between devices, local(): got = lax.all_to_all(send, 'col', 0, 0, tiled=True)  3.53 us
  transfers between devices with their start and end apart: 2, of which 2 were waited for; matrix products, arithmetic and copies ran while one was open for 8% of the time, Pallas kernels for 0%

profile of v7, /device:TPU:0, one launch (start us, length us, event | category | flops | bytes accessed | tf_op | source)
XLA Modules:
  0.0 72.2 jit_solution(7140965104200508559)
XLA Ops:
  0.0 0.0 copy-start.2
  0.0 0.0 copy-start.1
  0.0 0.7 and_select_fusion.1
  0.7 0.7 fusion.58
  1.4 1.0 %convolution_select_fusion = f32[3,1792]{1,0:T(4,128)S(1)} fusion(f32[8,1792]{1,0:T(8,128)} %param.5, pred[3]{0:T(512)(128)(4,1)S(1)} %fusion.58, s32[3]{0:T(128)S(1)} %and_select_fusion.1), kind=kOutput, calls=%fused_computation.15 | convolution fusion | flops 521496 | bytes 78863 | tf_op jit(solution)/shard_map/dot_general | solution.py:69
  2.4 0.7 broadcast_in_dim.36
  3.1 4.2 %all-to-all-start = ((f32[4,3,1792]{2,1,0:T(4,128)}), f32[4,3,1792]{2,1,0:T(4,128)S(1)}, u32[]{:S(2)}, u32[]{:S(2)}) async-start(f32[4,3,1792]{2,1,0:T(4,128)} %broadcast_in_dim.36), calls=%async_computation | async-start | bytes 229376 | tf_op jit(solution)/shard_map/all_to_all | solution.py:72
  7.3 0.9 %broadcast_in_dim.33 = f32[8,1,1792]{2,1,0:T(1,128)S(1)} reshape(f32[8,1792]{1,0:T(8,128)} %param.5) | data formatting | bytes 114688 | tf_op jit(solution)/shard_map/broadcast_in_dim | solution.py:74
  8.2 0.1 broadcast_add_fusion
  8.3 0.4 fusion.17
  8.7 3.1 %all-to-all-done = f32[4,3,1792]{2,1,0:T(4,128)S(1)} async-done(((f32[4,3,1792]{2,1,0:T(4,128)}), f32[4,3,1792]{2,1,0:T(4,128)S(1)}, u32[]{:S(2)}, u32[]{:S(2)}) %all-to-all-start) | async-done | bytes 86048 | tf_op jit(solution)/shard_map/all_to_all | solution.py:72
  11.8 0.8 %pad_maximum_fusion = f32[8,4,1792]{2,1,0:T(4,128)} fusion(f32[8,3,1792]{2,1,0:T(4,128)S(1)} %broadcast_in_dim.37, f32[8,1,1792]{2,1,0:T(1,128)S(1)} %broadcast_in_dim.33), kind=kLoop, calls=%fused_computation.32 | loop fusion | flops 57344 | bytes 458752 | tf_op jit(solution)/shard_map/concatenate | solution.py:73
  12.6 1.2 %slice.21 = s32[1]{0:T(128)} slice(s32[448]{0:T(512)} %param.7), slice={[0:1]} | slice | bytes 8 | tf_op jit(solution)/shard_map/slice | solution.py:77
  13.8 0.8 %lt.80 = s32[8,56]{1,0:T(8,128)S(1)} reshape(s32[448]{0:T(512)} %param.7) | data formatting | bytes 3584 | tf_op jit(solution)/shard_map/lt | solution.py:39
  15.3 0.1 multiply_add_fusion
  15.4 0.1 copy.46
  15.5 0.6 gather_fusion
  16.0 0.1 maximum_bitcast_fusion
  16.1 0.1 dot_general.54
  16.2 6.3 %all-to-all-start.1 = ((f32[8,4,1792]{2,1,0:T(4,128)}), f32[8,4,1792]{2,1,0:T(4,128)S(1)}, u32[]{:S(2)}, u32[]{:S(2)}) async-start(f32[8,4,1792]{2,1,0:T(4,128)} %pad_maximum_fusion), calls=%async_computation.1 | async-start | bytes 458752 | tf_op jit(solution)/shard_map/all_to_all | solution.py:76
  22.5 0.0 copy-done.2
  22.5 0.0 copy-done.1
  22.6 0.3 fusion.30
  22.9 0.3 fusion.31
  23.2 2.7 %broadcast_multiply_fusion = f32[48,48,448]{2,1,0:T(8,128)} fusion(f32[48,448]{1,0:T(8,128)S(1)} %fusion.31, f32[48,448]{1,0:T(8,128)S(1)} %fusion.30), kind=kLoop, calls=%fused_computation.14 | loop fusion | flops 1032192 | bytes 4300800 | tf_op jit(solution)/shard_map/mul | solution.py:49
  25.9 0.6 gather_fusion.1
  26.5 0.1 copy.47
  26.6 0.1 iota_compare_fusion
  26.7 0.4 fusion.28
  27.1 3.5 %all-to-all-done.1 = f32[8,4,1792]{2,1,0:T(4,128)S(1)} async-done(((f32[8,4,1792]{2,1,0:T(4,128)}), f32[8,4,1792]{2,1,0:T(4,128)S(1)}, u32[]{:S(2)}, u32[]{:S(2)}) %all-to-all-start.1) | async-done | bytes 229408 | tf_op jit(solution)/shard_map/all_to_all | solution.py:76
  30.7 0.3 reshape.210
  31.0 0.0 copy-start
  31.0 0.1 broadcast_select_fusion
  31.1 1.4 %fusion.35 = f32[448,4,2,48]{0,3,2,1:T(8,128)S(1)} fusion(f32[448,4,32,1]{2,0,3,1:T(8,128)S(1)} %bitcast.80, f32[2,48,32]{1,0,2:T(2,128)S(1)} %dot_general.54), kind=kOutput, calls=%fused_computation.57 | convolution fusion | flops 66060288 | bytes 929792 | tf_op jit(solution)/shard_map/dot_general | solution.py:87
  32.4 0.1 fusion.92
  32.5 0.1 fusion.19
  32.6 0.7 copy-done
  33.3 8.2 %fusion.93 = f32[48,48,4,48]{3,1,2,0:T(8,128)S(1)} fusion(f32[48,48,448,1]{2,1,3,0:T(8,128)S(1)} %bitcast.77, f32[4,48,448,1]{2,1,0,3:T(8,128)S(1)} %bitcast.82), kind=kOutput, calls=%fused_computation.138 | convolution fusion | flops 2378170368 | bytes 6242304 | tf_op jit(solution)/shard_map/dot_general | solution.py:89
  41.5 0.1 slice_bitcast_fusion
  41.6 1.9 %fusion.8 = f32[48,48,3,48]{3,1,2,0:T(8,128)S(1)} fusion(f32[48,48,4,48]{3,1,2,0:T(8,128)S(1)} %fusion.93, f32[48,48,48]{2,1,0:T(8,128)S(1)} %slice_bitcast_fusion, f32[]{:T(128)} %bitcast), kind=kOutput, calls=%fused_computation.11 | convolution fusion | flops 95910912 | bytes 6045700 | tf_op jit(solution)/shard_map/absc,ck->absk/dot_general | solution.py:53
  43.5 1.9 %convolution_bitcast_fusion.1 = f32[48,48,3,48]{3,1,2,0:T(8,128)S(1)} fusion(f32[48,48,3,48]{3,1,2,0:T(8,128)S(1)} %fusion.8, f32[]{:T(128)} %bitcast), kind=kOutput, calls=%fused_computation.17 | convolution fusion | flops 95579136 | bytes 2654212 | tf_op jit(solution)/shard_map/absc,kb->aksc/dot_general | solution.py:54
  45.4 3.0 %fusion.11 = f32[48,48,3,48]{3,0,2,1:T(8,128)S(1)} fusion(f32[48,48,3,48]{3,1,2,0:T(8,128)S(1)} %convolution_bitcast_fusion.1, f32[48,48,48]{2,0,1:T(8,128)S(1)} %fusion.17, f32[]{:T(128)} %bitcast), kind=kOutput, calls=%fused_computation.18 | convolution fusion | flops 95910912 | bytes 3096580 | tf_op jit(solution)/shard_map/absc,ka->kbsc/dot_general | solution.py:55
  48.4 2.8 %fusion.4 = f32[48,48,3,48]{3,1,2,0:T(8,128)S(1)} fusion(f32[48,48,3,48]{3,0,2,1:T(8,128)S(1)} %fusion.11, f32[]{:T(128)} %bitcast), kind=kOutput, calls=%fused_computation.7 | convolution fusion | flops 95579136 | bytes 2654212 | tf_op jit(solution)/shard_map/absc,ck->absk/dot_general | solution.py:53
  51.2 1.9 %convolution_bitcast_fusion = f32[48,48,3,48]{3,1,2,0:T(8,128)S(1)} fusion(f32[48,48,3,48]{3,1,2,0:T(8,128)S(1)} %fusion.4, f32[]{:T(128)} %bitcast), kind=kOutput, calls=%fused_computation.16 | convolution fusion | flops 95579136 | bytes 2654212 | tf_op jit(solution)/shard_map/absc,kb->aksc/dot_general | solution.py:54
  53.1 0.0 copy-start.3
  53.1 3.2 %fusion.2 = f32[48,48,3,48]{3,0,2,1:T(8,128)S(1)} fusion(f32[48,48,3,48]{3,1,2,0:T(8,128)S(1)} %convolution_bitcast_fusion, f32[]{:T(128)} %bitcast), kind=kOutput, calls=%fused_computation.5 | convolution fusion | flops 95579136 | bytes 2654212 | tf_op jit(solution)/shard_map/absc,ka->kbsc/dot_general | solution.py:55
  56.3 0.0 copy-done.3
  56.3 1.5 %fusion.1 = f32[48,48,48]{2,1,0:T(8,128)S(1)} fusion(f32[48,48,3,48]{3,0,2,1:T(8,128)S(1)} %fusion.2, f32[48,48,4,48]{3,1,2,0:T(8,128)S(1)} %fusion.93, f32[3]{0:T(128)S(1)} %copy-done.3), kind=kLoop, calls=%fused_computation.4 | loop fusion | flops 884736 | bytes 3096588 | tf_op jit(solution)/shard_map/reduce_sum | solution.py:95
  57.7 3.3 %fusion.34 = (f32[448,48]{0,1:T(8,128)S(1)}, f32[448,48]{0,1:T(8,128)S(1)}) fusion(s32[448]{0:T(512)S(1)} %get-tuple-element.19, f32[2304,448]{1,0:T(8,128)S(1)} %bitcast.78, f32[2304,48]{1,0:T(8,128)S(1)} %bitcast.79), kind=kOutput, calls=%fused_computation.56 | convolution fusion | flops 594800640 | bytes 4744960 | tf_op jit(solution)/shard_map/dot_general | solution.py:96
  61.0 0.3 fusion.18
  61.3 0.1 copy.48
  61.5 0.2 reshape.235
  61.6 10.0 %all_to_all.15 = f32[8,1,1792]{2,1,0:T(1,128)S(1)} all-to-all(f32[8,1,1792]{2,1,0:T(1,128)S(1)} %reshape.235), channel_id=1, replica_groups=mesh['grp'=4,'col'=8] {'col'}, dimensions={0} | all-to-all | bytes 114688 | tf_op jit(solution)/shard_map/all_to_all | solution.py:100
  71.6 0.6 copy.75
  (8 shorter events, 0.2 us)
Async XLA Ops:
  0.0 22.5 %copy-start.2 = (s32[448]{0:T(512)S(1)}, s32[448]{0:T(512)}, u32[]{:S(2)}) copy-start(s32[448]{0:T(512)} %param.6) | copy-start | bytes 5380
  0.0 22.5 %copy-start.1 = (s32[448]{0:T(512)S(1)}, s32[448]{0:T(512)}, u32[]{:S(2)}) copy-start(s32[448]{0:T(512)} %param.7) | copy-start | bytes 5380
  3.1 8.7 %all-to-all-start = ((f32[4,3,1792]{2,1,0:T(4,128)}), f32[4,3,1792]{2,1,0:T(4,128)S(1)}, u32[]{:S(2)}, u32[]{:S(2)}) async-start(f32[4,3,1792]{2,1,0:T(4,128)} %broadcast_in_dim.36), calls=%async_computation | async-start | bytes 229376 | tf_op jit(solution)/shard_map/all_to_all | solution.py:72
  16.2 14.4 %all-to-all-start.1 = ((f32[8,4,1792]{2,1,0:T(4,128)}), f32[8,4,1792]{2,1,0:T(4,128)S(1)}, u32[]{:S(2)}, u32[]{:S(2)}) async-start(f32[8,4,1792]{2,1,0:T(4,128)} %pad_maximum_fusion), calls=%async_computation.1 | async-start | bytes 458752 | tf_op jit(solution)/shard_map/all_to_all | solution.py:76
  31.0 2.3 %copy-start = (f32[48,48,448]{2,1,0:T(8,128)S(1)}, f32[48,48,448]{2,1,0:T(8,128)}, u32[]{:S(2)}) copy-start(f32[48,48,448]{2,1,0:T(8,128)} %broadcast_multiply_fusion) | copy-start | bytes 12386308
  53.1 3.2 %copy-start.3 = (f32[3]{0:T(128)S(1)}, f32[3]{0:T(128)}, u32[]{:S(2)}) copy-start(f32[3]{0:T(128)} %param.9) | copy-start | bytes 40

commit v8 on v7

--- a/solution.py
+++ b/solution.py
@@ -86,14 +86,14 @@
         coeff = jnp.where(live[:, None, :], coeff, 0.0)
         both = jnp.dot(coeff.reshape(count * n, depth), fwd, precision=HI).reshape(count, n, 2, extent)
         cols = cos_h[:, None, :] * both[:, :, 0] - sin_h[:, None, :] * both[:, :, 1]
-        grids = jnp.dot(w, cols.reshape(count, n * extent), precision=HI)
+        grids = jnp.dot(w, cols.reshape(count, n * extent), precision=MID)
         grids = grids.reshape(extent, extent, n, extent)
         own = grids[:, :, :1]
         src = grids[:, :, 1:]
         density = own * src
         potential = cas_three(kernel[:, :, None, :] * cas_three(density, table), table)
         total = jnp.sum(weights[None, None, :, None] * potential * src, axis=2)
-        back = lax.dot_general(w, total.reshape(extent * extent, extent), (((0,), (0,)), ((), ())), precision=HI)
+        back = lax.dot_general(w, total.reshape(extent * extent, extent), (((0,), (0,)), ((), ())), precision=MID)
         scaled = jnp.concatenate([back * cos_h, -(back * sin_h)], axis=1)
         out = -jnp.dot(scaled, bwd, precision=HI)
         out = jnp.where(live, out, 0.0)

time: 72.8 us -> 66.8 us (0.918)
  matrix products: 29.3 us -> 23.3 us
    dot_general x1, matrix products: 8.18 us -> 4.04 us  [local(): grids = jnp.dot(w, cols.reshape(count, n * extent), precision=MID)]
    dot_general x1, matrix products: 3.29 us -> 1.7 us  [local(): lax.dot_general(w, total.reshape(extent * extent, extent), (((0,), (0,)),...]
  transfers between devices with their start and end apart: 2 -> 2, of which waited for: 2 -> 2; matrix products, arithmetic and copies ran while one was open for 8% -> 9% of each run, Pallas kernels for 0% -> 0%
where the time goes in v8:
time: 66.8 us; the launch traced here: 66.3 us
  matrix products  23.3 us (35%)
  starting transfers between devices  10.5 us (16%)
  blocking collectives  10 us (15%)
  other arithmetic  7.81 us (12%)
  local copies, waits for them, and re-layouts  7.01 us (10%)
  waiting for transfers between devices  6.62 us (10%)
  between operations  0.93 us (1%)
    all_to_all x1, blocking collectives, local(): lax.all_to_all(out.reshape(n_col, 1, width), 'col', 0, 0, tiled=True)  10 us
    all_to_all x1, starting transfers between devices, local(): got = lax.all_to_all(send, 'col', 0, 0, tiled=True)  6.31 us
    dot_general x2, matrix products, cas_three(): return jnp.einsum('absc,ka->kbsc', field, table, precision=MID)  6.12 us
    dot_general x2, matrix products, cas_three(): field = jnp.einsum('absc,ck->absk', field, table, precision=MID)  4.45 us
    all_to_all x1, starting transfers between devices, local(): picked = jnp.sum(lax.all_to_all(spread, 'grp', 0, 0, tiled=True), axis=0)  4.24 us
    dot_general x1, matrix products, local(): grids = jnp.dot(w, cols.reshape(count, n * extent), precision=MID)  4.04 us
    dot_general x2, matrix products, cas_three(): field = jnp.einsum('absc,kb->aksc', field, table, precision=MID)  3.76 us
    all_to_all x1, waiting for transfers between devices, local(): got = lax.all_to_all(send, 'col', 0, 0, tiled=True)  3.53 us
  transfers between devices with their start and end apart: 2, of which 2 were waited for; matrix products, arithmetic and copies ran while one was open for 9% of the time, Pallas kernels for 0%

profile of v8, /device:TPU:0, one launch (start us, length us, event | category | flops | bytes accessed | tf_op | source)
XLA Modules:
  0.0 66.3 jit_solution(16286631308607460990)
XLA Ops:
  0.0 0.0 copy-start.2
  0.0 0.0 copy-start.1
  0.0 0.7 %and_select_fusion.1 = s32[3]{0:T(128)S(1)} fusion(s32[3]{0:T(128)} %param.8), kind=kLoop, calls=%fused_computation.93 | loop fusion | flops 33 | bytes 24 | tf_op jit(solution)/shard_map/jit(remainder)/select_n | solution.py:68
  0.7 0.7 %fusion.58 = pred[3]{0:T(512)(128)(4,1)S(1)} fusion(s32[3]{0:T(128)} %param.8, s32[]{:T(128)S(6)} %axis_index.15), kind=kLoop, calls=%fused_computation.103 | loop fusion | flops 48 | bytes 19 | tf_op jit(solution)/shard_map/eq | solution.py:70
  1.4 1.0 %convolution_select_fusion = f32[3,1792]{1,0:T(4,128)S(1)} fusion(f32[8,1792]{1,0:T(8,128)} %param.5, pred[3]{0:T(512)(128)(4,1)S(1)} %fusion.58, s32[3]{0:T(128)S(1)} %and_select_fusion.1), kind=kOutput, calls=%fused_computation.15 | convolution fusion | flops 521496 | bytes 78863 | tf_op jit(solution)/shard_map/dot_general | solution.py:69
  2.4 0.7 broadcast_in_dim.36
  3.1 4.2 %all-to-all-start = ((f32[4,3,1792]{2,1,0:T(4,128)}), f32[4,3,1792]{2,1,0:T(4,128)S(1)}, u32[]{:S(2)}, u32[]{:S(2)}) async-start(f32[4,3,1792]{2,1,0:T(4,128)} %broadcast_in_dim.36), calls=%async_computation | async-start | bytes 229376 | tf_op jit(solution)/shard_map/all_to_all | solution.py:72
  7.3 0.9 %broadcast_in_dim.33 = f32[8,1,1792]{2,1,0:T(1,128)S(1)} reshape(f32[8,1792]{1,0:T(8,128)} %param.5) | data formatting | bytes 114688 | tf_op jit(solution)/shard_map/broadcast_in_dim | solution.py:74
  8.2 0.1 broadcast_add_fusion
  8.3 0.4 fusion.17
  8.7 3.1 %all-to-all-done = f32[4,3,1792]{2,1,0:T(4,128)S(1)} async-done(((f32[4,3,1792]{2,1,0:T(4,128)}), f32[4,3,1792]{2,1,0:T(4,128)S(1)}, u32[]{:S(2)}, u32[]{:S(2)}) %all-to-all-start) | async-done | bytes 86048 | tf_op jit(solution)/shard_map/all_to_all | solution.py:72
  11.8 0.8 %pad_maximum_fusion = f32[8,4,1792]{2,1,0:T(4,128)} fusion(f32[8,3,1792]{2,1,0:T(4,128)S(1)} %broadcast_in_dim.37, f32[8,1,1792]{2,1,0:T(1,128)S(1)} %broadcast_in_dim.33), kind=kLoop, calls=%fused_computation.32 | loop fusion | flops 57344 | bytes 458752 | tf_op jit(solution)/shard_map/concatenate | solution.py:73
  12.6 1.2 %slice.21 = s32[1]{0:T(128)} slice(s32[448]{0:T(512)} %param.7), slice={[0:1]} | slice | bytes 8 | tf_op jit(solution)/shard_map/slice | solution.py:77
  13.8 0.8 %lt.80 = s32[8,56]{1,0:T(8,128)S(1)} reshape(s32[448]{0:T(512)} %param.7) | data formatting | bytes 3584 | tf_op jit(solution)/shard_map/lt | solution.py:39
  15.3 0.1 multiply_add_fusion
  15.4 0.1 copy.46
  15.5 0.6 gather_fusion
  16.0 0.1 maximum_bitcast_fusion
  16.1 0.1 dot_general.54
  16.2 6.3 %all-to-all-start.1 = ((f32[8,4,1792]{2,1,0:T(4,128)}), f32[8,4,1792]{2,1,0:T(4,128)S(1)}, u32[]{:S(2)}, u32[]{:S(2)}) async-start(f32[8,4,1792]{2,1,0:T(4,128)} %pad_maximum_fusion), calls=%async_computation.1 | async-start | bytes 458752 | tf_op jit(solution)/shard_map/all_to_all | solution.py:76
  22.5 0.0 copy-done.2
  22.5 0.0 copy-done.1
  22.6 0.3 fusion.30
  22.9 0.3 fusion.31
  23.2 2.7 %broadcast_multiply_fusion = f32[48,48,448]{2,1,0:T(8,128)} fusion(f32[48,448]{1,0:T(8,128)S(1)} %fusion.31, f32[48,448]{1,0:T(8,128)S(1)} %fusion.30), kind=kLoop, calls=%fused_computation.14 | loop fusion | flops 1032192 | bytes 4300800 | tf_op jit(solution)/shard_map/mul | solution.py:49
  25.9 0.6 gather_fusion.1
  26.5 0.1 copy.47
  26.6 0.1 iota_compare_fusion
  26.7 0.4 fusion.28
  27.1 3.5 %all-to-all-done.1 = f32[8,4,1792]{2,1,0:T(4,128)S(1)} async-done(((f32[8,4,1792]{2,1,0:T(4,128)}), f32[8,4,1792]{2,1,0:T(4,128)S(1)}, u32[]{:S(2)}, u32[]{:S(2)}) %all-to-all-start.1) | async-done | bytes 229408 | tf_op jit(solution)/shard_map/all_to_all | solution.py:76
  30.7 0.3 reshape.210
  31.0 0.0 copy-start
  31.0 0.1 broadcast_select_fusion
  31.1 1.4 %fusion.35 = f32[448,4,2,48]{0,3,2,1:T(8,128)S(1)} fusion(f32[448,4,32,1]{2,0,3,1:T(8,128)S(1)} %bitcast.80, f32[2,48,32]{1,0,2:T(2,128)S(1)} %dot_general.54), kind=kOutput, calls=%fused_computation.57 | convolution fusion | flops 66060288 | bytes 929792 | tf_op jit(solution)/shard_map/dot_general | solution.py:87
  32.4 0.1 fusion.92
  32.5 0.1 fusion.19
  32.6 0.7 %copy-done = f32[48,48,448]{2,1,0:T(8,128)S(1)} copy-done((f32[48,48,448]{2,1,0:T(8,128)S(1)}, f32[48,48,448]{2,1,0:T(8,128)}, u32[]{:S(2)}) %copy-start) | copy-done | bytes 4128792
  33.3 4.0 %fusion.93 = f32[48,48,4,48]{3,1,2,0:T(8,128)S(1)} fusion(f32[48,48,448,1]{2,1,3,0:T(8,128)S(1)} %bitcast.77, f32[4,48,448,1]{2,1,0,3:T(8,128)S(1)} %bitcast.82), kind=kOutput, calls=%fused_computation.138 | convolution fusion | flops 1189085184 | bytes 6242304 | tf_op jit(solution)/shard_map/dot_general | solution.py:89
  37.4 0.1 slice_bitcast_fusion
  37.5 1.7 %fusion.8 = f32[48,48,3,48]{3,1,2,0:T(8,128)S(1)} fusion(f32[48,48,4,48]{3,1,2,0:T(8,128)S(1)} %fusion.93, f32[48,48,48]{2,1,0:T(8,128)S(1)} %slice_bitcast_fusion, f32[]{:T(128)} %bitcast), kind=kOutput, calls=%fused_computation.11 | convolution fusion | flops 95910912 | bytes 6045700 | tf_op jit(solution)/shard_map/absc,ck->absk/dot_general | solution.py:53
  39.2 1.9 %convolution_bitcast_fusion.1 = f32[48,48,3,48]{3,1,2,0:T(8,128)S(1)} fusion(f32[48,48,3,48]{3,1,2,0:T(8,128)S(1)} %fusion.8, f32[]{:T(128)} %bitcast), kind=kOutput, calls=%fused_computation.17 | convolution fusion | flops 95579136 | bytes 2654212 | tf_op jit(solution)/shard_map/absc,kb->aksc/dot_general | solution.py:54
  41.0 3.2 %fusion.11 = f32[48,48,3,48]{3,0,2,1:T(8,128)S(1)} fusion(f32[48,48,3,48]{3,1,2,0:T(8,128)S(1)} %convolution_bitcast_fusion.1, f32[48,48,48]{2,0,1:T(8,128)S(1)} %fusion.17, f32[]{:T(128)} %bitcast), kind=kOutput, calls=%fused_computation.18 | convolution fusion | flops 95910912 | bytes 3096580 | tf_op jit(solution)/shard_map/absc,ka->kbsc/dot_general | solution.py:55
  44.2 2.8 %fusion.4 = f32[48,48,3,48]{3,1,2,0:T(8,128)S(1)} fusion(f32[48,48,3,48]{3,0,2,1:T(8,128)S(1)} %fusion.11, f32[]{:T(128)} %bitcast), kind=kOutput, calls=%fused_computation.7 | convolution fusion | flops 95579136 | bytes 2654212 | tf_op jit(solution)/shard_map/absc,ck->absk/dot_general | solution.py:53
  47.0 1.9 %convolution_bitcast_fusion = f32[48,48,3,48]{3,1,2,0:T(8,128)S(1)} fusion(f32[48,48,3,48]{3,1,2,0:T(8,128)S(1)} %fusion.4, f32[]{:T(128)} %bitcast), kind=kOutput, calls=%fused_computation.16 | convolution fusion | flops 95579136 | bytes 2654212 | tf_op jit(solution)/shard_map/absc,kb->aksc/dot_general | solution.py:54
  48.9 0.0 copy-start.3
  48.9 3.0 %fusion.2 = f32[48,48,3,48]{3,0,2,1:T(8,128)S(1)} fusion(f32[48,48,3,48]{3,1,2,0:T(8,128)S(1)} %convolution_bitcast_fusion, f32[]{:T(128)} %bitcast), kind=kOutput, calls=%fused_computation.5 | convolution fusion | flops 95579136 | bytes 2654212 | tf_op jit(solution)/shard_map/absc,ka->kbsc/dot_general | solution.py:55
  51.9 0.0 copy-done.3
  51.9 1.5 %fusion.1 = f32[48,48,48]{2,1,0:T(8,128)S(1)} fusion(f32[48,48,3,48]{3,0,2,1:T(8,128)S(1)} %fusion.2, f32[48,48,4,48]{3,1,2,0:T(8,128)S(1)} %fusion.93, f32[3]{0:T(128)S(1)} %copy-done.3), kind=kLoop, calls=%fused_computation.4 | loop fusion | flops 884736 | bytes 3096588 | tf_op jit(solution)/shard_map/reduce_sum | solution.py:95
  53.3 1.7 %fusion.34 = (f32[448,48]{0,1:T(8,128)S(1)}, f32[448,48]{0,1:T(8,128)S(1)}) fusion(s32[448]{0:T(512)S(1)} %get-tuple-element.19, f32[2304,448]{1,0:T(8,128)S(1)} %bitcast.78, f32[2304,48]{1,0:T(8,128)S(1)} %bitcast.79), kind=kOutput, calls=%fused_computation.56 | convolution fusion | flops 297529344 | bytes 4744960 | tf_op jit(solution)/shard_map/dot_general | solution.py:96
  55.0 0.3 fusion.18
  55.3 0.1 copy.48
  55.5 0.2 reshape.235
  55.6 10.0 %all_to_all.15 = f32[8,1,1792]{2,1,0:T(1,128)S(1)} all-to-all(f32[8,1,1792]{2,1,0:T(1,128)S(1)} %reshape.235), channel_id=1, replica_groups=mesh['grp'=4,'col'=8] {'col'}, dimensions={0} | all-to-all | bytes 114688 | tf_op jit(solution)/shard_map/all_to_all | solution.py:100
  65.6 0.6 copy.75
  (8 shorter events, 0.2 us)
Async XLA Ops:
  0.0 22.5 %copy-start.2 = (s32[448]{0:T(512)S(1)}, s32[448]{0:T(512)}, u32[]{:S(2)}) copy-start(s32[448]{0:T(512)} %param.6) | copy-start | bytes 5380
  0.0 22.5 %copy-start.1 = (s32[448]{0:T(512)S(1)}, s32[448]{0:T(512)}, u32[]{:S(2)}) copy-start(s32[448]{0:T(512)} %param.7) | copy-start | bytes 5380
  3.1 8.7 %all-to-all-start = ((f32[4,3,1792]{2,1,0:T(4,128)}), f32[4,3,1792]{2,1,0:T(4,128)S(1)}, u32[]{:S(2)}, u32[]{:S(2)}) async-start(f32[4,3,1792]{2,1,0:T(4,128)} %broadcast_in_dim.36), calls=%async_computation | async-start | bytes 229376 | tf_op jit(solution)/shard_map/all_to_all | solution.py:72
  16.2 14.4 %all-to-all-start.1 = ((f32[8,4,1792]{2,1,0:T(4,128)}), f32[8,4,1792]{2,1,0:T(4,128)S(1)}, u32[]{:S(2)}, u32[]{:S(2)}) async-start(f32[8,4,1792]{2,1,0:T(4,128)} %pad_maximum_fusion), calls=%async_computation.1 | async-start | bytes 458752 | tf_op jit(solution)/shard_map/all_to_all | solution.py:76
  31.0 2.3 %copy-start = (f32[48,48,448]{2,1,0:T(8,128)S(1)}, f32[48,48,448]{2,1,0:T(8,128)}, u32[]{:S(2)}) copy-start(f32[48,48,448]{2,1,0:T(8,128)} %broadcast_multiply_fusion) | copy-start | bytes 12386308
  48.9 3.0 %copy-start.3 = (f32[3]{0:T(128)S(1)}, f32[3]{0:T(128)}, u32[]{:S(2)}) copy-start(f32[3]{0:T(128)} %param.9) | copy-start | bytes 40

commit v9 on v8

--- a/solution.py
+++ b/solution.py
@@ -74,7 +74,7 @@
             [orbitals[:, None, :], jnp.broadcast_to(picked[None], (n_grp_bands, n_src, width))], axis=1)
         send, column_cell, column_length = lax.optimization_barrier((send, column_cell, column_length))
         got = lax.all_to_all(send, "col", 0, 0, tiled=True)
-        table = cas_matrix(extent) + 0.0 * column_length[0]
+        table = cas_matrix(extent)
         kernel = kernel_grid(extent)
         cos_h, sin_h, live = shift_tables(column_length, depth, extent)
         slot = jnp.arange(depth, dtype=jnp.int32)

time: 66.8 us -> 64 us (0.958)
  local copies, waits for them, and re-layouts: 7.01 us -> 5.82 us
  waiting for transfers between devices: 6.62 us -> 5.69 us
    all_to_all x1, waiting for transfers between devices: 3.09 us -> 1.5 us  [local(): picked = jnp.sum(lax.all_to_all(spread, 'grp', 0, 0, tiled=True), axis=0)]
    slice x1 -> x0, local copies, waits for them, and re-layouts: 1.19 us -> none  [local(): table = cas_matrix(extent) + 0.0 * column_length[0]]
  transfers between devices with their start and end apart: 2 -> 2, of which waited for: 2 -> 2; matrix products, arithmetic and copies ran while one was open for 9% -> 11% of each run, Pallas kernels for 0% -> 0%
where the time goes in v9:
time: 64 us; the launch traced here: 63.4 us
  matrix products  23.3 us (36%)
  starting transfers between devices  10.5 us (16%)
  blocking collectives  10 us (16%)
  other arithmetic  7.79 us (12%)
  local copies, waits for them, and re-layouts  5.82 us (9%)
  waiting for transfers between devices  5.69 us (9%)
    all_to_all x1, blocking collectives, local(): lax.all_to_all(out.reshape(n_col, 1, width), 'col', 0, 0, tiled=True)  10 us
    all_to_all x1, starting transfers between devices, local(): got = lax.all_to_all(send, 'col', 0, 0, tiled=True)  6.31 us
    dot_general x2, matrix products, cas_three(): return jnp.einsum('absc,ka->kbsc', field, table, precision=MID)  6.12 us
    dot_general x2, matrix products, cas_three(): field = jnp.einsum('absc,ck->absk', field, table, precision=MID)  4.43 us
    all_to_all x1, starting transfers between devices, local(): picked = jnp.sum(lax.all_to_all(spread, 'grp', 0, 0, tiled=True), axis=0)  4.24 us
    all_to_all x1, waiting for transfers between devices, local(): got = lax.all_to_all(send, 'col', 0, 0, tiled=True)  4.19 us
    dot_general x1, matrix products, local(): grids = jnp.dot(w, cols.reshape(count, n * extent), precision=MID)  4.04 us
    dot_general x2, matrix products, cas_three(): field = jnp.einsum('absc,kb->aksc', field, table, precision=MID)  3.76 us
  transfers between devices with their start and end apart: 2, of which 2 were waited for; matrix products, arithmetic and copies ran while one was open for 11% of the time, Pallas kernels for 0%

profile of v9, /device:TPU:0, one launch (start us, length us, event | category | flops | bytes accessed | tf_op | source)
XLA Modules:
  0.0 63.4 jit_solution(12032760015932990981)
XLA Ops:
  0.0 0.0 copy-start.2
  0.0 0.0 copy-start.1
  0.0 0.7 %and_select_fusion.1 = s32[3]{0:T(128)S(1)} fusion(s32[3]{0:T(128)} %param.8), kind=kLoop, calls=%fused_computation.93 | loop fusion | flops 33 | bytes 24 | tf_op jit(solution)/shard_map/jit(remainder)/select_n | solution.py:68
  0.7 0.7 %fusion.58 = pred[3]{0:T(512)(128)(4,1)S(1)} fusion(s32[3]{0:T(128)} %param.8, s32[]{:T(128)S(6)} %axis_index.15), kind=kLoop, calls=%fused_computation.103 | loop fusion | flops 48 | bytes 19 | tf_op jit(solution)/shard_map/eq | solution.py:70
  1.4 1.0 %convolution_select_fusion = f32[3,1792]{1,0:T(4,128)S(1)} fusion(f32[8,1792]{1,0:T(8,128)} %param.5, pred[3]{0:T(512)(128)(4,1)S(1)} %fusion.58, s32[3]{0:T(128)S(1)} %and_select_fusion.1), kind=kOutput, calls=%fused_computation.15 | convolution fusion | flops 521496 | bytes 78863 | tf_op jit(solution)/shard_map/dot_general | solution.py:69
  2.4 0.7 %broadcast_in_dim.36 = f32[4,3,1792]{2,1,0:T(4,128)} broadcast(f32[3,1792]{1,0:T(4,128)S(1)} %convolution_select_fusion), dimensions={1,2} | broadcast | bytes 107520 | tf_op jit(solution)/shard_map/broadcast_in_dim | solution.py:71
  3.1 4.2 %all-to-all-start = ((f32[4,3,1792]{2,1,0:T(4,128)}), f32[4,3,1792]{2,1,0:T(4,128)S(1)}, u32[]{:S(2)}, u32[]{:S(2)}) async-start(f32[4,3,1792]{2,1,0:T(4,128)} %broadcast_in_dim.36), calls=%async_computation | async-start | bytes 229376 | tf_op jit(solution)/shard_map/all_to_all | solution.py:72
  7.3 0.1 add_multiply_fusion
  7.4 0.9 %broadcast_in_dim.33 = f32[8,1,1792]{2,1,0:T(1,128)S(1)} reshape(f32[8,1792]{1,0:T(8,128)} %param.5) | data formatting | bytes 114688 | tf_op jit(solution)/shard_map/broadcast_in_dim | solution.py:74
  8.3 0.1 copy.46
  8.4 0.6 gather_fusion
  9.0 0.1 broadcast_add_fusion
  9.1 0.4 fusion.17
  9.4 0.1 maximum_bitcast_fusion
  9.5 0.1 dot_general.54
  9.6 0.6 gather_fusion.1
  10.2 0.1 copy.47
  10.3 1.5 %all-to-all-done = f32[4,3,1792]{2,1,0:T(4,128)S(1)} async-done(((f32[4,3,1792]{2,1,0:T(4,128)}), f32[4,3,1792]{2,1,0:T(4,128)S(1)}, u32[]{:S(2)}, u32[]{:S(2)}) %all-to-all-start) | async-done | bytes 86048 | tf_op jit(solution)/shard_map/all_to_all | solution.py:72
  11.8 0.8 %pad_maximum_fusion = f32[8,4,1792]{2,1,0:T(4,128)} fusion(f32[8,3,1792]{2,1,0:T(4,128)S(1)} %broadcast_in_dim.37, f32[8,1,1792]{2,1,0:T(1,128)S(1)} %broadcast_in_dim.33), kind=kLoop, calls=%fused_computation.32 | loop fusion | flops 57344 | bytes 458752 | tf_op jit(solution)/shard_map/concatenate | solution.py:73
  12.6 0.8 %lt.102 = s32[8,56]{1,0:T(8,128)S(1)} reshape(s32[448]{0:T(512)} %param.7) | data formatting | bytes 3584 | tf_op jit(solution)/shard_map/lt | solution.py:39
  13.4 6.3 %all-to-all-start.1 = ((f32[8,4,1792]{2,1,0:T(4,128)}), f32[8,4,1792]{2,1,0:T(4,128)S(1)}, u32[]{:S(2)}, u32[]{:S(2)}) async-start(f32[8,4,1792]{2,1,0:T(4,128)} %pad_maximum_fusion), calls=%async_computation.1 | async-start | bytes 458752 | tf_op jit(solution)/shard_map/all_to_all | solution.py:76
  19.7 0.0 copy-done.2
  19.7 0.0 copy-done.1
  19.7 0.3 fusion.30
  20.1 0.3 fusion.31
  20.4 2.7 %broadcast_multiply_fusion = f32[48,48,448]{2,1,0:T(8,128)} fusion(f32[48,448]{1,0:T(8,128)S(1)} %fusion.31, f32[48,448]{1,0:T(8,128)S(1)} %fusion.30), kind=kLoop, calls=%fused_computation.14 | loop fusion | flops 1032192 | bytes 4300800 | tf_op jit(solution)/shard_map/mul | solution.py:49
  23.1 0.1 iota_compare_fusion
  23.2 0.4 fusion.28
  23.6 4.2 %all-to-all-done.1 = f32[8,4,1792]{2,1,0:T(4,128)S(1)} async-done(((f32[8,4,1792]{2,1,0:T(4,128)}), f32[8,4,1792]{2,1,0:T(4,128)S(1)}, u32[]{:S(2)}, u32[]{:S(2)}) %all-to-all-start.1) | async-done | bytes 229408 | tf_op jit(solution)/shard_map/all_to_all | solution.py:76
  27.9 0.3 reshape.207
  28.2 0.0 copy-start
  28.2 0.1 broadcast_select_fusion
  28.3 1.3 %fusion.35 = f32[448,4,2,48]{0,3,2,1:T(8,128)S(1)} fusion(f32[448,4,32,1]{2,0,3,1:T(8,128)S(1)} %bitcast.79, f32[2,48,32]{1,0,2:T(2,128)S(1)} %dot_general.54), kind=kOutput, calls=%fused_computation.57 | convolution fusion | flops 66060288 | bytes 929792 | tf_op jit(solution)/shard_map/dot_general | solution.py:87
  29.6 0.1 fusion.92
  29.7 0.1 fusion.19
  29.8 0.7 %copy-done = f32[48,48,448]{2,1,0:T(8,128)S(1)} copy-done((f32[48,48,448]{2,1,0:T(8,128)S(1)}, f32[48,48,448]{2,1,0:T(8,128)}, u32[]{:S(2)}) %copy-start) | copy-done | bytes 4128792
  30.5 4.0 %fusion.93 = f32[48,48,4,48]{3,1,2,0:T(8,128)S(1)} fusion(f32[48,48,448,1]{2,1,3,0:T(8,128)S(1)} %bitcast.76, f32[4,48,448,1]{2,1,0,3:T(8,128)S(1)} %bitcast.81), kind=kOutput, calls=%fused_computation.138 | convolution fusion | flops 1189085184 | bytes 6242304 | tf_op jit(solution)/shard_map/dot_general | solution.py:89
  34.6 0.1 slice_bitcast_fusion
  34.6 1.7 %fusion.8 = f32[48,48,3,48]{3,1,2,0:T(8,128)S(1)} fusion(f32[48,48,4,48]{3,1,2,0:T(8,128)S(1)} %fusion.93, f32[48,48,48]{2,1,0:T(8,128)S(1)} %slice_bitcast_fusion), kind=kOutput, calls=%fused_computation.11 | convolution fusion | flops 95908608 | bytes 6045696 | tf_op jit(solution)/shard_map/absc,ck->absk/dot_general | solution.py:53
  36.3 1.9 %convolution_bitcast_fusion.1 = f32[48,48,3,48]{3,1,2,0:T(8,128)S(1)} fusion(f32[48,48,3,48]{3,1,2,0:T(8,128)S(1)} %fusion.8), kind=kOutput, calls=%fused_computation.17 | convolution fusion | flops 95576832 | bytes 2654208 | tf_op jit(solution)/shard_map/absc,kb->aksc/dot_general | solution.py:54
  38.2 3.2 %fusion.11 = f32[48,48,3,48]{3,0,2,1:T(8,128)S(1)} fusion(f32[48,48,3,48]{3,1,2,0:T(8,128)S(1)} %convolution_bitcast_fusion.1, f32[48,48,48]{2,0,1:T(8,128)S(1)} %fusion.17), kind=kOutput, calls=%fused_computation.18 | convolution fusion | flops 95908608 | bytes 3096576 | tf_op jit(solution)/shard_map/absc,ka->kbsc/dot_general | solution.py:55
  41.4 2.7 %fusion.4 = f32[48,48,3,48]{3,1,2,0:T(8,128)S(1)} fusion(f32[48,48,3,48]{3,0,2,1:T(8,128)S(1)} %fusion.11), kind=kOutput, calls=%fused_computation.7 | convolution fusion | flops 95576832 | bytes 2654208 | tf_op jit(solution)/shard_map/absc,ck->absk/dot_general | solution.py:53
  44.1 1.9 %convolution_bitcast_fusion = f32[48,48,3,48]{3,1,2,0:T(8,128)S(1)} fusion(f32[48,48,3,48]{3,1,2,0:T(8,128)S(1)} %fusion.4), kind=kOutput, calls=%fused_computation.16 | convolution fusion | flops 95576832 | bytes 2654208 | tf_op jit(solution)/shard_map/absc,kb->aksc/dot_general | solution.py:54
  46.0 0.0 copy-start.3
  46.1 2.9 %fusion.2 = f32[48,48,3,48]{3,0,2,1:T(8,128)S(1)} fusion(f32[48,48,3,48]{3,1,2,0:T(8,128)S(1)} %convolution_bitcast_fusion), kind=kOutput, calls=%fused_computation.5 | convolution fusion | flops 95576832 | bytes 2654208 | tf_op jit(solution)/shard_map/absc,ka->kbsc/dot_general | solution.py:55
  49.0 0.0 copy-done.3
  49.0 1.5 %fusion.1 = f32[48,48,48]{2,1,0:T(8,128)S(1)} fusion(f32[48,48,3,48]{3,0,2,1:T(8,128)S(1)} %fusion.2, f32[48,48,4,48]{3,1,2,0:T(8,128)S(1)} %fusion.93, f32[3]{0:T(128)S(1)} %copy-done.3), kind=kLoop, calls=%fused_computation.4 | loop fusion | flops 884736 | bytes 3096588 | tf_op jit(solution)/shard_map/reduce_sum | solution.py:95
  50.5 1.7 %fusion.34 = (f32[448,48]{0,1:T(8,128)S(1)}, f32[448,48]{0,1:T(8,128)S(1)}) fusion(s32[448]{0:T(512)S(1)} %get-tuple-element.19, f32[2304,448]{1,0:T(8,128)S(1)} %bitcast.77, f32[2304,48]{1,0:T(8,128)S(1)} %bitcast.78), kind=kOutput, calls=%fused_computation.56 | convolution fusion | flops 297529344 | bytes 4744960 | tf_op jit(solution)/shard_map/dot_general | solution.py:96
  52.2 0.3 fusion.18
  52.5 0.1 copy.48
  52.6 0.2 reshape.232
  52.8 10.0 %all_to_all.15 = f32[8,1,1792]{2,1,0:T(1,128)S(1)} all-to-all(f32[8,1,1792]{2,1,0:T(1,128)S(1)} %reshape.232), channel_id=1, replica_groups=mesh['grp'=4,'col'=8] {'col'}, dimensions={0} | all-to-all | bytes 114688 | tf_op jit(solution)/shard_map/all_to_all | solution.py:100
  62.8 0.6 copy.75
  (8 shorter events, 0.1 us)
Async XLA Ops:
  0.0 19.7 %copy-start.2 = (s32[448]{0:T(512)S(1)}, s32[448]{0:T(512)}, u32[]{:S(2)}) copy-start(s32[448]{0:T(512)} %param.6) | copy-start | bytes 5380
  0.0 19.7 %copy-start.1 = (s32[448]{0:T(512)S(1)}, s32[448]{0:T(512)}, u32[]{:S(2)}) copy-start(s32[448]{0:T(512)} %param.7) | copy-start | bytes 5380
  3.1 8.7 %all-to-all-start = ((f32[4,3,1792]{2,1,0:T(4,128)}), f32[4,3,1792]{2,1,0:T(4,128)S(1)}, u32[]{:S(2)}, u32[]{:S(2)}) async-start(f32[4,3,1792]{2,1,0:T(4,128)} %broadcast_in_dim.36), calls=%async_computation | async-start | bytes 229376 | tf_op jit(solution)/shard_map/all_to_all | solution.py:72
  13.4 14.4 %all-to-all-start.1 = ((f32[8,4,1792]{2,1,0:T(4,128)}), f32[8,4,1792]{2,1,0:T(4,128)S(1)}, u32[]{:S(2)}, u32[]{:S(2)}) async-start(f32[8,4,1792]{2,1,0:T(4,128)} %pad_maximum_fusion), calls=%async_computation.1 | async-start | bytes 458752 | tf_op jit(solution)/shard_map/all_to_all | solution.py:76
  28.2 2.3 %copy-start = (f32[48,48,448]{2,1,0:T(8,128)S(1)}, f32[48,48,448]{2,1,0:T(8,128)}, u32[]{:S(2)}) copy-start(f32[48,48,448]{2,1,0:T(8,128)} %broadcast_multiply_fusion) | copy-start | bytes 12386308
  46.0 3.0 %copy-start.3 = (f32[3]{0:T(128)S(1)}, f32[3]{0:T(128)}, u32[]{:S(2)}) copy-start(f32[3]{0:T(128)} %param.9) | copy-start | bytes 40

commit v10 on v9

--- a/solution.py
+++ b/solution.py
@@ -64,10 +64,10 @@
         n_src = sources.shape[0]
 
         g = lax.axis_index("grp")
-        owner = sources // n_grp_bands
-        rows = (sources % n_grp_bands)[:, None] == jnp.arange(n_grp_bands, dtype=jnp.int32)[None, :]
+        owner = lax.div(sources, jnp.int32(n_grp_bands))
+        local_row = lax.rem(sources, jnp.int32(n_grp_bands))
+        rows = (local_row[:, None] == jnp.arange(n_grp_bands, dtype=jnp.int32)[None, :]) & (owner == g)[:, None]
         picked = jnp.dot(rows.astype(jnp.float32), orbitals, precision=HI)
-        picked = jnp.where((owner == g)[:, None], picked, 0.0)
         spread = jnp.broadcast_to(picked[None], (n_grp, n_src, width))
         picked = jnp.sum(lax.all_to_all(spread, "grp", 0, 0, tiled=True), axis=0)
         send = jnp.concatenate(

time: 64 us -> 64 us (level)
    select_n x1 -> x0, other arithmetic: 0.69 us -> none  [local(): sources % n_grp_bands]
    rem x0 -> x1, other arithmetic: none -> 0.69 us  [local(): local_row = lax.rem(sources, jnp.int32(n_grp_bands))]
where the time goes in v10:
time: 64 us; the launch traced here: 63.4 us
  matrix products  23.3 us (36%)
  starting transfers between devices  10.5 us (16%)
  blocking collectives  10 us (16%)
  other arithmetic  7.79 us (12%)
  local copies, waits for them, and re-layouts  5.82 us (9%)
  waiting for transfers between devices  5.69 us (9%)
    all_to_all x1, blocking collectives, local(): lax.all_to_all(out.reshape(n_col, 1, width), 'col', 0, 0, tiled=True)  10 us
    all_to_all x1, starting transfers between devices, local(): got = lax.all_to_all(send, 'col', 0, 0, tiled=True)  6.31 us
    dot_general x2, matrix products, cas_three(): return jnp.einsum('absc,ka->kbsc', field, table, precision=MID)  6.13 us
    dot_general x2, matrix products, cas_three(): field = jnp.einsum('absc,ck->absk', field, table, precision=MID)  4.43 us
    all_to_all x1, starting transfers between devices, local(): picked = jnp.sum(lax.all_to_all(spread, 'grp', 0, 0, tiled=True), axis=0)  4.24 us
    all_to_all x1, waiting for transfers between devices, local(): got = lax.all_to_all(send, 'col', 0, 0, tiled=True)  4.19 us
    dot_general x1, matrix products, local(): grids = jnp.dot(w, cols.reshape(count, n * extent), precision=MID)  4.04 us
    dot_general x2, matrix products, cas_three(): field = jnp.einsum('absc,kb->aksc', field, table, precision=MID)  3.76 us
  transfers between devices with their start and end apart: 2, of which 2 were waited for; matrix products, arithmetic and copies ran while one was open for 11% of the time, Pallas kernels for 0%

profile of v10, /device:TPU:0, one launch (start us, length us, event | category | flops | bytes accessed | tf_op | source)
XLA Modules:
  0.0 63.4 jit_solution(4197609026306261430)
XLA Ops:
  0.0 0.0 copy-start.2
  0.0 0.0 copy-start.1
  0.0 0.7 %compare_select_fusion.2 = s32[3]{0:T(128)S(1)} fusion(s32[3]{0:T(128)} %param.8), kind=kLoop, calls=%fused_computation.96 | loop fusion | flops 18 | bytes 24 | tf_op jit(solution)/shard_map/rem | solution.py:68
  0.7 0.7 %fusion.62 = pred[3]{0:T(512)(128)(4,1)S(1)} fusion(s32[3]{0:T(128)} %param.8, s32[]{:T(128)S(6)} %axis_index.15), kind=kLoop, calls=%fused_computation.103 | loop fusion | flops 21 | bytes 19 | tf_op jit(solution)/shard_map/eq | solution.py:69
  1.4 1.0 %fusion.54 = f32[3,1792]{1,0:T(4,128)S(1)} fusion(f32[8,1792]{1,0:T(8,128)} %param.5, s32[3]{0:T(128)S(1)} %compare_select_fusion.2, pred[3]{0:T(512)(128)(4,1)S(1)} %fusion.62), kind=kOutput, calls=%fused_computation.90 | convolution fusion | flops 516144 | bytes 78863 | tf_op jit(solution)/shard_map/dot_general | solution.py:70
  2.4 0.7 %broadcast_in_dim.22 = f32[4,3,1792]{2,1,0:T(4,128)} broadcast(f32[3,1792]{1,0:T(4,128)S(1)} %fusion.54), dimensions={1,2} | broadcast | bytes 107520 | tf_op jit(solution)/shard_map/broadcast_in_dim | solution.py:71
  3.1 4.2 %all-to-all-start = ((f32[4,3,1792]{2,1,0:T(4,128)}), f32[4,3,1792]{2,1,0:T(4,128)S(1)}, u32[]{:S(2)}, u32[]{:S(2)}) async-start(f32[4,3,1792]{2,1,0:T(4,128)} %broadcast_in_dim.22), calls=%async_computation | async-start | bytes 229376 | tf_op jit(solution)/shard_map/all_to_all | solution.py:72
  7.3 0.1 add_multiply_fusion
  7.4 0.9 %broadcast_in_dim.21 = f32[8,1,1792]{2,1,0:T(1,128)S(1)} reshape(f32[8,1792]{1,0:T(8,128)} %param.5) | data formatting | bytes 114688 | tf_op jit(solution)/shard_map/broadcast_in_dim | solution.py:74
  8.3 0.1 copy.46
  8.4 0.6 gather_fusion
  9.0 0.1 broadcast_add_fusion
  9.0 0.4 fusion.17
  9.4 0.1 maximum_bitcast_fusion
  9.5 0.1 dot_general.54
  9.6 0.6 gather_fusion.1
  10.2 0.1 copy.47
  10.3 1.5 %all-to-all-done = f32[4,3,1792]{2,1,0:T(4,128)S(1)} async-done(((f32[4,3,1792]{2,1,0:T(4,128)}), f32[4,3,1792]{2,1,0:T(4,128)S(1)}, u32[]{:S(2)}, u32[]{:S(2)}) %all-to-all-start) | async-done | bytes 86048 | tf_op jit(solution)/shard_map/all_to_all | solution.py:72
  11.8 0.8 %pad_maximum_fusion = f32[8,4,1792]{2,1,0:T(4,128)} fusion(f32[8,3,1792]{2,1,0:T(4,128)S(1)} %broadcast_in_dim.23, f32[8,1,1792]{2,1,0:T(1,128)S(1)} %broadcast_in_dim.21), kind=kLoop, calls=%fused_computation.31 | loop fusion | flops 57344 | bytes 458752 | tf_op jit(solution)/shard_map/concatenate | solution.py:73
  12.6 0.8 %lt.95 = s32[8,56]{1,0:T(8,128)S(1)} reshape(s32[448]{0:T(512)} %param.7) | data formatting | bytes 3584 | tf_op jit(solution)/shard_map/lt | solution.py:39
  13.4 6.3 %all-to-all-start.1 = ((f32[8,4,1792]{2,1,0:T(4,128)}), f32[8,4,1792]{2,1,0:T(4,128)S(1)}, u32[]{:S(2)}, u32[]{:S(2)}) async-start(f32[8,4,1792]{2,1,0:T(4,128)} %pad_maximum_fusion), calls=%async_computation.1 | async-start | bytes 458752 | tf_op jit(solution)/shard_map/all_to_all | solution.py:76
  19.7 0.0 copy-done.2
  19.7 0.0 copy-done.1
  19.7 0.3 fusion.30
  20.0 0.3 fusion.31
  20.3 2.7 %broadcast_multiply_fusion = f32[48,48,448]{2,1,0:T(8,128)} fusion(f32[48,448]{1,0:T(8,128)S(1)} %fusion.31, f32[48,448]{1,0:T(8,128)S(1)} %fusion.30), kind=kLoop, calls=%fused_computation.14 | loop fusion | flops 1032192 | bytes 4300800 | tf_op jit(solution)/shard_map/mul | solution.py:49
  23.1 0.1 iota_compare_fusion
  23.2 0.4 fusion.28
  23.6 4.2 %all-to-all-done.1 = f32[8,4,1792]{2,1,0:T(4,128)S(1)} async-done(((f32[8,4,1792]{2,1,0:T(4,128)}), f32[8,4,1792]{2,1,0:T(4,128)S(1)}, u32[]{:S(2)}, u32[]{:S(2)}) %all-to-all-start.1) | async-done | bytes 229408 | tf_op jit(solution)/shard_map/all_to_all | solution.py:76
  27.9 0.3 reshape.207
  28.2 0.0 copy-start
  28.2 0.1 broadcast_select_fusion
  28.3 1.4 %fusion.35 = f32[448,4,2,48]{0,3,2,1:T(8,128)S(1)} fusion(f32[448,4,32,1]{2,0,3,1:T(8,128)S(1)} %bitcast.79, f32[2,48,32]{1,0,2:T(2,128)S(1)} %dot_general.54), kind=kOutput, calls=%fused_computation.56 | convolution fusion | flops 66060288 | bytes 929792 | tf_op jit(solution)/shard_map/dot_general | solution.py:87
  29.6 0.1 fusion.96
  29.7 0.1 fusion.19
  29.8 0.7 %copy-done = f32[48,48,448]{2,1,0:T(8,128)S(1)} copy-done((f32[48,48,448]{2,1,0:T(8,128)S(1)}, f32[48,48,448]{2,1,0:T(8,128)}, u32[]{:S(2)}) %copy-start) | copy-done | bytes 4128792
  30.5 4.0 %fusion.97 = f32[48,48,4,48]{3,1,2,0:T(8,128)S(1)} fusion(f32[48,48,448,1]{2,1,3,0:T(8,128)S(1)} %bitcast.76, f32[4,48,448,1]{2,1,0,3:T(8,128)S(1)} %bitcast.81), kind=kOutput, calls=%fused_computation.138 | convolution fusion | flops 1189085184 | bytes 6242304 | tf_op jit(solution)/shard_map/dot_general | solution.py:89
  34.5 0.1 slice_bitcast_fusion
  34.6 1.7 %fusion.8 = f32[48,48,3,48]{3,1,2,0:T(8,128)S(1)} fusion(f32[48,48,4,48]{3,1,2,0:T(8,128)S(1)} %fusion.97, f32[48,48,48]{2,1,0:T(8,128)S(1)} %slice_bitcast_fusion), kind=kOutput, calls=%fused_computation.11 | convolution fusion | flops 95908608 | bytes 6045696 | tf_op jit(solution)/shard_map/absc,ck->absk/dot_general | solution.py:53
  36.3 1.9 %convolution_bitcast_fusion.1 = f32[48,48,3,48]{3,1,2,0:T(8,128)S(1)} fusion(f32[48,48,3,48]{3,1,2,0:T(8,128)S(1)} %fusion.8), kind=kOutput, calls=%fused_computation.16 | convolution fusion | flops 95576832 | bytes 2654208 | tf_op jit(solution)/shard_map/absc,kb->aksc/dot_general | solution.py:54
  38.2 3.2 %fusion.11 = f32[48,48,3,48]{3,0,2,1:T(8,128)S(1)} fusion(f32[48,48,3,48]{3,1,2,0:T(8,128)S(1)} %convolution_bitcast_fusion.1, f32[48,48,48]{2,0,1:T(8,128)S(1)} %fusion.17), kind=kOutput, calls=%fused_computation.17 | convolution fusion | flops 95908608 | bytes 3096576 | tf_op jit(solution)/shard_map/absc,ka->kbsc/dot_general | solution.py:55
  41.4 2.7 %fusion.4 = f32[48,48,3,48]{3,1,2,0:T(8,128)S(1)} fusion(f32[48,48,3,48]{3,0,2,1:T(8,128)S(1)} %fusion.11), kind=kOutput, calls=%fused_computation.7 | convolution fusion | flops 95576832 | bytes 2654208 | tf_op jit(solution)/shard_map/absc,ck->absk/dot_general | solution.py:53
  44.1 1.9 %convolution_bitcast_fusion = f32[48,48,3,48]{3,1,2,0:T(8,128)S(1)} fusion(f32[48,48,3,48]{3,1,2,0:T(8,128)S(1)} %fusion.4), kind=kOutput, calls=%fused_computation.15 | convolution fusion | flops 95576832 | bytes 2654208 | tf_op jit(solution)/shard_map/absc,kb->aksc/dot_general | solution.py:54
  46.0 0.0 copy-start.3
  46.1 2.9 %fusion.2 = f32[48,48,3,48]{3,0,2,1:T(8,128)S(1)} fusion(f32[48,48,3,48]{3,1,2,0:T(8,128)S(1)} %convolution_bitcast_fusion), kind=kOutput, calls=%fused_computation.5 | convolution fusion | flops 95576832 | bytes 2654208 | tf_op jit(solution)/shard_map/absc,ka->kbsc/dot_general | solution.py:55
  49.0 0.0 copy-done.3
  49.0 1.5 %fusion.1 = f32[48,48,48]{2,1,0:T(8,128)S(1)} fusion(f32[48,48,3,48]{3,0,2,1:T(8,128)S(1)} %fusion.2, f32[48,48,4,48]{3,1,2,0:T(8,128)S(1)} %fusion.97, f32[3]{0:T(128)S(1)} %copy-done.3), kind=kLoop, calls=%fused_computation.4 | loop fusion | flops 884736 | bytes 3096588 | tf_op jit(solution)/shard_map/reduce_sum | solution.py:95
  50.5 1.7 %fusion.34 = (f32[448,48]{0,1:T(8,128)S(1)}, f32[448,48]{0,1:T(8,128)S(1)}) fusion(s32[448]{0:T(512)S(1)} %get-tuple-element.19, f32[2304,448]{1,0:T(8,128)S(1)} %bitcast.77, f32[2304,48]{1,0:T(8,128)S(1)} %bitcast.78), kind=kOutput, calls=%fused_computation.55 | convolution fusion | flops 297529344 | bytes 4744960 | tf_op jit(solution)/shard_map/dot_general | solution.py:96
  52.2 0.3 fusion.18
  52.5 0.1 copy.48
  52.6 0.2 reshape.232
  52.8 10.0 %all_to_all.15 = f32[8,1,1792]{2,1,0:T(1,128)S(1)} all-to-all(f32[8,1,1792]{2,1,0:T(1,128)S(1)} %reshape.232), channel_id=1, replica_groups=mesh['grp'=4,'col'=8] {'col'}, dimensions={0} | all-to-all | bytes 114688 | tf_op jit(solution)/shard_map/all_to_all | solution.py:100
  62.8 0.6 copy.75
  (8 shorter events, 0.1 us)
Async XLA Ops:
  0.0 19.7 %copy-start.2 = (s32[448]{0:T(512)S(1)}, s32[448]{0:T(512)}, u32[]{:S(2)}) copy-start(s32[448]{0:T(512)} %param.6) | copy-start | bytes 5380
  0.0 19.7 %copy-start.1 = (s32[448]{0:T(512)S(1)}, s32[448]{0:T(512)}, u32[]{:S(2)}) copy-start(s32[448]{0:T(512)} %param.7) | copy-start | bytes 5380
  3.1 8.7 %all-to-all-start = ((f32[4,3,1792]{2,1,0:T(4,128)}), f32[4,3,1792]{2,1,0:T(4,128)S(1)}, u32[]{:S(2)}, u32[]{:S(2)}) async-start(f32[4,3,1792]{2,1,0:T(4,128)} %broadcast_in_dim.22), calls=%async_computation | async-start | bytes 229376 | tf_op jit(solution)/shard_map/all_to_all | solution.py:72
  13.4 14.4 %all-to-all-start.1 = ((f32[8,4,1792]{2,1,0:T(4,128)}), f32[8,4,1792]{2,1,0:T(4,128)S(1)}, u32[]{:S(2)}, u32[]{:S(2)}) async-start(f32[8,4,1792]{2,1,0:T(4,128)} %pad_maximum_fusion), calls=%async_computation.1 | async-start | bytes 458752 | tf_op jit(solution)/shard_map/all_to_all | solution.py:76
  28.2 2.3 %copy-start = (f32[48,48,448]{2,1,0:T(8,128)S(1)}, f32[48,48,448]{2,1,0:T(8,128)}, u32[]{:S(2)}) copy-start(f32[48,48,448]{2,1,0:T(8,128)} %broadcast_multiply_fusion) | copy-start | bytes 12386308
  46.0 3.0 %copy-start.3 = (f32[3]{0:T(128)S(1)}, f32[3]{0:T(128)}, u32[]{:S(2)}) copy-start(f32[3]{0:T(128)} %param.9) | copy-start | bytes 40

commit v11 on v9

--- a/solution.py
+++ b/solution.py
@@ -72,6 +72,10 @@
         picked = jnp.sum(lax.all_to_all(spread, "grp", 0, 0, tiled=True), axis=0)
         send = jnp.concatenate(
             [orbitals[:, None, :], jnp.broadcast_to(picked[None], (n_grp_bands, n_src, width))], axis=1)
+        per_dev = count // n_col
+        mine = lax.dynamic_slice_in_dim(column_length, lax.axis_index("col") * per_dev, per_dev)
+        live_mine = (jnp.arange(depth, dtype=jnp.int32)[None, :] < mine[:, None]).reshape(-1)
+        send = jnp.where(live_mine[None, None, :], send, 0.0)
         send, column_cell, column_length = lax.optimization_barrier((send, column_cell, column_length))
         got = lax.all_to_all(send, "col", 0, 0, tiled=True)
         table = cas_matrix(extent)
@@ -83,7 +87,6 @@
         w = lax.optimization_barrier(plane_matrix(column_cell, table, extent))
         n = 1 + n_src
         coeff = got.reshape(n_col, n, width // depth, depth).transpose(0, 2, 1, 3).reshape(count, n, depth)
-        coeff = jnp.where(live[:, None, :], coeff, 0.0)
         both = jnp.dot(coeff.reshape(count * n, depth), fwd, precision=HI).reshape(count, n, 2, extent)
         cols = cos_h[:, None, :] * both[:, :, 0] - sin_h[:, None, :] * both[:, :, 1]
         grids = jnp.dot(w, cols.reshape(count, n * extent), precision=MID)
@@ -97,7 +100,7 @@
         scaled = jnp.concatenate([back * cos_h, -(back * sin_h)], axis=1)
         out = -jnp.dot(scaled, bwd, precision=HI)
         out = jnp.where(live, out, 0.0)
-        return lax.all_to_all(out.reshape(n_col, 1, width), "col", 0, 0, tiled=True).reshape(n_col, width)
+        return lax.all_to_all(out.reshape(n_col, width), "col", 0, 0, tiled=True)
 
     return local
 

time: 64 us -> 65 us (1.016)
  matrix products: 23.3 us -> 25.5 us
    dot_general x1, matrix products: 4.04 us -> 6.15 us  [local(): grids = jnp.dot(w, cols.reshape(count, n * extent), precision=MID)]
    all_to_all x1, waiting for transfers between devices: 1.5 us -> 0.57 us  [local(): picked = jnp.sum(lax.all_to_all(spread, 'grp', 0, 0, tiled=True), axis=0)]
    concatenate x1 -> x0, other arithmetic: 0.82 us -> none  [local(): jnp.concatenate([orbitals[:, None, :], jnp.broadcast_to(picked[None], (n_...]
    dynamic_slice x0 -> x1, local copies, waits for them, and re-layouts: none -> 0.76 us  [local(): lax.dynamic_slice_in_dim(column_length, lax.axis_index('col') * per_dev,...]
    select_n x1, other arithmetic: 0.07 us -> 0.83 us  [local(): send = jnp.where(live_mine[None, None, :], send, 0.0)]
    unnamed x9 -> x11, local copies, waits for them, and re-layouts: 1.36 us -> 0.65 us
    lt x1, local copies, waits for them, and re-layouts: 0.76 us -> 0.09 us  [local(): jnp.arange(depth, dtype=jnp.int32)[None, :] < mine[:, None]]
  transfers between devices with their start and end apart: 2 -> 2, of which waited for: 2 -> 2; matrix products, arithmetic and copies ran while one was open for 11% -> 12% of each run, Pallas kernels for 0% -> 0%
where the time goes in v11:
time: 65 us; the launch traced here: 64.5 us
  matrix products  25.5 us (39%)
  starting transfers between devices  10.5 us (16%)
  blocking collectives  10 us (15%)
  other arithmetic  7.7 us (12%)
  waiting for transfers between devices  5.33 us (8%)
  local copies, waits for them, and re-layouts  5.18 us (8%)
    all_to_all x1, blocking collectives, local(): return lax.all_to_all(out.reshape(n_col, width), 'col', 0, 0, tiled=True)  10 us
    all_to_all x1, starting transfers between devices, local(): got = lax.all_to_all(send, 'col', 0, 0, tiled=True)  6.3 us
    dot_general x2, matrix products, cas_three(): return jnp.einsum('absc,ka->kbsc', field, table, precision=MID)  6.16 us
    dot_general x1, matrix products, local(): grids = jnp.dot(w, cols.reshape(count, n * extent), precision=MID)  6.15 us
    all_to_all x1, waiting for transfers between devices, local(): got = lax.all_to_all(send, 'col', 0, 0, tiled=True)  4.76 us
    dot_general x2, matrix products, cas_three(): field = jnp.einsum('absc,ck->absk', field, table, precision=MID)  4.42 us
    all_to_all x1, starting transfers between devices, local(): picked = jnp.sum(lax.all_to_all(spread, 'grp', 0, 0, tiled=True), axis=0)  4.24 us
    dot_general x2, matrix products, cas_three(): field = jnp.einsum('absc,kb->aksc', field, table, precision=MID)  3.76 us
  transfers between devices with their start and end apart: 2, of which 2 were waited for; matrix products, arithmetic and copies ran while one was open for 12% of the time, Pallas kernels for 0%

profile of v11, /device:TPU:0, one launch (start us, length us, event | category | flops | bytes accessed | tf_op | source)
XLA Modules:
  0.0 64.5 jit_solution(14623404684938024968)
XLA Ops:
  0.0 0.0 copy-start
  0.0 0.0 copy-start.1
  0.0 0.7 %and_select_fusion.1 = s32[3]{0:T(128)S(1)} fusion(s32[3]{0:T(128)} %param.8), kind=kLoop, calls=%fused_computation.92 | loop fusion | flops 33 | bytes 24 | tf_op jit(solution)/shard_map/jit(remainder)/select_n | solution.py:68
  0.7 0.7 %fusion.58 = pred[3]{0:T(512)(128)(4,1)S(1)} fusion(s32[3]{0:T(128)} %param.8, s32[]{:T(128)S(6)} %axis_index.25), kind=kLoop, calls=%fused_computation.102 | loop fusion | flops 48 | bytes 19 | tf_op jit(solution)/shard_map/eq | solution.py:70
  1.4 1.0 %convolution_select_fusion = f32[3,1792]{1,0:T(4,128)S(1)} fusion(f32[8,1792]{1,0:T(8,128)} %param.5, pred[3]{0:T(512)(128)(4,1)S(1)} %fusion.58, s32[3]{0:T(128)S(1)} %and_select_fusion.1), kind=kOutput, calls=%fused_computation.15 | convolution fusion | flops 521496 | bytes 78863 | tf_op jit(solution)/shard_map/dot_general | solution.py:69
  2.4 0.7 %broadcast_in_dim.41 = f32[4,3,1792]{2,1,0:T(4,128)} broadcast(f32[3,1792]{1,0:T(4,128)S(1)} %convolution_select_fusion), dimensions={1,2} | broadcast | bytes 107520 | tf_op jit(solution)/shard_map/broadcast_in_dim | solution.py:71
  3.1 4.2 %all-to-all-start = ((f32[4,3,1792]{2,1,0:T(4,128)}), f32[4,3,1792]{2,1,0:T(4,128)S(1)}, u32[]{:S(2)}, u32[]{:S(2)}) async-start(f32[4,3,1792]{2,1,0:T(4,128)} %broadcast_in_dim.41), calls=%async_computation | async-start | bytes 229376 | tf_op jit(solution)/shard_map/all_to_all | solution.py:72
  7.3 0.9 %broadcast_in_dim.38 = f32[8,1,1792]{2,1,0:T(1,128)S(1)} reshape(f32[8,1792]{1,0:T(8,128)} %param.5) | data formatting | bytes 114688 | tf_op jit(solution)/shard_map/broadcast_in_dim | solution.py:74
  8.2 0.1 add_multiply_fusion
  8.3 0.1 copy.46
  8.4 0.8 %dynamic_slice.3 = s32[56]{0:T(128)S(1)} dynamic-slice(s32[448]{0:T(512)} %param.7, s32[]{:T(128)S(6)} %select_n.124), dynamic_slice_sizes={56} | dynamic-slice | bytes 452 | tf_op jit(solution)/shard_map/dynamic_slice | solution.py:76
  9.2 0.1 iota_compare_fusion.5
  9.2 0.1 lt.110
  9.3 0.6 gather_fusion
  9.9 0.1 broadcast_add_fusion
  10.0 0.4 fusion.17
  10.4 0.1 maximum_bitcast_fusion
  10.5 0.1 dot_general.57
  10.5 0.6 gather_fusion.1
  11.1 0.1 copy.47
  11.2 0.6 all-to-all-done
  11.8 0.8 %maximum_select_fusion = f32[8,4,1792]{2,1,0:T(4,128)} fusion(f32[8,3,1792]{2,1,0:T(4,128)S(1)} %broadcast_in_dim.42, f32[8,1,1792]{2,1,0:T(1,128)S(1)} %broadcast_in_dim.38, pred[1792]{0:T(1024)(128)(4,1)S(1)} %lt.110), kind=kLoop, calls=%fused_computation.31 | loop fusion | flops 114688 | bytes 460544 | tf_op jit(solution)/shard_map/jit(_where)/select_n | solution.py:78
  12.7 6.3 %all-to-all-start.1 = ((f32[8,4,1792]{2,1,0:T(4,128)}), f32[8,4,1792]{2,1,0:T(4,128)S(1)}, u32[]{:S(2)}, u32[]{:S(2)}) async-start(f32[8,4,1792]{2,1,0:T(4,128)} %maximum_select_fusion), calls=%async_computation.1 | async-start | bytes 458752 | tf_op jit(solution)/shard_map/all_to_all | solution.py:80
  19.0 0.0 copy-done
  19.0 0.0 copy-done.1
  19.0 0.3 fusion.30
  19.3 0.3 fusion.31
  19.6 2.7 %broadcast_multiply_fusion = f32[48,48,448]{2,1,0:T(8,128)} fusion(f32[48,448]{1,0:T(8,128)S(1)} %fusion.31, f32[48,448]{1,0:T(8,128)S(1)} %fusion.30), kind=kLoop, calls=%fused_computation.14 | loop fusion | flops 1032192 | bytes 4300800 | tf_op jit(solution)/shard_map/mul | solution.py:49
  22.3 0.4 fusion.28
  22.8 4.8 %all-to-all-done.1 = f32[8,4,1792]{2,1,0:T(4,128)S(1)} async-done(((f32[8,4,1792]{2,1,0:T(4,128)}), f32[8,4,1792]{2,1,0:T(4,128)S(1)}, u32[]{:S(2)}, u32[]{:S(2)}) %all-to-all-start.1) | async-done | bytes 229408 | tf_op jit(solution)/shard_map/all_to_all | solution.py:80
  27.6 0.3 reshape.198
  27.9 1.3 %fusion.35 = f32[448,4,2,48]{0,3,2,1:T(8,128)S(1)} fusion(f32[448,4,32,1]{2,0,3,1:T(8,128)S(1)} %bitcast.81, f32[2,48,32]{1,0,2:T(2,128)S(1)} %dot_general.57), kind=kOutput, calls=%fused_computation.55 | convolution fusion | flops 66060288 | bytes 929792 | tf_op jit(solution)/shard_map/dot_general | solution.py:90
  29.2 0.1 fusion.92
  29.3 0.1 fusion.19
  29.4 6.2 %fusion.93 = f32[48,48,4,48]{3,1,2,0:T(8,128)S(1)} fusion(f32[48,48,448,1]{2,1,3,0:T(8,128)} %bitcast.76, f32[4,48,448,1]{2,1,0,3:T(8,128)S(1)} %bitcast.83), kind=kOutput, calls=%fused_computation.137 | convolution fusion | flops 1189085184 | bytes 6242304 | tf_op jit(solution)/shard_map/dot_general | solution.py:92
  35.5 0.1 slice_bitcast_fusion
  35.6 1.7 %fusion.8 = f32[48,48,3,48]{3,1,2,0:T(8,128)S(1)} fusion(f32[48,48,4,48]{3,1,2,0:T(8,128)S(1)} %fusion.93, f32[48,48,48]{2,1,0:T(8,128)S(1)} %slice_bitcast_fusion), kind=kOutput, calls=%fused_computation.11 | convolution fusion | flops 95908608 | bytes 6045696 | tf_op jit(solution)/shard_map/absc,ck->absk/dot_general | solution.py:53
  37.3 1.9 %convolution_bitcast_fusion.1 = f32[48,48,3,48]{3,1,2,0:T(8,128)S(1)} fusion(f32[48,48,3,48]{3,1,2,0:T(8,128)S(1)} %fusion.8), kind=kOutput, calls=%fused_computation.17 | convolution fusion | flops 95576832 | bytes 2654208 | tf_op jit(solution)/shard_map/absc,kb->aksc/dot_general | solution.py:54
  39.2 3.0 %fusion.11 = f32[48,48,3,48]{3,0,2,1:T(8,128)S(1)} fusion(f32[48,48,3,48]{3,1,2,0:T(8,128)S(1)} %convolution_bitcast_fusion.1, f32[48,48,48]{2,0,1:T(8,128)S(1)} %fusion.17), kind=kOutput, calls=%fused_computation.18 | convolution fusion | flops 95908608 | bytes 3096576 | tf_op jit(solution)/shard_map/absc,ka->kbsc/dot_general | solution.py:55
  42.2 2.7 %fusion.4 = f32[48,48,3,48]{3,1,2,0:T(8,128)S(1)} fusion(f32[48,48,3,48]{3,0,2,1:T(8,128)S(1)} %fusion.11), kind=kOutput, calls=%fused_computation.7 | convolution fusion | flops 95576832 | bytes 2654208 | tf_op jit(solution)/shard_map/absc,ck->absk/dot_general | solution.py:53
  45.0 1.9 %convolution_bitcast_fusion = f32[48,48,3,48]{3,1,2,0:T(8,128)S(1)} fusion(f32[48,48,3,48]{3,1,2,0:T(8,128)S(1)} %fusion.4), kind=kOutput, calls=%fused_computation.16 | convolution fusion | flops 95576832 | bytes 2654208 | tf_op jit(solution)/shard_map/absc,kb->aksc/dot_general | solution.py:54
  46.9 0.0 copy-start.2
  46.9 0.0 slice-start
  46.9 3.2 %fusion.2 = f32[48,48,3,48]{3,0,2,1:T(8,128)S(1)} fusion(f32[48,48,3,48]{3,1,2,0:T(8,128)S(1)} %convolution_bitcast_fusion), kind=kOutput, calls=%fused_computation.5 | convolution fusion | flops 95576832 | bytes 2654208 | tf_op jit(solution)/shard_map/absc,ka->kbsc/dot_general | solution.py:55
  50.0 0.0 copy-done.2
  50.0 0.0 slice-start.1
  50.1 1.5 %fusion.1 = f32[48,48,48]{2,1,0:T(8,128)S(1)} fusion(f32[48,48,3,48]{3,0,2,1:T(8,128)S(1)} %fusion.2, f32[48,48,4,48]{3,1,2,0:T(8,128)S(1)} %fusion.93, f32[3]{0:T(128)S(1)} %copy-done.2), kind=kLoop, calls=%fused_computation.4 | loop fusion | flops 884736 | bytes 3096588 | tf_op jit(solution)/shard_map/reduce_sum | solution.py:98
  51.5 0.0 slice-done
  51.5 0.0 slice-done.1
  51.6 1.7 %fusion.34 = (f32[448,48]{0,1:T(8,128)S(1)}, f32[448,48]{0,1:T(8,128)S(1)}) fusion(s32[448]{0:T(512)S(1)} %get-tuple-element.19, f32[2304,448]{1,0:T(8,128)S(1)} %bitcast.79, f32[2304,48]{1,0:T(8,128)S(1)} %bitcast.80), kind=kOutput, calls=%fused_computation.54 | convolution fusion | flops 297529344 | bytes 4744960 | tf_op jit(solution)/shard_map/dot_general | solution.py:99
  53.3 0.3 fusion.18
  53.6 0.1 copy.48
  53.7 0.2 all_to_all.19
  53.8 10.0 %all_to_all.23 = f32[8,1,1792]{2,1,0:T(1,128)S(1)} all-to-all(f32[8,1,1792]{2,1,0:T(1,128)S(1)} %all_to_all.19), channel_id=1, replica_groups=mesh['grp'=4,'col'=8] {'col'}, dimensions={0} | all-to-all | bytes 114688 | tf_op jit(solution)/shard_map/all_to_all | solution.py:103
  63.9 0.6 copy.76
  (9 shorter events, 0.2 us)
Async XLA Ops:
  0.0 19.0 %copy-start = (s32[448]{0:T(512)S(1)}, s32[448]{0:T(512)}, u32[]{:S(2)}) copy-start(s32[448]{0:T(512)} %param.7) | copy-start | bytes 5380
  0.0 19.0 %copy-start.1 = (s32[448]{0:T(512)S(1)}, s32[448]{0:T(512)}, u32[]{:S(2)}) copy-start(s32[448]{0:T(512)} %param.6) | copy-start | bytes 5380
  3.1 8.7 %all-to-all-start = ((f32[4,3,1792]{2,1,0:T(4,128)}), f32[4,3,1792]{2,1,0:T(4,128)S(1)}, u32[]{:S(2)}, u32[]{:S(2)}) async-start(f32[4,3,1792]{2,1,0:T(4,128)} %broadcast_in_dim.41), calls=%async_computation | async-start | bytes 229376 | tf_op jit(solution)/shard_map/all_to_all | solution.py:72
  12.7 14.9 %all-to-all-start.1 = ((f32[8,4,1792]{2,1,0:T(4,128)}), f32[8,4,1792]{2,1,0:T(4,128)S(1)}, u32[]{:S(2)}, u32[]{:S(2)}) async-start(f32[8,4,1792]{2,1,0:T(4,128)} %maximum_select_fusion), calls=%async_computation.1 | async-start | bytes 458752 | tf_op jit(solution)/shard_map/all_to_all | solution.py:80
  46.9 3.2 %copy-start.2 = (f32[3]{0:T(128)S(1)}, f32[3]{0:T(128)}, u32[]{:S(2)}) copy-start(f32[3]{0:T(128)} %param.9) | copy-start | bytes 40
  46.9 4.7 %slice-start = ((s8[4718592]{0:T(1024)(128)(4,1)}), s8[4194304]{0:T(1024)(128)(4,1)S(1)}, s32[]{:S(2)}) async-start(s8[4718592]{0:T(1024)(128)(4,1)} %bitcast.77), calls=%async_computation.3 | async-start | bytes 8388608
  50.0 1.5 %slice-start.1 = ((s8[4718592]{0:T(1024)(128)(4,1)}), s8[524288]{0:T(1024)(128)(4,1)S(1)}, s32[]{:S(2)}) async-start(s8[4718592]{0:T(1024)(128)(4,1)} %bitcast.77), calls=%async_computation.4 | async-start | bytes 1048576

commit v12 on v10

--- a/solution.py
+++ b/solution.py
@@ -63,13 +63,10 @@
         depth = width * n_col // count
         n_src = sources.shape[0]
 
-        g = lax.axis_index("grp")
-        owner = lax.div(sources, jnp.int32(n_grp_bands))
-        local_row = lax.rem(sources, jnp.int32(n_grp_bands))
-        rows = (local_row[:, None] == jnp.arange(n_grp_bands, dtype=jnp.int32)[None, :]) & (owner == g)[:, None]
-        picked = jnp.dot(rows.astype(jnp.float32), orbitals, precision=HI)
-        spread = jnp.broadcast_to(picked[None], (n_grp, n_src, width))
-        picked = jnp.sum(lax.all_to_all(spread, "grp", 0, 0, tiled=True), axis=0)
+        everyone = lax.all_to_all(jnp.broadcast_to(orbitals[None], (n_grp,) + orbitals.shape), "grp", 0, 0, tiled=True)
+        everyone = everyone.reshape(n_grp * n_grp_bands, width)
+        rows = sources[:, None] == jnp.arange(n_grp * n_grp_bands, dtype=jnp.int32)[None, :]
+        picked = jnp.dot(rows.astype(jnp.float32), everyone, precision=HI)
         send = jnp.concatenate(
             [orbitals[:, None, :], jnp.broadcast_to(picked[None], (n_grp_bands, n_src, width))], axis=1)
         send, column_cell, column_length = lax.optimization_barrier((send, column_cell, column_length))

time: 64 us -> 64 us (level)
  other arithmetic: 7.79 us -> 6.41 us
  waiting for transfers between devices: 5.69 us -> 7.04 us
    all_to_all x1, waiting for transfers between devices: 1.5 us -> 2.72 us  [local(): lax.all_to_all(jnp.broadcast_to(orbitals[None], (n_grp,) + orbitals.shape...]
    broadcast_in_dim x1, local copies, waits for them, and re-layouts: 0.66 us -> 1.55 us  [local(): jnp.broadcast_to(orbitals[None], (n_grp,) + orbitals.shape)]
    rem x1 -> x0, other arithmetic: 0.69 us -> none  [local(): local_row = lax.rem(sources, jnp.int32(n_grp_bands))]
    lt x1, local copies, waits for them, and re-layouts: 0.76 us -> 0.08 us  [shift_tables(): live = slot[None, :] < column_length[:, None]]
    eq x1 -> x0, other arithmetic: 0.66 us -> none  [local(): owner == g]
where the time goes in v12:
time: 64 us; the launch traced here: 63.5 us
  matrix products  23.1 us (36%)
  starting transfers between devices  10.6 us (17%)
  blocking collectives  10 us (16%)
  waiting for transfers between devices  7.04 us (11%)
  other arithmetic  6.41 us (10%)
  local copies, waits for them, and re-layouts  6.03 us (9%)
    all_to_all x1, blocking collectives, local(): lax.all_to_all(out.reshape(n_col, 1, width), 'col', 0, 0, tiled=True)  10 us
    all_to_all x1, starting transfers between devices, local(): got = lax.all_to_all(send, 'col', 0, 0, tiled=True)  6.38 us
    dot_general x2, matrix products, cas_three(): return jnp.einsum('absc,ka->kbsc', field, table, precision=MID)  6.12 us
    dot_general x2, matrix products, cas_three(): field = jnp.einsum('absc,ck->absk', field, table, precision=MID)  4.42 us
    all_to_all x1, waiting for transfers between devices, local(): got = lax.all_to_all(send, 'col', 0, 0, tiled=True)  4.32 us
    all_to_all x1, starting transfers between devices, local(): lax.all_to_all(jnp.broadcast_to(orbitals[None], (n_grp,) + orbitals.shape...  4.24 us
    dot_general x1, matrix products, local(): grids = jnp.dot(w, cols.reshape(count, n * extent), precision=MID)  4.04 us
    dot_general x2, matrix products, cas_three(): field = jnp.einsum('absc,kb->aksc', field, table, precision=MID)  3.76 us
  transfers between devices with their start and end apart: 2, of which 2 were waited for; matrix products, arithmetic and copies ran while one was open for 11% of the time, Pallas kernels for 0%

profile of v12, /device:TPU:0, one launch (start us, length us, event | category | flops | bytes accessed | tf_op | source)
XLA Modules:
  0.0 63.5 jit_solution(12230152678033980644)
XLA Ops:
  0.0 0.0 copy-start.2
  0.0 0.0 copy-start.1
  0.0 1.5 %broadcast_in_dim.22 = f32[4,8,1792]{2,1,0:T(8,128)} broadcast(f32[8,1792]{1,0:T(8,128)} %param.5), dimensions={1,2} | broadcast | bytes 286720 | tf_op jit(solution)/shard_map/broadcast_in_dim | solution.py:66
  1.6 4.2 %all-to-all-start = ((f32[4,8,1792]{2,1,0:T(8,128)}), f32[4,8,1792]{2,1,0:T(8,128)S(1)}, u32[]{:S(2)}, u32[]{:S(2)}) async-start(f32[4,8,1792]{2,1,0:T(8,128)} %broadcast_in_dim.22), calls=%async_computation | async-start | bytes 458752 | tf_op jit(solution)/shard_map/all_to_all | solution.py:66
  5.8 0.1 add_multiply_fusion
  5.9 0.9 %broadcast_in_dim.21 = f32[8,1,1792]{2,1,0:T(1,128)S(1)} reshape(f32[8,1792]{1,0:T(8,128)} %param.5) | data formatting | bytes 114688 | tf_op jit(solution)/shard_map/broadcast_in_dim | solution.py:71
  6.8 0.1 copy.23
  6.9 0.6 gather_fusion
  7.5 0.1 maximum_bitcast_fusion
  7.6 0.1 dot_general.54
  7.7 0.1 broadcast_add_fusion
  7.7 0.6 gather_fusion.1
  8.3 0.1 copy.24
  8.4 0.4 fusion.17
  8.8 2.7 %all-to-all-done = f32[4,8,1792]{2,1,0:T(8,128)S(1)} async-done(((f32[4,8,1792]{2,1,0:T(8,128)}), f32[4,8,1792]{2,1,0:T(8,128)S(1)}, u32[]{:S(2)}, u32[]{:S(2)}) %all-to-all-start) | async-done | bytes 229408 | tf_op jit(solution)/shard_map/all_to_all | solution.py:66
  11.5 0.9 %fusion.20 = f32[3,1792]{1,0:T(4,128)S(1)} fusion(f32[4,8,1792]{2,1,0:T(8,128)S(1)} %all-to-all-done, s32[3]{0:T(128)} %param.8), kind=kOutput, calls=%fused_computation.32 | convolution fusion | flops 2064480 | bytes 250892 | tf_op jit(solution)/shard_map/dot_general | solution.py:69
  12.4 0.8 %pad_maximum_fusion = f32[8,4,1792]{2,1,0:T(4,128)} fusion(f32[8,3,1792]{2,1,0:T(4,128)S(1)} %broadcast_in_dim.23, f32[8,1,1792]{2,1,0:T(1,128)S(1)} %broadcast_in_dim.21), kind=kLoop, calls=%fused_computation.31 | loop fusion | flops 57344 | bytes 458752 | tf_op jit(solution)/shard_map/concatenate | solution.py:70
  13.2 0.0 copy-done.1
  13.2 0.1 lt.95
  13.3 6.4 %all-to-all-start.1 = ((f32[8,4,1792]{2,1,0:T(4,128)}), f32[8,4,1792]{2,1,0:T(4,128)S(1)}, u32[]{:S(2)}, u32[]{:S(2)}) async-start(f32[8,4,1792]{2,1,0:T(4,128)} %pad_maximum_fusion), calls=%async_computation.1 | async-start | bytes 458752 | tf_op jit(solution)/shard_map/all_to_all | solution.py:73
  19.7 0.0 copy-done.2
  19.7 0.3 fusion.32
  20.0 0.3 fusion.33
  20.3 2.7 %broadcast_multiply_fusion = f32[48,48,448]{2,1,0:T(8,128)} fusion(f32[48,448]{1,0:T(8,128)S(1)} %fusion.33, f32[48,448]{1,0:T(8,128)S(1)} %fusion.32), kind=kLoop, calls=%fused_computation.14 | loop fusion | flops 1032192 | bytes 4300800 | tf_op jit(solution)/shard_map/mul | solution.py:49
  23.0 0.1 iota_compare_fusion
  23.2 0.4 fusion.30
  23.6 4.3 %all-to-all-done.1 = f32[8,4,1792]{2,1,0:T(4,128)S(1)} async-done(((f32[8,4,1792]{2,1,0:T(4,128)}), f32[8,4,1792]{2,1,0:T(4,128)S(1)}, u32[]{:S(2)}, u32[]{:S(2)}) %all-to-all-start.1) | async-done | bytes 229408 | tf_op jit(solution)/shard_map/all_to_all | solution.py:73
  28.0 0.3 reshape.210
  28.3 0.0 copy-start
  28.3 0.1 broadcast_select_fusion
  28.4 1.4 %fusion.37 = f32[448,4,2,48]{0,3,2,1:T(8,128)S(1)} fusion(f32[448,4,32,1]{2,0,3,1:T(8,128)S(1)} %bitcast.81, f32[2,48,32]{1,0,2:T(2,128)S(1)} %dot_general.54), kind=kOutput, calls=%fused_computation.58 | convolution fusion | flops 66060288 | bytes 929792 | tf_op jit(solution)/shard_map/dot_general | solution.py:84
  29.7 0.1 fusion.93
  29.8 0.1 fusion.19
  29.9 0.7 %copy-done = f32[48,48,448]{2,1,0:T(8,128)S(1)} copy-done((f32[48,48,448]{2,1,0:T(8,128)S(1)}, f32[48,48,448]{2,1,0:T(8,128)}, u32[]{:S(2)}) %copy-start) | copy-done | bytes 4128792
  30.6 4.0 %fusion.94 = f32[48,48,4,48]{3,1,2,0:T(8,128)S(1)} fusion(f32[48,48,448,1]{2,1,3,0:T(8,128)S(1)} %bitcast.78, f32[4,48,448,1]{2,1,0,3:T(8,128)S(1)} %bitcast.83), kind=kOutput, calls=%fused_computation.133 | convolution fusion | flops 1189085184 | bytes 6242304 | tf_op jit(solution)/shard_map/dot_general | solution.py:86
  34.6 0.1 slice_bitcast_fusion
  34.7 1.7 %fusion.8 = f32[48,48,3,48]{3,1,2,0:T(8,128)S(1)} fusion(f32[48,48,4,48]{3,1,2,0:T(8,128)S(1)} %fusion.94, f32[48,48,48]{2,1,0:T(8,128)S(1)} %slice_bitcast_fusion), kind=kOutput, calls=%fused_computation.11 | convolution fusion | flops 95908608 | bytes 6045696 | tf_op jit(solution)/shard_map/absc,ck->absk/dot_general | solution.py:53
  36.4 1.9 %convolution_bitcast_fusion.1 = f32[48,48,3,48]{3,1,2,0:T(8,128)S(1)} fusion(f32[48,48,3,48]{3,1,2,0:T(8,128)S(1)} %fusion.8), kind=kOutput, calls=%fused_computation.16 | convolution fusion | flops 95576832 | bytes 2654208 | tf_op jit(solution)/shard_map/absc,kb->aksc/dot_general | solution.py:54
  38.3 3.2 %fusion.11 = f32[48,48,3,48]{3,0,2,1:T(8,128)S(1)} fusion(f32[48,48,3,48]{3,1,2,0:T(8,128)S(1)} %convolution_bitcast_fusion.1, f32[48,48,48]{2,0,1:T(8,128)S(1)} %fusion.17), kind=kOutput, calls=%fused_computation.17 | convolution fusion | flops 95908608 | bytes 3096576 | tf_op jit(solution)/shard_map/absc,ka->kbsc/dot_general | solution.py:55
  41.5 2.7 %fusion.4 = f32[48,48,3,48]{3,1,2,0:T(8,128)S(1)} fusion(f32[48,48,3,48]{3,0,2,1:T(8,128)S(1)} %fusion.11), kind=kOutput, calls=%fused_computation.7 | convolution fusion | flops 95576832 | bytes 2654208 | tf_op jit(solution)/shard_map/absc,ck->absk/dot_general | solution.py:53
  44.2 1.9 %convolution_bitcast_fusion = f32[48,48,3,48]{3,1,2,0:T(8,128)S(1)} fusion(f32[48,48,3,48]{3,1,2,0:T(8,128)S(1)} %fusion.4), kind=kOutput, calls=%fused_computation.15 | convolution fusion | flops 95576832 | bytes 2654208 | tf_op jit(solution)/shard_map/absc,kb->aksc/dot_general | solution.py:54
  46.1 0.0 copy-start.3
  46.1 2.9 %fusion.2 = f32[48,48,3,48]{3,0,2,1:T(8,128)S(1)} fusion(f32[48,48,3,48]{3,1,2,0:T(8,128)S(1)} %convolution_bitcast_fusion), kind=kOutput, calls=%fused_computation.5 | convolution fusion | flops 95576832 | bytes 2654208 | tf_op jit(solution)/shard_map/absc,ka->kbsc/dot_general | solution.py:55
  49.1 0.0 copy-done.3
  49.1 1.5 %fusion.1 = f32[48,48,48]{2,1,0:T(8,128)S(1)} fusion(f32[48,48,3,48]{3,0,2,1:T(8,128)S(1)} %fusion.2, f32[48,48,4,48]{3,1,2,0:T(8,128)S(1)} %fusion.94, f32[3]{0:T(128)S(1)} %copy-done.3), kind=kLoop, calls=%fused_computation.4 | loop fusion | flops 884736 | bytes 3096588 | tf_op jit(solution)/shard_map/reduce_sum | solution.py:92
  50.6 1.7 %fusion.36 = (f32[448,48]{0,1:T(8,128)S(1)}, f32[448,48]{0,1:T(8,128)S(1)}) fusion(s32[448]{0:T(512)S(1)} %get-tuple-element.19, f32[2304,448]{1,0:T(8,128)S(1)} %bitcast.79, f32[2304,48]{1,0:T(8,128)S(1)} %bitcast.80), kind=kOutput, calls=%fused_computation.57 | convolution fusion | flops 297529344 | bytes 4744960 | tf_op jit(solution)/shard_map/dot_general | solution.py:93
  52.3 0.3 fusion.18
  52.6 0.1 copy.25
  52.7 0.2 reshape.235
  52.9 10.0 %all_to_all.15 = f32[8,1,1792]{2,1,0:T(1,128)S(1)} all-to-all(f32[8,1,1792]{2,1,0:T(1,128)S(1)} %reshape.235), channel_id=1, replica_groups=mesh['grp'=4,'col'=8] {'col'}, dimensions={0} | all-to-all | bytes 114688 | tf_op jit(solution)/shard_map/all_to_all | solution.py:97
  62.9 0.6 copy.51
  (7 shorter events, 0.1 us)
Async XLA Ops:
  0.0 19.7 %copy-start.2 = (s32[448]{0:T(512)S(1)}, s32[448]{0:T(512)}, u32[]{:S(2)}) copy-start(s32[448]{0:T(512)} %param.6) | copy-start | bytes 5380
  0.0 13.2 %copy-start.1 = (s32[448]{0:T(512)S(1)}, s32[448]{0:T(512)}, u32[]{:S(2)}) copy-start(s32[448]{0:T(512)} %param.7) | copy-start | bytes 5380
  1.6 9.9 %all-to-all-start = ((f32[4,8,1792]{2,1,0:T(8,128)}), f32[4,8,1792]{2,1,0:T(8,128)S(1)}, u32[]{:S(2)}, u32[]{:S(2)}) async-start(f32[4,8,1792]{2,1,0:T(8,128)} %broadcast_in_dim.22), calls=%async_computation | async-start | bytes 458752 | tf_op jit(solution)/shard_map/all_to_all | solution.py:66
  13.3 14.6 %all-to-all-start.1 = ((f32[8,4,1792]{2,1,0:T(4,128)}), f32[8,4,1792]{2,1,0:T(4,128)S(1)}, u32[]{:S(2)}, u32[]{:S(2)}) async-start(f32[8,4,1792]{2,1,0:T(4,128)} %pad_maximum_fusion), calls=%async_computation.1 | async-start | bytes 458752 | tf_op jit(solution)/shard_map/all_to_all | solution.py:73
  28.3 2.3 %copy-start = (f32[48,48,448]{2,1,0:T(8,128)S(1)}, f32[48,48,448]{2,1,0:T(8,128)}, u32[]{:S(2)}) copy-start(f32[48,48,448]{2,1,0:T(8,128)} %broadcast_multiply_fusion) | copy-start | bytes 12386308
  46.1 3.0 %copy-start.3 = (f32[3]{0:T(128)S(1)}, f32[3]{0:T(128)}, u32[]{:S(2)}) copy-start(f32[3]{0:T(128)} %param.9) | copy-start | bytes 40

commit v13 on v9

--- a/solution.py
+++ b/solution.py
@@ -55,6 +55,12 @@
     return jnp.einsum("absc,ka->kbsc", field, table, precision=MID)
 
 
+def cas_three_reversed(field, table):
+    field = jnp.einsum("absc,ka->kbsc", field, table, precision=MID)
+    field = jnp.einsum("absc,kb->aksc", field, table, precision=MID)
+    return jnp.einsum("absc,ck->absk", field, table, precision=MID)
+
+
 def make_local(n_grp_bands, n_grp, n_col):
     def local(orbitals, column_cell, column_length, sources, weights):
         extent = GRID
@@ -91,7 +97,7 @@
         own = grids[:, :, :1]
         src = grids[:, :, 1:]
         density = own * src
-        potential = cas_three(kernel[:, :, None, :] * cas_three(density, table), table)
+        potential = cas_three_reversed(kernel[:, :, None, :] * cas_three(density, table), table)
         total = jnp.sum(weights[None, None, :, None] * potential * src, axis=2)
         back = lax.dot_general(w, total.reshape(extent * extent, extent), (((0,), (0,)), ((), ())), precision=MID)
         scaled = jnp.concatenate([back * cos_h, -(back * sin_h)], axis=1)

time: 64 us -> 60.7 us (0.948)
  matrix products: 23.3 us -> 21.5 us
  other arithmetic: 7.79 us -> 6.32 us
    dot_general x0 -> x3, matrix products: none -> 6.24 us  [the longest x1 2.89 us: cas_three_reversed(): field = jnp.einsum('absc,kb->aksc', field, table, precision=MID)]
    dot_general x2 -> x1, matrix products: 6.12 us -> 3.07 us  [cas_three(): return jnp.einsum('absc,ka->kbsc', field, table, precision=MID)]
    dot_general x2 -> x1, matrix products: 4.43 us -> 1.67 us  [cas_three(): field = jnp.einsum('absc,ck->absk', field, table, precision=MID)]
    dot_general x2 -> x1, matrix products: 3.76 us -> 1.78 us  [cas_three(): field = jnp.einsum('absc,kb->aksc', field, table, precision=MID)]
    reduce_sum x1 -> x0, other arithmetic: 1.47 us -> none  [local(): total = jnp.sum(weights[None, None, :, None] * potential * src, axis=2)]
where the time goes in v13:
time: 60.7 us; the launch traced here: 60.1 us
  matrix products  21.5 us (35%)
  starting transfers between devices  10.5 us (17%)
  blocking collectives  10 us (16%)
  other arithmetic  6.32 us (10%)
  local copies, waits for them, and re-layouts  5.82 us (10%)
  waiting for transfers between devices  5.69 us (9%)
    all_to_all x1, blocking collectives, local(): lax.all_to_all(out.reshape(n_col, 1, width), 'col', 0, 0, tiled=True)  10 us
    all_to_all x1, starting transfers between devices, local(): got = lax.all_to_all(send, 'col', 0, 0, tiled=True)  6.31 us
    all_to_all x1, starting transfers between devices, local(): picked = jnp.sum(lax.all_to_all(spread, 'grp', 0, 0, tiled=True), axis=0)  4.24 us
    all_to_all x1, waiting for transfers between devices, local(): got = lax.all_to_all(send, 'col', 0, 0, tiled=True)  4.19 us
    dot_general x1, matrix products, local(): grids = jnp.dot(w, cols.reshape(count, n * extent), precision=MID)  3.85 us
    dot_general x1, matrix products, cas_three(): return jnp.einsum('absc,ka->kbsc', field, table, precision=MID)  3.07 us
    dot_general x1, matrix products, cas_three_reversed(): field = jnp.einsum('absc,kb->aksc', field, table, precision=MID)  2.89 us
    mul x1, other arithmetic, plane_matrix(): return (ta[:, None, :] * tb[None, :, :]).reshape(extent * extent, -1)  2.73 us
  transfers between devices with their start and end apart: 2, of which 2 were waited for; matrix products, arithmetic and copies ran while one was open for 11% of the time, Pallas kernels for 0%

profile of v13, /device:TPU:0, one launch (start us, length us, event | category | flops | bytes accessed | tf_op | source)
XLA Modules:
  0.0 60.1 jit_solution(14275975045817455932)
XLA Ops:
  0.0 0.0 copy-start.2
  0.0 0.0 copy-start.1
  0.0 0.7 %and_select_fusion.1 = s32[3]{0:T(128)S(1)} fusion(s32[3]{0:T(128)} %param.8), kind=kLoop, calls=%fused_computation.92 | loop fusion | flops 33 | bytes 24 | tf_op jit(solution)/shard_map/jit(remainder)/select_n | solution.py:74
  0.7 0.7 %fusion.58 = pred[3]{0:T(512)(128)(4,1)S(1)} fusion(s32[3]{0:T(128)} %param.8, s32[]{:T(128)S(6)} %axis_index.15), kind=kLoop, calls=%fused_computation.102 | loop fusion | flops 48 | bytes 19 | tf_op jit(solution)/shard_map/eq | solution.py:76
  1.4 1.0 %convolution_select_fusion = f32[3,1792]{1,0:T(4,128)S(1)} fusion(f32[8,1792]{1,0:T(8,128)} %param.5, pred[3]{0:T(512)(128)(4,1)S(1)} %fusion.58, s32[3]{0:T(128)S(1)} %and_select_fusion.1), kind=kOutput, calls=%fused_computation.15 | convolution fusion | flops 521496 | bytes 78863 | tf_op jit(solution)/shard_map/dot_general | solution.py:75
  2.4 0.7 %broadcast_in_dim.36 = f32[4,3,1792]{2,1,0:T(4,128)} broadcast(f32[3,1792]{1,0:T(4,128)S(1)} %convolution_select_fusion), dimensions={1,2} | broadcast | bytes 107520 | tf_op jit(solution)/shard_map/broadcast_in_dim | solution.py:77
  3.1 4.2 %all-to-all-start = ((f32[4,3,1792]{2,1,0:T(4,128)}), f32[4,3,1792]{2,1,0:T(4,128)S(1)}, u32[]{:S(2)}, u32[]{:S(2)}) async-start(f32[4,3,1792]{2,1,0:T(4,128)} %broadcast_in_dim.36), calls=%async_computation | async-start | bytes 229376 | tf_op jit(solution)/shard_map/all_to_all | solution.py:78
  7.3 0.1 add_multiply_fusion
  7.4 0.9 %broadcast_in_dim.33 = f32[8,1,1792]{2,1,0:T(1,128)S(1)} reshape(f32[8,1792]{1,0:T(8,128)} %param.5) | data formatting | bytes 114688 | tf_op jit(solution)/shard_map/broadcast_in_dim | solution.py:80
  8.3 0.1 copy.38
  8.4 0.6 gather_fusion
  9.0 0.1 broadcast_add_fusion
  9.1 0.4 fusion.17
  9.4 0.1 maximum_bitcast_fusion
  9.5 0.1 dot_general.54
  9.6 0.6 gather_fusion.1
  10.2 0.1 copy.39
  10.3 1.5 %all-to-all-done = f32[4,3,1792]{2,1,0:T(4,128)S(1)} async-done(((f32[4,3,1792]{2,1,0:T(4,128)}), f32[4,3,1792]{2,1,0:T(4,128)S(1)}, u32[]{:S(2)}, u32[]{:S(2)}) %all-to-all-start) | async-done | bytes 86048 | tf_op jit(solution)/shard_map/all_to_all | solution.py:78
  11.8 0.8 %pad_maximum_fusion = f32[8,4,1792]{2,1,0:T(4,128)} fusion(f32[8,3,1792]{2,1,0:T(4,128)S(1)} %broadcast_in_dim.37, f32[8,1,1792]{2,1,0:T(1,128)S(1)} %broadcast_in_dim.33), kind=kLoop, calls=%fused_computation.31 | loop fusion | flops 57344 | bytes 458752 | tf_op jit(solution)/shard_map/concatenate | solution.py:79
  12.6 0.8 %lt.102 = s32[8,56]{1,0:T(8,128)S(1)} reshape(s32[448]{0:T(512)} %param.7) | data formatting | bytes 3584 | tf_op jit(solution)/shard_map/lt | solution.py:39
  13.4 6.3 %all-to-all-start.1 = ((f32[8,4,1792]{2,1,0:T(4,128)}), f32[8,4,1792]{2,1,0:T(4,128)S(1)}, u32[]{:S(2)}, u32[]{:S(2)}) async-start(f32[8,4,1792]{2,1,0:T(4,128)} %pad_maximum_fusion), calls=%async_computation.1 | async-start | bytes 458752 | tf_op jit(solution)/shard_map/all_to_all | solution.py:82
  19.7 0.0 copy-done.2
  19.7 0.0 copy-done.1
  19.7 0.3 fusion.30
  20.1 0.3 fusion.31
  20.4 2.7 %broadcast_multiply_fusion = f32[48,48,448]{2,1,0:T(8,128)} fusion(f32[48,448]{1,0:T(8,128)S(1)} %fusion.31, f32[48,448]{1,0:T(8,128)S(1)} %fusion.30), kind=kLoop, calls=%fused_computation.14 | loop fusion | flops 1032192 | bytes 4300800 | tf_op jit(solution)/shard_map/mul | solution.py:49
  23.1 0.1 iota_compare_fusion
  23.2 0.4 fusion.28
  23.6 4.2 %all-to-all-done.1 = f32[8,4,1792]{2,1,0:T(4,128)S(1)} async-done(((f32[8,4,1792]{2,1,0:T(4,128)}), f32[8,4,1792]{2,1,0:T(4,128)S(1)}, u32[]{:S(2)}, u32[]{:S(2)}) %all-to-all-start.1) | async-done | bytes 229408 | tf_op jit(solution)/shard_map/all_to_all | solution.py:82
  27.9 0.3 reshape.207
  28.2 0.0 copy-start
  28.2 0.1 broadcast_select_fusion
  28.3 1.3 %fusion.35 = f32[448,4,2,48]{0,3,2,1:T(8,128)S(1)} fusion(f32[448,4,32,1]{2,0,3,1:T(8,128)S(1)} %bitcast.81, f32[2,48,32]{1,0,2:T(2,128)S(1)} %dot_general.54), kind=kOutput, calls=%fused_computation.56 | convolution fusion | flops 66060288 | bytes 929792 | tf_op jit(solution)/shard_map/dot_general | solution.py:93
  29.6 0.1 fusion.92
  29.7 0.1 fusion.19
  29.8 0.7 %copy-done = f32[48,48,448]{2,1,0:T(8,128)S(1)} copy-done((f32[48,48,448]{2,1,0:T(8,128)S(1)}, f32[48,48,448]{2,1,0:T(8,128)}, u32[]{:S(2)}) %copy-start) | copy-done | bytes 4128792
  30.5 3.8 %fusion.93 = f32[48,48,4,48]{3,1,2,0:T(8,128)S(1)} fusion(f32[48,48,448,1]{2,1,3,0:T(8,128)S(1)} %bitcast.78, f32[4,48,448,1]{2,1,0,3:T(8,128)S(1)} %bitcast.83), kind=kOutput, calls=%fused_computation.137 | convolution fusion | flops 1189085184 | bytes 6242304 | tf_op jit(solution)/shard_map/dot_general | solution.py:95
  34.4 0.1 slice_bitcast_fusion
  34.5 1.7 %fusion.8 = f32[48,48,3,48]{3,1,2,0:T(8,128)S(1)} fusion(f32[48,48,4,48]{3,1,2,0:T(8,128)S(1)} %fusion.93, f32[48,48,48]{2,1,0:T(8,128)S(1)} %slice_bitcast_fusion), kind=kOutput, calls=%fused_computation.11 | convolution fusion | flops 95908608 | bytes 6045696 | tf_op jit(solution)/shard_map/absc,ck->absk/dot_general | solution.py:53
  36.1 1.8 %convolution_bitcast_fusion = f32[48,48,3,48]{3,1,2,0:T(8,128)S(1)} fusion(f32[48,48,3,48]{3,1,2,0:T(8,128)S(1)} %fusion.8), kind=kOutput, calls=%fused_computation.16 | convolution fusion | flops 95576832 | bytes 2654208 | tf_op jit(solution)/shard_map/absc,kb->aksc/dot_general | solution.py:54
  37.9 3.1 %fusion.4 = f32[48,48,3,48]{3,0,2,1:T(8,128)S(1)} fusion(f32[48,48,3,48]{3,1,2,0:T(8,128)S(1)} %convolution_bitcast_fusion), kind=kOutput, calls=%fused_computation.6 | convolution fusion | flops 95576832 | bytes 2654208 | tf_op jit(solution)/shard_map/absc,ka->kbsc/dot_general | solution.py:55
  41.0 1.7 %fusion.6 = f32[48,48,3,48]{3,0,2,1:T(8,128)S(1)} fusion(f32[48,48,3,48]{3,0,2,1:T(8,128)S(1)} %fusion.4, f32[48,48,48]{2,0,1:T(8,128)S(1)} %fusion.17), kind=kOutput, calls=%fused_computation.9 | convolution fusion | flops 95908608 | bytes 3096576 | tf_op jit(solution)/shard_map/absc,ka->kbsc/dot_general | solution.py:59
  42.7 0.0 copy-start.3
  42.7 2.9 %fusion.2 = f32[48,48,3,48]{3,0,2,1:T(8,128)S(1)} fusion(f32[48,48,3,48]{3,0,2,1:T(8,128)S(1)} %fusion.6), kind=kOutput, calls=%fused_computation.4 | convolution fusion | flops 95576832 | bytes 2654208 | tf_op jit(solution)/shard_map/absc,kb->aksc/dot_general | solution.py:60
  45.6 0.0 copy-done.3
  45.6 1.7 %multiply_reduce_fusion = f32[48,48,48]{2,1,0:T(8,128)S(1)} fusion(f32[48,48,4,48]{3,1,2,0:T(8,128)S(1)} %fusion.93, f32[48,48,3,48]{3,0,2,1:T(8,128)S(1)} %fusion.2, f32[3]{0:T(128)S(1)} %copy-done.3), kind=kOutput, calls=%fused_computation.8 | convolution fusion | flops 96461568 | bytes 3096588 | tf_op jit(solution)/shard_map/absc,ck->absk/dot_general | solution.py:61
  47.3 1.6 %fusion.34 = (f32[448,48]{0,1:T(8,128)S(1)}, f32[448,48]{0,1:T(8,128)S(1)}) fusion(s32[448]{0:T(512)S(1)} %get-tuple-element.19, f32[2304,448]{1,0:T(8,128)S(1)} %bitcast.79, f32[2304,48]{1,0:T(8,128)S(1)} %bitcast.80), kind=kOutput, calls=%fused_computation.55 | convolution fusion | flops 297529344 | bytes 4744960 | tf_op jit(solution)/shard_map/dot_general | solution.py:102
  48.9 0.3 fusion.18
  49.2 0.1 copy.40
  49.3 0.2 reshape.232
  49.5 10.0 %all_to_all.15 = f32[8,1,1792]{2,1,0:T(1,128)S(1)} all-to-all(f32[8,1,1792]{2,1,0:T(1,128)S(1)} %reshape.232), channel_id=1, replica_groups=mesh['grp'=4,'col'=8] {'col'}, dimensions={0} | all-to-all | bytes 114688 | tf_op jit(solution)/shard_map/all_to_all | solution.py:106
  59.5 0.6 %copy.58 = f32[8,1,1792]{2,0,1:T(8,128)} copy(f32[8,1,1792]{2,1,0:T(1,128)S(1)} %all_to_all.15) | data formatting | bytes 114688
  (8 shorter events, 0.2 us)
Async XLA Ops:
  0.0 19.7 %copy-start.2 = (s32[448]{0:T(512)S(1)}, s32[448]{0:T(512)}, u32[]{:S(2)}) copy-start(s32[448]{0:T(512)} %param.6) | copy-start | bytes 5380
  0.0 19.7 %copy-start.1 = (s32[448]{0:T(512)S(1)}, s32[448]{0:T(512)}, u32[]{:S(2)}) copy-start(s32[448]{0:T(512)} %param.7) | copy-start | bytes 5380
  3.1 8.7 %all-to-all-start = ((f32[4,3,1792]{2,1,0:T(4,128)}), f32[4,3,1792]{2,1,0:T(4,128)S(1)}, u32[]{:S(2)}, u32[]{:S(2)}) async-start(f32[4,3,1792]{2,1,0:T(4,128)} %broadcast_in_dim.36), calls=%async_computation | async-start | bytes 229376 | tf_op jit(solution)/shard_map/all_to_all | solution.py:78
  13.4 14.4 %all-to-all-start.1 = ((f32[8,4,1792]{2,1,0:T(4,128)}), f32[8,4,1792]{2,1,0:T(4,128)S(1)}, u32[]{:S(2)}, u32[]{:S(2)}) async-start(f32[8,4,1792]{2,1,0:T(4,128)} %pad_maximum_fusion), calls=%async_computation.1 | async-start | bytes 458752 | tf_op jit(solution)/shard_map/all_to_all | solution.py:82
  28.2 2.3 %copy-start = (f32[48,48,448]{2,1,0:T(8,128)S(1)}, f32[48,48,448]{2,1,0:T(8,128)}, u32[]{:S(2)}) copy-start(f32[48,48,448]{2,1,0:T(8,128)} %broadcast_multiply_fusion) | copy-start | bytes 12386308
  42.7 2.9 %copy-start.3 = (f32[3]{0:T(128)S(1)}, f32[3]{0:T(128)}, u32[]{:S(2)}) copy-start(f32[3]{0:T(128)} %param.9) | copy-start | bytes 40

commit v14 on v13

--- a/solution.py
+++ b/solution.py
@@ -97,7 +97,7 @@
         own = grids[:, :, :1]
         src = grids[:, :, 1:]
         density = own * src
-        potential = cas_three_reversed(kernel[:, :, None, :] * cas_three(density, table), table)
+        potential = cas_three(kernel[:, :, None, :] * cas_three_reversed(density, table), table)
         total = jnp.sum(weights[None, None, :, None] * potential * src, axis=2)
         back = lax.dot_general(w, total.reshape(extent * extent, extent), (((0,), (0,)), ((), ())), precision=MID)
         scaled = jnp.concatenate([back * cos_h, -(back * sin_h)], axis=1)

time: 60.7 us -> 64.5 us (1.063)
  other arithmetic: 6.32 us -> 8.26 us
  matrix products: 21.5 us -> 23.4 us
    reduce_sum x0 -> x1, other arithmetic: none -> 1.47 us  [local(): total = jnp.sum(weights[None, None, :, None] * potential * src, axis=2)]
    dot_general x1, matrix products: 1.7 us -> 2.95 us  [cas_three_reversed(): field = jnp.einsum('absc,ka->kbsc', field, table, precision=MID)]
where the time goes in v14:
time: 64.5 us; the launch traced here: 64 us
  matrix products  23.4 us (36%)
  starting transfers between devices  10.5 us (16%)
  blocking collectives  10 us (16%)
  other arithmetic  8.26 us (13%)
  local copies, waits for them, and re-layouts  5.82 us (9%)
  waiting for transfers between devices  5.69 us (9%)
    all_to_all x1, blocking collectives, local(): lax.all_to_all(out.reshape(n_col, 1, width), 'col', 0, 0, tiled=True)  10 us
    all_to_all x1, starting transfers between devices, local(): got = lax.all_to_all(send, 'col', 0, 0, tiled=True)  6.31 us
    all_to_all x1, starting transfers between devices, local(): picked = jnp.sum(lax.all_to_all(spread, 'grp', 0, 0, tiled=True), axis=0)  4.24 us
    all_to_all x1, waiting for transfers between devices, local(): got = lax.all_to_all(send, 'col', 0, 0, tiled=True)  4.19 us
    dot_general x1, matrix products, local(): grids = jnp.dot(w, cols.reshape(count, n * extent), precision=MID)  4.04 us
    dot_general x1, matrix products, cas_three_reversed(): field = jnp.einsum('absc,kb->aksc', field, table, precision=MID)  3.14 us
    dot_general x1, matrix products, cas_three(): return jnp.einsum('absc,ka->kbsc', field, table, precision=MID)  2.95 us
    dot_general x1, matrix products, cas_three_reversed(): field = jnp.einsum('absc,ka->kbsc', field, table, precision=MID)  2.95 us
  transfers between devices with their start and end apart: 2, of which 2 were waited for; matrix products, arithmetic and copies ran while one was open for 11% of the time, Pallas kernels for 0%

profile of v14, /device:TPU:0, one launch (start us, length us, event | category | flops | bytes accessed | tf_op | source)
XLA Modules:
  0.0 64.0 jit_solution(8591393450508358548)
XLA Ops:
  0.0 0.0 copy-start.2
  0.0 0.0 copy-start.1
  0.0 0.7 %and_select_fusion.1 = s32[3]{0:T(128)S(1)} fusion(s32[3]{0:T(128)} %param.8), kind=kLoop, calls=%fused_computation.93 | loop fusion | flops 33 | bytes 24 | tf_op jit(solution)/shard_map/jit(remainder)/select_n | solution.py:74
  0.7 0.7 %fusion.56 = pred[3]{0:T(512)(128)(4,1)S(1)} fusion(s32[3]{0:T(128)} %param.8, s32[]{:T(128)S(6)} %axis_index.15), kind=kLoop, calls=%fused_computation.103 | loop fusion | flops 48 | bytes 19 | tf_op jit(solution)/shard_map/eq | solution.py:76
  1.4 1.0 %convolution_select_fusion = f32[3,1792]{1,0:T(4,128)S(1)} fusion(f32[8,1792]{1,0:T(8,128)} %param.5, pred[3]{0:T(512)(128)(4,1)S(1)} %fusion.56, s32[3]{0:T(128)S(1)} %and_select_fusion.1), kind=kOutput, calls=%fused_computation.17 | convolution fusion | flops 521496 | bytes 78863 | tf_op jit(solution)/shard_map/dot_general | solution.py:75
  2.4 0.7 %broadcast_in_dim.36 = f32[4,3,1792]{2,1,0:T(4,128)} broadcast(f32[3,1792]{1,0:T(4,128)S(1)} %convolution_select_fusion), dimensions={1,2} | broadcast | bytes 107520 | tf_op jit(solution)/shard_map/broadcast_in_dim | solution.py:77
  3.1 4.2 %all-to-all-start = ((f32[4,3,1792]{2,1,0:T(4,128)}), f32[4,3,1792]{2,1,0:T(4,128)S(1)}, u32[]{:S(2)}, u32[]{:S(2)}) async-start(f32[4,3,1792]{2,1,0:T(4,128)} %broadcast_in_dim.36), calls=%async_computation | async-start | bytes 229376 | tf_op jit(solution)/shard_map/all_to_all | solution.py:78
  7.3 0.1 add_multiply_fusion
  7.4 0.9 %broadcast_in_dim.33 = f32[8,1,1792]{2,1,0:T(1,128)S(1)} reshape(f32[8,1792]{1,0:T(8,128)} %param.5) | data formatting | bytes 114688 | tf_op jit(solution)/shard_map/broadcast_in_dim | solution.py:80
  8.3 0.1 copy.46
  8.4 0.6 gather_fusion
  9.0 0.1 broadcast_add_fusion
  9.1 0.4 fusion.15
  9.4 0.1 maximum_bitcast_fusion
  9.5 0.1 dot_general.54
  9.6 0.6 gather_fusion.1
  10.2 0.1 copy.47
  10.3 1.5 %all-to-all-done = f32[4,3,1792]{2,1,0:T(4,128)S(1)} async-done(((f32[4,3,1792]{2,1,0:T(4,128)}), f32[4,3,1792]{2,1,0:T(4,128)S(1)}, u32[]{:S(2)}, u32[]{:S(2)}) %all-to-all-start) | async-done | bytes 86048 | tf_op jit(solution)/shard_map/all_to_all | solution.py:78
  11.8 0.8 %pad_maximum_fusion = f32[8,4,1792]{2,1,0:T(4,128)} fusion(f32[8,3,1792]{2,1,0:T(4,128)S(1)} %broadcast_in_dim.37, f32[8,1,1792]{2,1,0:T(1,128)S(1)} %broadcast_in_dim.33), kind=kLoop, calls=%fused_computation.32 | loop fusion | flops 57344 | bytes 458752 | tf_op jit(solution)/shard_map/concatenate | solution.py:79
  12.6 0.8 %lt.102 = s32[8,56]{1,0:T(8,128)S(1)} reshape(s32[448]{0:T(512)} %param.7) | data formatting | bytes 3584 | tf_op jit(solution)/shard_map/lt | solution.py:39
  13.4 6.3 %all-to-all-start.1 = ((f32[8,4,1792]{2,1,0:T(4,128)}), f32[8,4,1792]{2,1,0:T(4,128)S(1)}, u32[]{:S(2)}, u32[]{:S(2)}) async-start(f32[8,4,1792]{2,1,0:T(4,128)} %pad_maximum_fusion), calls=%async_computation.1 | async-start | bytes 458752 | tf_op jit(solution)/shard_map/all_to_all | solution.py:82
  19.7 0.0 copy-done.2
  19.7 0.0 copy-done.1
  19.7 0.3 fusion.28
  20.1 0.3 fusion.29
  20.4 2.7 %broadcast_multiply_fusion = f32[48,48,448]{2,1,0:T(8,128)} fusion(f32[48,448]{1,0:T(8,128)S(1)} %fusion.29, f32[48,448]{1,0:T(8,128)S(1)} %fusion.28), kind=kLoop, calls=%fused_computation.16 | loop fusion | flops 1032192 | bytes 4300800 | tf_op jit(solution)/shard_map/mul | solution.py:49
  23.1 0.1 iota_compare_fusion
  23.2 0.4 fusion.26
  23.6 4.2 %all-to-all-done.1 = f32[8,4,1792]{2,1,0:T(4,128)S(1)} async-done(((f32[8,4,1792]{2,1,0:T(4,128)}), f32[8,4,1792]{2,1,0:T(4,128)S(1)}, u32[]{:S(2)}, u32[]{:S(2)}) %all-to-all-start.1) | async-done | bytes 229408 | tf_op jit(solution)/shard_map/all_to_all | solution.py:82
  27.9 0.3 reshape.207
  28.2 0.0 copy-start
  28.2 0.1 broadcast_select_fusion
  28.3 1.3 %fusion.33 = f32[448,4,2,48]{0,3,2,1:T(8,128)S(1)} fusion(f32[448,4,32,1]{2,0,3,1:T(8,128)S(1)} %bitcast.79, f32[2,48,32]{1,0,2:T(2,128)S(1)} %dot_general.54), kind=kOutput, calls=%fused_computation.57 | convolution fusion | flops 66060288 | bytes 929792 | tf_op jit(solution)/shard_map/dot_general | solution.py:93
  29.6 0.1 fusion.90
  29.7 0.1 fusion.17
  29.8 0.7 %copy-done = f32[48,48,448]{2,1,0:T(8,128)S(1)} copy-done((f32[48,48,448]{2,1,0:T(8,128)S(1)}, f32[48,48,448]{2,1,0:T(8,128)}, u32[]{:S(2)}) %copy-start) | copy-done | bytes 4128792
  30.5 4.0 %fusion.91 = f32[48,48,4,48]{3,1,2,0:T(8,128)S(1)} fusion(f32[48,48,448,1]{2,1,3,0:T(8,128)S(1)} %bitcast.76, f32[4,48,448,1]{2,1,0,3:T(8,128)S(1)} %bitcast.81), kind=kOutput, calls=%fused_computation.138 | convolution fusion | flops 1189085184 | bytes 6242304 | tf_op jit(solution)/shard_map/dot_general | solution.py:95
  34.6 0.1 slice_bitcast_fusion
  34.6 0.5 slice_multiply_fusion
  35.1 2.9 %fusion.8 = f32[48,48,3,48]{3,0,2,1:T(8,128)S(1)} fusion(f32[48,48,3,48]{3,1,2,0:T(8,128)S(1)} %slice_multiply_fusion), kind=kOutput, calls=%fused_computation.11 | convolution fusion | flops 95576832 | bytes 2654208 | tf_op jit(solution)/shard_map/absc,ka->kbsc/dot_general | solution.py:59
  38.1 3.1 %fusion.6 = f32[48,48,3,48]{3,0,2,1:T(8,128)S(1)} fusion(f32[48,48,3,48]{3,0,2,1:T(8,128)S(1)} %fusion.8), kind=kOutput, calls=%fused_computation.9 | convolution fusion | flops 95576832 | bytes 2654208 | tf_op jit(solution)/shard_map/absc,kb->aksc/dot_general | solution.py:60
  41.2 1.7 %fusion = f32[48,48,3,48]{3,1,2,0:T(8,128)S(1)} fusion(f32[48,48,3,48]{3,0,2,1:T(8,128)S(1)} %fusion.6), kind=kOutput, calls=%fused_computation.2 | convolution fusion | flops 95576832 | bytes 2654208 | tf_op jit(solution)/shard_map/absc,ck->absk/dot_general | solution.py:61
  43.0 1.7 %fusion.10 = f32[48,48,3,48]{3,1,2,0:T(8,128)S(1)} fusion(f32[48,48,3,48]{3,1,2,0:T(8,128)S(1)} %fusion, f32[48,48,48]{2,1,0:T(8,128)S(1)} %fusion.15), kind=kOutput, calls=%fused_computation.13 | convolution fusion | flops 95908608 | bytes 3096576 | tf_op jit(solution)/shard_map/absc,ck->absk/dot_general | solution.py:53
  44.7 1.9 %convolution_bitcast_fusion = f32[48,48,3,48]{3,1,2,0:T(8,128)S(1)} fusion(f32[48,48,3,48]{3,1,2,0:T(8,128)S(1)} %fusion.10), kind=kOutput, calls=%fused_computation.18 | convolution fusion | flops 95576832 | bytes 2654208 | tf_op jit(solution)/shard_map/absc,kb->aksc/dot_general | solution.py:54
  46.6 0.0 copy-start.3
  46.6 2.9 %fusion.4 = f32[48,48,3,48]{3,0,2,1:T(8,128)S(1)} fusion(f32[48,48,3,48]{3,1,2,0:T(8,128)S(1)} %convolution_bitcast_fusion), kind=kOutput, calls=%fused_computation.7 | convolution fusion | flops 95576832 | bytes 2654208 | tf_op jit(solution)/shard_map/absc,ka->kbsc/dot_general | solution.py:55
  49.6 0.0 copy-done.3
  49.6 1.5 %fusion.3 = f32[48,48,48]{2,1,0:T(8,128)S(1)} fusion(f32[48,48,3,48]{3,0,2,1:T(8,128)S(1)} %fusion.4, f32[48,48,4,48]{3,1,2,0:T(8,128)S(1)} %fusion.91, f32[3]{0:T(128)S(1)} %copy-done.3), kind=kLoop, calls=%fused_computation.6 | loop fusion | flops 884736 | bytes 3096588 | tf_op jit(solution)/shard_map/reduce_sum | solution.py:101
  51.0 1.7 %fusion.32 = (f32[448,48]{0,1:T(8,128)S(1)}, f32[448,48]{0,1:T(8,128)S(1)}) fusion(s32[448]{0:T(512)S(1)} %get-tuple-element.19, f32[2304,448]{1,0:T(8,128)S(1)} %bitcast.77, f32[2304,48]{1,0:T(8,128)S(1)} %bitcast.78), kind=kOutput, calls=%fused_computation.56 | convolution fusion | flops 297529344 | bytes 4744960 | tf_op jit(solution)/shard_map/dot_general | solution.py:102
  52.7 0.3 fusion.16
  53.0 0.1 copy.48
  53.2 0.2 reshape.232
  53.3 10.0 %all_to_all.15 = f32[8,1,1792]{2,1,0:T(1,128)S(1)} all-to-all(f32[8,1,1792]{2,1,0:T(1,128)S(1)} %reshape.232), channel_id=1, replica_groups=mesh['grp'=4,'col'=8] {'col'}, dimensions={0} | all-to-all | bytes 114688 | tf_op jit(solution)/shard_map/all_to_all | solution.py:106
  63.3 0.6 copy.73
  (8 shorter events, 0.1 us)
Async XLA Ops:
  0.0 19.7 %copy-start.2 = (s32[448]{0:T(512)S(1)}, s32[448]{0:T(512)}, u32[]{:S(2)}) copy-start(s32[448]{0:T(512)} %param.6) | copy-start | bytes 5380
  0.0 19.7 %copy-start.1 = (s32[448]{0:T(512)S(1)}, s32[448]{0:T(512)}, u32[]{:S(2)}) copy-start(s32[448]{0:T(512)} %param.7) | copy-start | bytes 5380
  3.1 8.7 %all-to-all-start = ((f32[4,3,1792]{2,1,0:T(4,128)}), f32[4,3,1792]{2,1,0:T(4,128)S(1)}, u32[]{:S(2)}, u32[]{:S(2)}) async-start(f32[4,3,1792]{2,1,0:T(4,128)} %broadcast_in_dim.36), calls=%async_computation | async-start | bytes 229376 | tf_op jit(solution)/shard_map/all_to_all | solution.py:78
  13.4 14.4 %all-to-all-start.1 = ((f32[8,4,1792]{2,1,0:T(4,128)}), f32[8,4,1792]{2,1,0:T(4,128)S(1)}, u32[]{:S(2)}, u32[]{:S(2)}) async-start(f32[8,4,1792]{2,1,0:T(4,128)} %pad_maximum_fusion), calls=%async_computation.1 | async-start | bytes 458752 | tf_op jit(solution)/shard_map/all_to_all | solution.py:82
  28.2 2.3 %copy-start = (f32[48,48,448]{2,1,0:T(8,128)S(1)}, f32[48,48,448]{2,1,0:T(8,128)}, u32[]{:S(2)}) copy-start(f32[48,48,448]{2,1,0:T(8,128)} %broadcast_multiply_fusion) | copy-start | bytes 12386308
  46.6 3.0 %copy-start.3 = (f32[3]{0:T(128)S(1)}, f32[3]{0:T(128)}, u32[]{:S(2)}) copy-start(f32[3]{0:T(128)} %param.9) | copy-start | bytes 40

commit v15 on v13

--- a/solution.py
+++ b/solution.py
@@ -57,8 +57,8 @@
 
 def cas_three_reversed(field, table):
     field = jnp.einsum("absc,ka->kbsc", field, table, precision=MID)
-    field = jnp.einsum("absc,kb->aksc", field, table, precision=MID)
-    return jnp.einsum("absc,ck->absk", field, table, precision=MID)
+    field = jnp.einsum("absc,ck->absk", field, table, precision=MID)
+    return jnp.einsum("absc,kb->aksc", field, table, precision=MID)
 
 
 def make_local(n_grp_bands, n_grp, n_col):

time: 60.7 us -> 60.9 us (level)
  no operation moved by 1% of the time
where the time goes in v15:
time: 60.9 us; the launch traced here: 60.4 us
  matrix products  21.7 us (36%)
  starting transfers between devices  10.5 us (17%)
  blocking collectives  10 us (16%)
  other arithmetic  6.32 us (10%)
  local copies, waits for them, and re-layouts  5.82 us (10%)
  waiting for transfers between devices  5.69 us (9%)
    all_to_all x1, blocking collectives, local(): lax.all_to_all(out.reshape(n_col, 1, width), 'col', 0, 0, tiled=True)  10 us
    all_to_all x1, starting transfers between devices, local(): got = lax.all_to_all(send, 'col', 0, 0, tiled=True)  6.31 us
    all_to_all x1, starting transfers between devices, local(): picked = jnp.sum(lax.all_to_all(spread, 'grp', 0, 0, tiled=True), axis=0)  4.24 us
    all_to_all x1, waiting for transfers between devices, local(): got = lax.all_to_all(send, 'col', 0, 0, tiled=True)  4.19 us
    dot_general x1, matrix products, local(): grids = jnp.dot(w, cols.reshape(count, n * extent), precision=MID)  3.85 us
    dot_general x1, matrix products, cas_three(): return jnp.einsum('absc,ka->kbsc', field, table, precision=MID)  3.07 us
    mul x1, other arithmetic, plane_matrix(): return (ta[:, None, :] * tb[None, :, :]).reshape(extent * extent, -1)  2.73 us
    dot_general x1, matrix products, cas_three_reversed(): field = jnp.einsum('absc,ck->absk', field, table, precision=MID)  2.71 us
  transfers between devices with their start and end apart: 2, of which 2 were waited for; matrix products, arithmetic and copies ran while one was open for 11% of the time, Pallas kernels for 0%

profile of v15, /device:TPU:0, one launch (start us, length us, event | category | flops | bytes accessed | tf_op | source)
XLA Modules:
  0.0 60.4 jit_solution(3918450174527803714)
XLA Ops:
  0.0 0.0 copy-start.2
  0.0 0.0 copy-start.1
  0.0 0.7 %and_select_fusion.1 = s32[3]{0:T(128)S(1)} fusion(s32[3]{0:T(128)} %param.8), kind=kLoop, calls=%fused_computation.91 | loop fusion | flops 33 | bytes 24 | tf_op jit(solution)/shard_map/jit(remainder)/select_n | solution.py:74
  0.7 0.7 %fusion.55 = pred[3]{0:T(512)(128)(4,1)S(1)} fusion(s32[3]{0:T(128)} %param.8, s32[]{:T(128)S(6)} %axis_index.15), kind=kLoop, calls=%fused_computation.101 | loop fusion | flops 48 | bytes 19 | tf_op jit(solution)/shard_map/eq | solution.py:76
  1.4 1.0 %convolution_select_fusion = f32[3,1792]{1,0:T(4,128)S(1)} fusion(f32[8,1792]{1,0:T(8,128)} %param.5, pred[3]{0:T(512)(128)(4,1)S(1)} %fusion.55, s32[3]{0:T(128)S(1)} %and_select_fusion.1), kind=kOutput, calls=%fused_computation.14 | convolution fusion | flops 521496 | bytes 78863 | tf_op jit(solution)/shard_map/dot_general | solution.py:75
  2.4 0.7 %broadcast_in_dim.36 = f32[4,3,1792]{2,1,0:T(4,128)} broadcast(f32[3,1792]{1,0:T(4,128)S(1)} %convolution_select_fusion), dimensions={1,2} | broadcast | bytes 107520 | tf_op jit(solution)/shard_map/broadcast_in_dim | solution.py:77
  3.1 4.2 %all-to-all-start = ((f32[4,3,1792]{2,1,0:T(4,128)}), f32[4,3,1792]{2,1,0:T(4,128)S(1)}, u32[]{:S(2)}, u32[]{:S(2)}) async-start(f32[4,3,1792]{2,1,0:T(4,128)} %broadcast_in_dim.36), calls=%async_computation | async-start | bytes 229376 | tf_op jit(solution)/shard_map/all_to_all | solution.py:78
  7.3 0.1 add_multiply_fusion
  7.4 0.9 %broadcast_in_dim.33 = f32[8,1,1792]{2,1,0:T(1,128)S(1)} reshape(f32[8,1792]{1,0:T(8,128)} %param.5) | data formatting | bytes 114688 | tf_op jit(solution)/shard_map/broadcast_in_dim | solution.py:80
  8.3 0.1 copy.38
  8.4 0.6 gather_fusion
  9.0 0.1 broadcast_add_fusion
  9.1 0.4 fusion.14
  9.4 0.1 maximum_bitcast_fusion
  9.5 0.1 dot_general.54
  9.6 0.6 gather_fusion.1
  10.2 0.1 copy.39
  10.3 1.5 %all-to-all-done = f32[4,3,1792]{2,1,0:T(4,128)S(1)} async-done(((f32[4,3,1792]{2,1,0:T(4,128)}), f32[4,3,1792]{2,1,0:T(4,128)S(1)}, u32[]{:S(2)}, u32[]{:S(2)}) %all-to-all-start) | async-done | bytes 86048 | tf_op jit(solution)/shard_map/all_to_all | solution.py:78
  11.8 0.8 %pad_maximum_fusion = f32[8,4,1792]{2,1,0:T(4,128)} fusion(f32[8,3,1792]{2,1,0:T(4,128)S(1)} %broadcast_in_dim.37, f32[8,1,1792]{2,1,0:T(1,128)S(1)} %broadcast_in_dim.33), kind=kLoop, calls=%fused_computation.30 | loop fusion | flops 57344 | bytes 458752 | tf_op jit(solution)/shard_map/concatenate | solution.py:79
  12.6 0.8 %lt.102 = s32[8,56]{1,0:T(8,128)S(1)} reshape(s32[448]{0:T(512)} %param.7) | data formatting | bytes 3584 | tf_op jit(solution)/shard_map/lt | solution.py:39
  13.4 6.3 %all-to-all-start.1 = ((f32[8,4,1792]{2,1,0:T(4,128)}), f32[8,4,1792]{2,1,0:T(4,128)S(1)}, u32[]{:S(2)}, u32[]{:S(2)}) async-start(f32[8,4,1792]{2,1,0:T(4,128)} %pad_maximum_fusion), calls=%async_computation.1 | async-start | bytes 458752 | tf_op jit(solution)/shard_map/all_to_all | solution.py:82
  19.7 0.0 copy-done.2
  19.7 0.0 copy-done.1
  19.7 0.3 fusion.27
  20.1 0.3 fusion.28
  20.4 2.7 %broadcast_multiply_fusion = f32[48,48,448]{2,1,0:T(8,128)} fusion(f32[48,448]{1,0:T(8,128)S(1)} %fusion.28, f32[48,448]{1,0:T(8,128)S(1)} %fusion.27), kind=kLoop, calls=%fused_computation.13 | loop fusion | flops 1032192 | bytes 4300800 | tf_op jit(solution)/shard_map/mul | solution.py:49
  23.1 0.1 iota_compare_fusion
  23.2 0.4 fusion.25
  23.6 4.2 %all-to-all-done.1 = f32[8,4,1792]{2,1,0:T(4,128)S(1)} async-done(((f32[8,4,1792]{2,1,0:T(4,128)}), f32[8,4,1792]{2,1,0:T(4,128)S(1)}, u32[]{:S(2)}, u32[]{:S(2)}) %all-to-all-start.1) | async-done | bytes 229408 | tf_op jit(solution)/shard_map/all_to_all | solution.py:82
  27.9 0.3 reshape.207
  28.2 0.0 copy-start
  28.2 0.1 broadcast_select_fusion
  28.3 1.3 %fusion.32 = f32[448,4,2,48]{0,3,2,1:T(8,128)S(1)} fusion(f32[448,4,32,1]{2,0,3,1:T(8,128)S(1)} %bitcast.81, f32[2,48,32]{1,0,2:T(2,128)S(1)} %dot_general.54), kind=kOutput, calls=%fused_computation.55 | convolution fusion | flops 66060288 | bytes 929792 | tf_op jit(solution)/shard_map/dot_general | solution.py:93
  29.6 0.1 fusion.89
  29.7 0.1 fusion.16
  29.8 0.7 %copy-done = f32[48,48,448]{2,1,0:T(8,128)S(1)} copy-done((f32[48,48,448]{2,1,0:T(8,128)S(1)}, f32[48,48,448]{2,1,0:T(8,128)}, u32[]{:S(2)}) %copy-start) | copy-done | bytes 4128792
  30.5 3.8 %fusion.90 = f32[48,48,4,48]{3,1,2,0:T(8,128)S(1)} fusion(f32[48,48,448,1]{2,1,3,0:T(8,128)S(1)} %bitcast.78, f32[4,48,448,1]{2,1,0,3:T(8,128)S(1)} %bitcast.83), kind=kOutput, calls=%fused_computation.136 | convolution fusion | flops 1189085184 | bytes 6242304 | tf_op jit(solution)/shard_map/dot_general | solution.py:95
  34.4 0.1 slice_bitcast_fusion
  34.5 1.7 %fusion.7 = f32[48,48,3,48]{3,1,2,0:T(8,128)S(1)} fusion(f32[48,48,4,48]{3,1,2,0:T(8,128)S(1)} %fusion.90, f32[48,48,48]{2,1,0:T(8,128)S(1)} %slice_bitcast_fusion), kind=kOutput, calls=%fused_computation.10 | convolution fusion | flops 95908608 | bytes 6045696 | tf_op jit(solution)/shard_map/absc,ck->absk/dot_general | solution.py:53
  36.1 1.8 %convolution_bitcast_fusion = f32[48,48,3,48]{3,1,2,0:T(8,128)S(1)} fusion(f32[48,48,3,48]{3,1,2,0:T(8,128)S(1)} %fusion.7), kind=kOutput, calls=%fused_computation.15 | convolution fusion | flops 95576832 | bytes 2654208 | tf_op jit(solution)/shard_map/absc,kb->aksc/dot_general | solution.py:54
  37.9 3.1 %fusion.3 = f32[48,48,3,48]{3,0,2,1:T(8,128)S(1)} fusion(f32[48,48,3,48]{3,1,2,0:T(8,128)S(1)} %convolution_bitcast_fusion), kind=kOutput, calls=%fused_computation.6 | convolution fusion | flops 95576832 | bytes 2654208 | tf_op jit(solution)/shard_map/absc,ka->kbsc/dot_general | solution.py:55
  41.0 1.7 %fusion.5 = f32[48,48,3,48]{3,0,2,1:T(8,128)S(1)} fusion(f32[48,48,3,48]{3,0,2,1:T(8,128)S(1)} %fusion.3, f32[48,48,48]{2,0,1:T(8,128)S(1)} %fusion.14), kind=kOutput, calls=%fused_computation.8 | convolution fusion | flops 95908608 | bytes 3096576 | tf_op jit(solution)/shard_map/absc,ka->kbsc/dot_general | solution.py:59
  42.7 0.0 copy-start.3
  42.7 2.7 %fusion.1 = f32[48,48,3,48]{3,1,2,0:T(8,128)S(1)} fusion(f32[48,48,3,48]{3,0,2,1:T(8,128)S(1)} %fusion.5), kind=kOutput, calls=%fused_computation.4 | convolution fusion | flops 95576832 | bytes 2654208 | tf_op jit(solution)/shard_map/absc,ck->absk/dot_general | solution.py:60
  45.4 0.0 copy-done.3
  45.4 2.1 %fusion = f32[48,48,48]{2,1,0:T(8,128)S(1)} fusion(f32[48,48,4,48]{3,1,2,0:T(8,128)S(1)} %fusion.90, f32[48,48,3,48]{3,1,2,0:T(8,128)S(1)} %fusion.1, f32[3]{0:T(128)S(1)} %copy-done.3), kind=kOutput, calls=%fused_computation.3 | convolution fusion | flops 96461568 | bytes 3096588 | tf_op jit(solution)/shard_map/absc,kb->aksc/dot_general | solution.py:61
  47.5 1.6 %fusion.31 = (f32[448,48]{0,1:T(8,128)S(1)}, f32[448,48]{0,1:T(8,128)S(1)}) fusion(s32[448]{0:T(512)S(1)} %get-tuple-element.19, f32[2304,448]{1,0:T(8,128)S(1)} %bitcast.79, f32[2304,48]{1,0:T(8,128)S(1)} %bitcast.80), kind=kOutput, calls=%fused_computation.54 | convolution fusion | flops 297529344 | bytes 4744960 | tf_op jit(solution)/shard_map/dot_general | solution.py:102
  49.1 0.3 fusion.15
  49.4 0.1 copy.40
  49.6 0.2 reshape.232
  49.7 10.0 %all_to_all.15 = f32[8,1,1792]{2,1,0:T(1,128)S(1)} all-to-all(f32[8,1,1792]{2,1,0:T(1,128)S(1)} %reshape.232), channel_id=1, replica_groups=mesh['grp'=4,'col'=8] {'col'}, dimensions={0} | all-to-all | bytes 114688 | tf_op jit(solution)/shard_map/all_to_all | solution.py:106
  59.7 0.6 %copy.58 = f32[8,1,1792]{2,0,1:T(8,128)} copy(f32[8,1,1792]{2,1,0:T(1,128)S(1)} %all_to_all.15) | data formatting | bytes 114688
  (8 shorter events, 0.1 us)
Async XLA Ops:
  0.0 19.7 %copy-start.2 = (s32[448]{0:T(512)S(1)}, s32[448]{0:T(512)}, u32[]{:S(2)}) copy-start(s32[448]{0:T(512)} %param.6) | copy-start | bytes 5380
  0.0 19.7 %copy-start.1 = (s32[448]{0:T(512)S(1)}, s32[448]{0:T(512)}, u32[]{:S(2)}) copy-start(s32[448]{0:T(512)} %param.7) | copy-start | bytes 5380
  3.1 8.7 %all-to-all-start = ((f32[4,3,1792]{2,1,0:T(4,128)}), f32[4,3,1792]{2,1,0:T(4,128)S(1)}, u32[]{:S(2)}, u32[]{:S(2)}) async-start(f32[4,3,1792]{2,1,0:T(4,128)} %broadcast_in_dim.36), calls=%async_computation | async-start | bytes 229376 | tf_op jit(solution)/shard_map/all_to_all | solution.py:78
  13.4 14.4 %all-to-all-start.1 = ((f32[8,4,1792]{2,1,0:T(4,128)}), f32[8,4,1792]{2,1,0:T(4,128)S(1)}, u32[]{:S(2)}, u32[]{:S(2)}) async-start(f32[8,4,1792]{2,1,0:T(4,128)} %pad_maximum_fusion), calls=%async_computation.1 | async-start | bytes 458752 | tf_op jit(solution)/shard_map/all_to_all | solution.py:82
  28.2 2.3 %copy-start = (f32[48,48,448]{2,1,0:T(8,128)S(1)}, f32[48,48,448]{2,1,0:T(8,128)}, u32[]{:S(2)}) copy-start(f32[48,48,448]{2,1,0:T(8,128)} %broadcast_multiply_fusion) | copy-start | bytes 12386308
  42.7 2.7 %copy-start.3 = (f32[3]{0:T(128)S(1)}, f32[3]{0:T(128)}, u32[]{:S(2)}) copy-start(f32[3]{0:T(128)} %param.9) | copy-start | bytes 40

commit v16 on v13

--- a/solution.py
+++ b/solution.py
@@ -51,13 +51,13 @@
 
 def cas_three(field, table):
     field = jnp.einsum("absc,ck->absk", field, table, precision=MID)
-    field = jnp.einsum("absc,kb->aksc", field, table, precision=MID)
-    return jnp.einsum("absc,ka->kbsc", field, table, precision=MID)
+    field = jnp.einsum("absc,ka->kbsc", field, table, precision=MID)
+    return jnp.einsum("absc,kb->aksc", field, table, precision=MID)
 
 
 def cas_three_reversed(field, table):
+    field = jnp.einsum("absc,kb->aksc", field, table, precision=MID)
     field = jnp.einsum("absc,ka->kbsc", field, table, precision=MID)
-    field = jnp.einsum("absc,kb->aksc", field, table, precision=MID)
     return jnp.einsum("absc,ck->absk", field, table, precision=MID)
 
 

time: 60.7 us -> 63.4 us (1.044)
  matrix products: 21.5 us -> 23.8 us
    dot_general x1, matrix products: 1.7 us -> 2.9 us  [cas_three_reversed(): field = jnp.einsum('absc,ka->kbsc', field, table, precision=MID)]
    dot_general x1, matrix products: 2.89 us -> 1.75 us  [cas_three_reversed(): field = jnp.einsum('absc,kb->aksc', field, table, precision=MID)]
    dot_general x1, matrix products: 1.65 us -> 2.71 us  [cas_three_reversed(): return jnp.einsum('absc,ck->absk', field, table, precision=MID)]
    dot_general x1, matrix products: 1.67 us -> 2.73 us  [cas_three(): field = jnp.einsum('absc,ck->absk', field, table, precision=MID)]
where the time goes in v16:
time: 63.4 us; the launch traced here: 62.9 us
  matrix products  23.8 us (38%)
  starting transfers between devices  10.5 us (17%)
  blocking collectives  10 us (16%)
  other arithmetic  6.78 us (11%)
  local copies, waits for them, and re-layouts  5.82 us (9%)
  waiting for transfers between devices  5.69 us (9%)
    all_to_all x1, blocking collectives, local(): lax.all_to_all(out.reshape(n_col, 1, width), 'col', 0, 0, tiled=True)  10 us
    all_to_all x1, starting transfers between devices, local(): got = lax.all_to_all(send, 'col', 0, 0, tiled=True)  6.31 us
    all_to_all x1, starting transfers between devices, local(): picked = jnp.sum(lax.all_to_all(spread, 'grp', 0, 0, tiled=True), axis=0)  4.24 us
    all_to_all x1, waiting for transfers between devices, local(): got = lax.all_to_all(send, 'col', 0, 0, tiled=True)  4.19 us
    dot_general x1, matrix products, local(): grids = jnp.dot(w, cols.reshape(count, n * extent), precision=MID)  3.85 us
    dot_general x1, matrix products, cas_three_reversed(): field = jnp.einsum('absc,ka->kbsc', field, table, precision=MID)  2.9 us
    dot_general x1, matrix products, cas_three(): return jnp.einsum('absc,kb->aksc', field, table, precision=MID)  2.89 us
    dot_general x1, matrix products, cas_three(): field = jnp.einsum('absc,ck->absk', field, table, precision=MID)  2.73 us
  transfers between devices with their start and end apart: 2, of which 2 were waited for; matrix products, arithmetic and copies ran while one was open for 11% of the time, Pallas kernels for 0%

profile of v16, /device:TPU:0, one launch (start us, length us, event | category | flops | bytes accessed | tf_op | source)
XLA Modules:
  0.0 62.9 jit_solution(5932468293915483001)
XLA Ops:
  0.0 0.0 copy-start.2
  0.0 0.0 copy-start.1
  0.0 0.7 %and_select_fusion.1 = s32[3]{0:T(128)S(1)} fusion(s32[3]{0:T(128)} %param.8), kind=kLoop, calls=%fused_computation.92 | loop fusion | flops 33 | bytes 24 | tf_op jit(solution)/shard_map/jit(remainder)/select_n | solution.py:74
  0.7 0.7 %fusion.57 = pred[3]{0:T(512)(128)(4,1)S(1)} fusion(s32[3]{0:T(128)} %param.8, s32[]{:T(128)S(6)} %axis_index.15), kind=kLoop, calls=%fused_computation.102 | loop fusion | flops 48 | bytes 19 | tf_op jit(solution)/shard_map/eq | solution.py:76
  1.4 1.0 %convolution_select_fusion = f32[3,1792]{1,0:T(4,128)S(1)} fusion(f32[8,1792]{1,0:T(8,128)} %param.5, pred[3]{0:T(512)(128)(4,1)S(1)} %fusion.57, s32[3]{0:T(128)S(1)} %and_select_fusion.1), kind=kOutput, calls=%fused_computation.15 | convolution fusion | flops 521496 | bytes 78863 | tf_op jit(solution)/shard_map/dot_general | solution.py:75
  2.4 0.7 %broadcast_in_dim.36 = f32[4,3,1792]{2,1,0:T(4,128)} broadcast(f32[3,1792]{1,0:T(4,128)S(1)} %convolution_select_fusion), dimensions={1,2} | broadcast | bytes 107520 | tf_op jit(solution)/shard_map/broadcast_in_dim | solution.py:77
  3.1 4.2 %all-to-all-start = ((f32[4,3,1792]{2,1,0:T(4,128)}), f32[4,3,1792]{2,1,0:T(4,128)S(1)}, u32[]{:S(2)}, u32[]{:S(2)}) async-start(f32[4,3,1792]{2,1,0:T(4,128)} %broadcast_in_dim.36), calls=%async_computation | async-start | bytes 229376 | tf_op jit(solution)/shard_map/all_to_all | solution.py:78
  7.3 0.1 add_multiply_fusion
  7.4 0.9 %broadcast_in_dim.33 = f32[8,1,1792]{2,1,0:T(1,128)S(1)} reshape(f32[8,1792]{1,0:T(8,128)} %param.5) | data formatting | bytes 114688 | tf_op jit(solution)/shard_map/broadcast_in_dim | solution.py:80
  8.3 0.1 copy.44
  8.4 0.6 gather_fusion
  9.0 0.1 broadcast_add_fusion
  9.1 0.4 fusion.15
  9.4 0.1 maximum_bitcast_fusion
  9.5 0.1 dot_general.54
  9.6 0.6 gather_fusion.1
  10.2 0.1 copy.45
  10.3 1.5 %all-to-all-done = f32[4,3,1792]{2,1,0:T(4,128)S(1)} async-done(((f32[4,3,1792]{2,1,0:T(4,128)}), f32[4,3,1792]{2,1,0:T(4,128)S(1)}, u32[]{:S(2)}, u32[]{:S(2)}) %all-to-all-start) | async-done | bytes 86048 | tf_op jit(solution)/shard_map/all_to_all | solution.py:78
  11.8 0.8 %pad_maximum_fusion = f32[8,4,1792]{2,1,0:T(4,128)} fusion(f32[8,3,1792]{2,1,0:T(4,128)S(1)} %broadcast_in_dim.37, f32[8,1,1792]{2,1,0:T(1,128)S(1)} %broadcast_in_dim.33), kind=kLoop, calls=%fused_computation.30 | loop fusion | flops 57344 | bytes 458752 | tf_op jit(solution)/shard_map/concatenate | solution.py:79
  12.6 0.8 %lt.102 = s32[8,56]{1,0:T(8,128)S(1)} reshape(s32[448]{0:T(512)} %param.7) | data formatting | bytes 3584 | tf_op jit(solution)/shard_map/lt | solution.py:39
  13.4 6.3 %all-to-all-start.1 = ((f32[8,4,1792]{2,1,0:T(4,128)}), f32[8,4,1792]{2,1,0:T(4,128)S(1)}, u32[]{:S(2)}, u32[]{:S(2)}) async-start(f32[8,4,1792]{2,1,0:T(4,128)} %pad_maximum_fusion), calls=%async_computation.1 | async-start | bytes 458752 | tf_op jit(solution)/shard_map/all_to_all | solution.py:82
  19.7 0.0 copy-done.2
  19.7 0.0 copy-done.1
  19.7 0.3 fusion.28
  20.1 0.3 fusion.29
  20.4 2.7 %broadcast_multiply_fusion = f32[48,48,448]{2,1,0:T(8,128)} fusion(f32[48,448]{1,0:T(8,128)S(1)} %fusion.29, f32[48,448]{1,0:T(8,128)S(1)} %fusion.28), kind=kLoop, calls=%fused_computation.14 | loop fusion | flops 1032192 | bytes 4300800 | tf_op jit(solution)/shard_map/mul | solution.py:49
  23.1 0.1 iota_compare_fusion
  23.2 0.4 fusion.26
  23.6 4.2 %all-to-all-done.1 = f32[8,4,1792]{2,1,0:T(4,128)S(1)} async-done(((f32[8,4,1792]{2,1,0:T(4,128)}), f32[8,4,1792]{2,1,0:T(4,128)S(1)}, u32[]{:S(2)}, u32[]{:S(2)}) %all-to-all-start.1) | async-done | bytes 229408 | tf_op jit(solution)/shard_map/all_to_all | solution.py:82
  27.9 0.3 reshape.207
  28.2 0.0 copy-start
  28.2 0.1 broadcast_select_fusion
  28.3 1.3 %fusion.33 = f32[448,4,2,48]{0,3,2,1:T(8,128)S(1)} fusion(f32[448,4,32,1]{2,0,3,1:T(8,128)S(1)} %bitcast.81, f32[2,48,32]{1,0,2:T(2,128)S(1)} %dot_general.54), kind=kOutput, calls=%fused_computation.55 | convolution fusion | flops 66060288 | bytes 929792 | tf_op jit(solution)/shard_map/dot_general | solution.py:93
  29.6 0.1 fusion.91
  29.7 0.1 fusion.17
  29.8 0.7 %copy-done = f32[48,48,448]{2,1,0:T(8,128)S(1)} copy-done((f32[48,48,448]{2,1,0:T(8,128)S(1)}, f32[48,48,448]{2,1,0:T(8,128)}, u32[]{:S(2)}) %copy-start) | copy-done | bytes 4128792
  30.5 3.8 %fusion.92 = f32[48,48,4,48]{3,1,2,0:T(8,128)S(1)} fusion(f32[48,48,448,1]{2,1,3,0:T(8,128)S(1)} %bitcast.78, f32[4,48,448,1]{2,1,0,3:T(8,128)S(1)} %bitcast.83), kind=kOutput, calls=%fused_computation.137 | convolution fusion | flops 1189085184 | bytes 6242304 | tf_op jit(solution)/shard_map/dot_general | solution.py:95
  34.4 0.1 slice_bitcast_fusion
  34.5 0.5 slice_multiply_fusion
  34.9 2.7 %fusion.1 = f32[48,48,3,48]{3,0,2,1:T(8,128)S(1)} fusion(f32[48,48,3,48]{3,1,2,0:T(8,128)S(1)} %slice_multiply_fusion), kind=kOutput, calls=%fused_computation.4 | convolution fusion | flops 95576832 | bytes 2654208 | tf_op jit(solution)/shard_map/absc,ck->absk/dot_general | solution.py:53
  37.7 2.1 %fusion.42 = f32[48,48,3,48]{3,0,2,1:T(8,128)S(1)} fusion(f32[48,48,3,48]{3,0,2,1:T(8,128)S(1)} %fusion.1), kind=kOutput, calls=%fused_computation.64 | convolution fusion | flops 95576832 | bytes 2654208 | tf_op jit(solution)/shard_map/absc,ka->kbsc/dot_general | solution.py:54
  39.7 2.9 %fusion.7 = f32[48,48,3,48]{3,0,2,1:T(8,128)S(1)} fusion(f32[48,48,3,48]{3,0,2,1:T(8,128)S(1)} %fusion.42), kind=kOutput, calls=%fused_computation.10 | convolution fusion | flops 95576832 | bytes 2654208 | tf_op jit(solution)/shard_map/absc,kb->aksc/dot_general | solution.py:55
  42.6 1.8 %fusion.11 = f32[48,48,3,48]{3,1,2,0:T(8,128)S(1)} fusion(f32[48,48,3,48]{3,0,2,1:T(8,128)S(1)} %fusion.7, f32[48,48,48]{2,1,0:T(8,128)S(1)} %fusion.15), kind=kOutput, calls=%fused_computation.16 | convolution fusion | flops 95908608 | bytes 3096576 | tf_op jit(solution)/shard_map/absc,kb->aksc/dot_general | solution.py:59
  44.4 0.0 copy-start.3
  44.4 2.9 %fusion.5 = f32[48,48,3,48]{3,0,2,1:T(8,128)S(1)} fusion(f32[48,48,3,48]{3,1,2,0:T(8,128)S(1)} %fusion.11), kind=kOutput, calls=%fused_computation.8 | convolution fusion | flops 95576832 | bytes 2654208 | tf_op jit(solution)/shard_map/absc,ka->kbsc/dot_general | solution.py:60
  47.3 0.0 copy-done.3
  47.3 2.7 %multiply_reduce_fusion = f32[48,48,48]{2,1,0:T(8,128)S(1)} fusion(f32[48,48,4,48]{3,1,2,0:T(8,128)S(1)} %fusion.92, f32[48,48,3,48]{3,0,2,1:T(8,128)S(1)} %fusion.5, f32[3]{0:T(128)S(1)} %copy-done.3), kind=kOutput, calls=%fused_computation.12 | convolution fusion | flops 96461568 | bytes 3096588 | tf_op jit(solution)/shard_map/absc,ck->absk/dot_general | solution.py:61
  50.0 1.6 %fusion.32 = (f32[448,48]{0,1:T(8,128)S(1)}, f32[448,48]{0,1:T(8,128)S(1)}) fusion(s32[448]{0:T(512)S(1)} %get-tuple-element.19, f32[2304,448]{1,0:T(8,128)S(1)} %bitcast.79, f32[2304,48]{1,0:T(8,128)S(1)} %bitcast.80), kind=kOutput, calls=%fused_computation.54 | convolution fusion | flops 297529344 | bytes 4744960 | tf_op jit(solution)/shard_map/dot_general | solution.py:102
  51.7 0.3 fusion.16
  52.0 0.1 copy.46
  52.1 0.2 reshape.232
  52.2 10.0 %all_to_all.15 = f32[8,1,1792]{2,1,0:T(1,128)S(1)} all-to-all(f32[8,1,1792]{2,1,0:T(1,128)S(1)} %reshape.232), channel_id=1, replica_groups=mesh['grp'=4,'col'=8] {'col'}, dimensions={0} | all-to-all | bytes 114688 | tf_op jit(solution)/shard_map/all_to_all | solution.py:106
  62.3 0.6 copy.72
  (8 shorter events, 0.2 us)
Async XLA Ops:
  0.0 19.7 %copy-start.2 = (s32[448]{0:T(512)S(1)}, s32[448]{0:T(512)}, u32[]{:S(2)}) copy-start(s32[448]{0:T(512)} %param.6) | copy-start | bytes 5380
  0.0 19.7 %copy-start.1 = (s32[448]{0:T(512)S(1)}, s32[448]{0:T(512)}, u32[]{:S(2)}) copy-start(s32[448]{0:T(512)} %param.7) | copy-start | bytes 5380
  3.1 8.7 %all-to-all-start = ((f32[4,3,1792]{2,1,0:T(4,128)}), f32[4,3,1792]{2,1,0:T(4,128)S(1)}, u32[]{:S(2)}, u32[]{:S(2)}) async-start(f32[4,3,1792]{2,1,0:T(4,128)} %broadcast_in_dim.36), calls=%async_computation | async-start | bytes 229376 | tf_op jit(solution)/shard_map/all_to_all | solution.py:78
  13.4 14.4 %all-to-all-start.1 = ((f32[8,4,1792]{2,1,0:T(4,128)}), f32[8,4,1792]{2,1,0:T(4,128)S(1)}, u32[]{:S(2)}, u32[]{:S(2)}) async-start(f32[8,4,1792]{2,1,0:T(4,128)} %pad_maximum_fusion), calls=%async_computation.1 | async-start | bytes 458752 | tf_op jit(solution)/shard_map/all_to_all | solution.py:82
  28.2 2.3 %copy-start = (f32[48,48,448]{2,1,0:T(8,128)S(1)}, f32[48,48,448]{2,1,0:T(8,128)}, u32[]{:S(2)}) copy-start(f32[48,48,448]{2,1,0:T(8,128)} %broadcast_multiply_fusion) | copy-start | bytes 12386308
  44.4 2.9 %copy-start.3 = (f32[3]{0:T(128)S(1)}, f32[3]{0:T(128)}, u32[]{:S(2)}) copy-start(f32[3]{0:T(128)} %param.9) | copy-start | bytes 40

commit v17 on v13

--- a/solution.py
+++ b/solution.py
@@ -50,8 +50,8 @@
 
 
 def cas_three(field, table):
+    field = jnp.einsum("absc,kb->aksc", field, table, precision=MID)
     field = jnp.einsum("absc,ck->absk", field, table, precision=MID)
-    field = jnp.einsum("absc,kb->aksc", field, table, precision=MID)
     return jnp.einsum("absc,ka->kbsc", field, table, precision=MID)
 
 

time: 60.7 us -> 60.7 us (level)
    dot_general x1, matrix products: 1.67 us -> 2.73 us  [cas_three(): field = jnp.einsum('absc,ck->absk', field, table, precision=MID)]
    dot_general x1, matrix products: 3.07 us -> 2.07 us  [cas_three(): return jnp.einsum('absc,ka->kbsc', field, table, precision=MID)]
where the time goes in v17:
time: 60.7 us; the launch traced here: 60.1 us
  matrix products  21.5 us (35%)
  starting transfers between devices  10.5 us (17%)
  blocking collectives  10 us (16%)
  other arithmetic  6.32 us (10%)
  local copies, waits for them, and re-layouts  5.82 us (10%)
  waiting for transfers between devices  5.69 us (9%)
    all_to_all x1, blocking collectives, local(): lax.all_to_all(out.reshape(n_col, 1, width), 'col', 0, 0, tiled=True)  10 us
    all_to_all x1, starting transfers between devices, local(): got = lax.all_to_all(send, 'col', 0, 0, tiled=True)  6.31 us
    all_to_all x1, starting transfers between devices, local(): picked = jnp.sum(lax.all_to_all(spread, 'grp', 0, 0, tiled=True), axis=0)  4.24 us
    all_to_all x1, waiting for transfers between devices, local(): got = lax.all_to_all(send, 'col', 0, 0, tiled=True)  4.19 us
    dot_general x1, matrix products, local(): grids = jnp.dot(w, cols.reshape(count, n * extent), precision=MID)  3.85 us
    dot_general x1, matrix products, cas_three_reversed(): field = jnp.einsum('absc,kb->aksc', field, table, precision=MID)  2.89 us
    dot_general x1, matrix products, cas_three(): field = jnp.einsum('absc,ck->absk', field, table, precision=MID)  2.73 us
    mul x1, other arithmetic, plane_matrix(): return (ta[:, None, :] * tb[None, :, :]).reshape(extent * extent, -1)  2.73 us
  transfers between devices with their start and end apart: 2, of which 2 were waited for; matrix products, arithmetic and copies ran while one was open for 11% of the time, Pallas kernels for 0%

profile of v17, /device:TPU:0, one launch (start us, length us, event | category | flops | bytes accessed | tf_op | source)
XLA Modules:
  0.0 60.1 jit_solution(164954848791101084)
XLA Ops:
  0.0 0.0 copy-start.2
  0.0 0.0 copy-start.1
  0.0 0.7 %and_select_fusion.1 = s32[3]{0:T(128)S(1)} fusion(s32[3]{0:T(128)} %param.8), kind=kLoop, calls=%fused_computation.93 | loop fusion | flops 33 | bytes 24 | tf_op jit(solution)/shard_map/jit(remainder)/select_n | solution.py:74
  0.7 0.7 %fusion.62 = pred[3]{0:T(512)(128)(4,1)S(1)} fusion(s32[3]{0:T(128)} %param.8, s32[]{:T(128)S(6)} %axis_index.15), kind=kLoop, calls=%fused_computation.103 | loop fusion | flops 48 | bytes 19 | tf_op jit(solution)/shard_map/eq | solution.py:76
  1.4 1.0 %convolution_select_fusion = f32[3,1792]{1,0:T(4,128)S(1)} fusion(f32[8,1792]{1,0:T(8,128)} %param.5, pred[3]{0:T(512)(128)(4,1)S(1)} %fusion.62, s32[3]{0:T(128)S(1)} %and_select_fusion.1), kind=kOutput, calls=%fused_computation.15 | convolution fusion | flops 521496 | bytes 78863 | tf_op jit(solution)/shard_map/dot_general | solution.py:75
  2.4 0.7 %broadcast_in_dim.36 = f32[4,3,1792]{2,1,0:T(4,128)} broadcast(f32[3,1792]{1,0:T(4,128)S(1)} %convolution_select_fusion), dimensions={1,2} | broadcast | bytes 107520 | tf_op jit(solution)/shard_map/broadcast_in_dim | solution.py:77
  3.1 4.2 %all-to-all-start = ((f32[4,3,1792]{2,1,0:T(4,128)}), f32[4,3,1792]{2,1,0:T(4,128)S(1)}, u32[]{:S(2)}, u32[]{:S(2)}) async-start(f32[4,3,1792]{2,1,0:T(4,128)} %broadcast_in_dim.36), calls=%async_computation | async-start | bytes 229376 | tf_op jit(solution)/shard_map/all_to_all | solution.py:78
  7.3 0.1 add_multiply_fusion
  7.4 0.9 %broadcast_in_dim.33 = f32[8,1,1792]{2,1,0:T(1,128)S(1)} reshape(f32[8,1792]{1,0:T(8,128)} %param.5) | data formatting | bytes 114688 | tf_op jit(solution)/shard_map/broadcast_in_dim | solution.py:80
  8.3 0.1 copy.38
  8.4 0.6 gather_fusion
  9.0 0.1 broadcast_add_fusion
  9.1 0.4 fusion.20
  9.4 0.1 maximum_bitcast_fusion
  9.5 0.1 dot_general.54
  9.6 0.6 gather_fusion.1
  10.2 0.1 copy.39
  10.3 1.5 %all-to-all-done = f32[4,3,1792]{2,1,0:T(4,128)S(1)} async-done(((f32[4,3,1792]{2,1,0:T(4,128)}), f32[4,3,1792]{2,1,0:T(4,128)S(1)}, u32[]{:S(2)}, u32[]{:S(2)}) %all-to-all-start) | async-done | bytes 86048 | tf_op jit(solution)/shard_map/all_to_all | solution.py:78
  11.8 0.8 %pad_maximum_fusion = f32[8,4,1792]{2,1,0:T(4,128)} fusion(f32[8,3,1792]{2,1,0:T(4,128)S(1)} %broadcast_in_dim.37, f32[8,1,1792]{2,1,0:T(1,128)S(1)} %broadcast_in_dim.33), kind=kLoop, calls=%fused_computation.31 | loop fusion | flops 57344 | bytes 458752 | tf_op jit(solution)/shard_map/concatenate | solution.py:79
  12.6 0.8 %lt.102 = s32[8,56]{1,0:T(8,128)S(1)} reshape(s32[448]{0:T(512)} %param.7) | data formatting | bytes 3584 | tf_op jit(solution)/shard_map/lt | solution.py:39
  13.4 6.3 %all-to-all-start.1 = ((f32[8,4,1792]{2,1,0:T(4,128)}), f32[8,4,1792]{2,1,0:T(4,128)S(1)}, u32[]{:S(2)}, u32[]{:S(2)}) async-start(f32[8,4,1792]{2,1,0:T(4,128)} %pad_maximum_fusion), calls=%async_computation.1 | async-start | bytes 458752 | tf_op jit(solution)/shard_map/all_to_all | solution.py:82
  19.7 0.0 copy-done.2
  19.7 0.0 copy-done.1
  19.7 0.3 fusion.33
  20.1 0.3 fusion.34
  20.4 2.7 %broadcast_multiply_fusion = f32[48,48,448]{2,1,0:T(8,128)} fusion(f32[48,448]{1,0:T(8,128)S(1)} %fusion.34, f32[48,448]{1,0:T(8,128)S(1)} %fusion.33), kind=kLoop, calls=%fused_computation.14 | loop fusion | flops 1032192 | bytes 4300800 | tf_op jit(solution)/shard_map/mul | solution.py:49
  23.1 0.1 iota_compare_fusion
  23.2 0.4 fusion.31
  23.6 4.2 %all-to-all-done.1 = f32[8,4,1792]{2,1,0:T(4,128)S(1)} async-done(((f32[8,4,1792]{2,1,0:T(4,128)}), f32[8,4,1792]{2,1,0:T(4,128)S(1)}, u32[]{:S(2)}, u32[]{:S(2)}) %all-to-all-start.1) | async-done | bytes 229408 | tf_op jit(solution)/shard_map/all_to_all | solution.py:82
  27.9 0.3 reshape.207
  28.2 0.0 copy-start
  28.2 0.1 broadcast_select_fusion
  28.3 1.3 %fusion.38 = f32[448,4,2,48]{0,3,2,1:T(8,128)S(1)} fusion(f32[448,4,32,1]{2,0,3,1:T(8,128)S(1)} %bitcast.81, f32[2,48,32]{1,0,2:T(2,128)S(1)} %dot_general.54), kind=kOutput, calls=%fused_computation.56 | convolution fusion | flops 66060288 | bytes 929792 | tf_op jit(solution)/shard_map/dot_general | solution.py:93
  29.6 0.1 fusion.96
  29.7 0.1 fusion.22
  29.8 0.7 %copy-done = f32[48,48,448]{2,1,0:T(8,128)S(1)} copy-done((f32[48,48,448]{2,1,0:T(8,128)S(1)}, f32[48,48,448]{2,1,0:T(8,128)}, u32[]{:S(2)}) %copy-start) | copy-done | bytes 4128792
  30.5 3.8 %fusion.97 = f32[48,48,4,48]{3,1,2,0:T(8,128)S(1)} fusion(f32[48,48,448,1]{2,1,3,0:T(8,128)S(1)} %bitcast.78, f32[4,48,448,1]{2,1,0,3:T(8,128)S(1)} %bitcast.83), kind=kOutput, calls=%fused_computation.138 | convolution fusion | flops 1189085184 | bytes 6242304 | tf_op jit(solution)/shard_map/dot_general | solution.py:95
  34.4 0.1 slice_bitcast_fusion
  34.5 1.7 %fusion.11 = f32[48,48,3,48]{3,1,2,0:T(8,128)S(1)} fusion(f32[48,48,4,48]{3,1,2,0:T(8,128)S(1)} %fusion.97, f32[48,48,48]{2,1,0:T(8,128)S(1)} %slice_bitcast_fusion), kind=kOutput, calls=%fused_computation.16 | convolution fusion | flops 95908608 | bytes 6045696 | tf_op jit(solution)/shard_map/absc,kb->aksc/dot_general | solution.py:53
  36.2 2.7 %fusion.2 = f32[48,48,3,48]{3,0,2,1:T(8,128)S(1)} fusion(f32[48,48,3,48]{3,1,2,0:T(8,128)S(1)} %fusion.11), kind=kOutput, calls=%fused_computation.4 | convolution fusion | flops 95576832 | bytes 2654208 | tf_op jit(solution)/shard_map/absc,ck->absk/dot_general | solution.py:54
  38.9 2.1 %fusion.46 = f32[48,48,3,48]{3,0,2,1:T(8,128)S(1)} fusion(f32[48,48,3,48]{3,0,2,1:T(8,128)S(1)} %fusion.2), kind=kOutput, calls=%fused_computation.64 | convolution fusion | flops 95576832 | bytes 2654208 | tf_op jit(solution)/shard_map/absc,ka->kbsc/dot_general | solution.py:55
  41.0 1.7 %fusion.6 = f32[48,48,3,48]{3,0,2,1:T(8,128)S(1)} fusion(f32[48,48,3,48]{3,0,2,1:T(8,128)S(1)} %fusion.46, f32[48,48,48]{2,0,1:T(8,128)S(1)} %fusion.20), kind=kOutput, calls=%fused_computation.9 | convolution fusion | flops 95908608 | bytes 3096576 | tf_op jit(solution)/shard_map/absc,ka->kbsc/dot_general | solution.py:59
  42.7 0.0 copy-start.3
  42.7 2.9 %fusion.4 = f32[48,48,3,48]{3,0,2,1:T(8,128)S(1)} fusion(f32[48,48,3,48]{3,0,2,1:T(8,128)S(1)} %fusion.6), kind=kOutput, calls=%fused_computation.6 | convolution fusion | flops 95576832 | bytes 2654208 | tf_op jit(solution)/shard_map/absc,kb->aksc/dot_general | solution.py:60
  45.6 0.0 copy-done.3
  45.6 1.7 %multiply_reduce_fusion = f32[48,48,48]{2,1,0:T(8,128)S(1)} fusion(f32[48,48,4,48]{3,1,2,0:T(8,128)S(1)} %fusion.97, f32[48,48,3,48]{3,0,2,1:T(8,128)S(1)} %fusion.4, f32[3]{0:T(128)S(1)} %copy-done.3), kind=kOutput, calls=%fused_computation.8 | convolution fusion | flops 96461568 | bytes 3096588 | tf_op jit(solution)/shard_map/absc,ck->absk/dot_general | solution.py:61
  47.3 1.6 %fusion.37 = (f32[448,48]{0,1:T(8,128)S(1)}, f32[448,48]{0,1:T(8,128)S(1)}) fusion(s32[448]{0:T(512)S(1)} %get-tuple-element.19, f32[2304,448]{1,0:T(8,128)S(1)} %bitcast.79, f32[2304,48]{1,0:T(8,128)S(1)} %bitcast.80), kind=kOutput, calls=%fused_computation.55 | convolution fusion | flops 297529344 | bytes 4744960 | tf_op jit(solution)/shard_map/dot_general | solution.py:102
  48.9 0.3 fusion.21
  49.2 0.1 copy.40
  49.3 0.2 reshape.232
  49.5 10.0 %all_to_all.15 = f32[8,1,1792]{2,1,0:T(1,128)S(1)} all-to-all(f32[8,1,1792]{2,1,0:T(1,128)S(1)} %reshape.232), channel_id=1, replica_groups=mesh['grp'=4,'col'=8] {'col'}, dimensions={0} | all-to-all | bytes 114688 | tf_op jit(solution)/shard_map/all_to_all | solution.py:106
  59.5 0.6 %copy.60 = f32[8,1,1792]{2,0,1:T(8,128)} copy(f32[8,1,1792]{2,1,0:T(1,128)S(1)} %all_to_all.15) | data formatting | bytes 114688
  (8 shorter events, 0.1 us)
Async XLA Ops:
  0.0 19.7 %copy-start.2 = (s32[448]{0:T(512)S(1)}, s32[448]{0:T(512)}, u32[]{:S(2)}) copy-start(s32[448]{0:T(512)} %param.6) | copy-start | bytes 5380
  0.0 19.7 %copy-start.1 = (s32[448]{0:T(512)S(1)}, s32[448]{0:T(512)}, u32[]{:S(2)}) copy-start(s32[448]{0:T(512)} %param.7) | copy-start | bytes 5380
  3.1 8.7 %all-to-all-start = ((f32[4,3,1792]{2,1,0:T(4,128)}), f32[4,3,1792]{2,1,0:T(4,128)S(1)}, u32[]{:S(2)}, u32[]{:S(2)}) async-start(f32[4,3,1792]{2,1,0:T(4,128)} %broadcast_in_dim.36), calls=%async_computation | async-start | bytes 229376 | tf_op jit(solution)/shard_map/all_to_all | solution.py:78
  13.4 14.4 %all-to-all-start.1 = ((f32[8,4,1792]{2,1,0:T(4,128)}), f32[8,4,1792]{2,1,0:T(4,128)S(1)}, u32[]{:S(2)}, u32[]{:S(2)}) async-start(f32[8,4,1792]{2,1,0:T(4,128)} %pad_maximum_fusion), calls=%async_computation.1 | async-start | bytes 458752 | tf_op jit(solution)/shard_map/all_to_all | solution.py:82
  28.2 2.3 %copy-start = (f32[48,48,448]{2,1,0:T(8,128)S(1)}, f32[48,48,448]{2,1,0:T(8,128)}, u32[]{:S(2)}) copy-start(f32[48,48,448]{2,1,0:T(8,128)} %broadcast_multiply_fusion) | copy-start | bytes 12386308
  42.7 2.9 %copy-start.3 = (f32[3]{0:T(128)S(1)}, f32[3]{0:T(128)}, u32[]{:S(2)}) copy-start(f32[3]{0:T(128)} %param.9) | copy-start | bytes 40
